TPU v7x, 32 devices: a whole 2x2x4 slice. The times are simulated.
32 devices in a mesh: amp: 8 (over y, x, core), int: 4 (over z).
Axes of the slice: x: 2, y: 2, z: 4, core: 2. Of those that a mesh axis runs over, the one named last changes fastest.
Arguments:
- amplitudes: float32 [768, 512], P('int'), may hold values from -6 to 6
- slab_integrals: float32 [512, 51200], P('int', 'amp'), may hold values from -0.25 to 0.25
- cycle_integrals: float32 [96, 800, 512], P('int', 'amp'), may hold values from -0.03125 to 0.03125
- occ_irrep: int32 [96], replicated, may hold values from 0 to 7
- vir_irrep: int32 [800], replicated, may hold values from 0 to 7
Outputs:
- ladder: float32 [768, 51200], P('int', 'amp')
- cycle: float32 [512, 512], P('int', 'amp')
All inputs are finite; a program needn't handle non-finite values.
Results may differ from a plain program's by a relative error of at most 0.00011.
Values sent between devices are 32-bit elements; how exact they have to be, the bound alone decides.
No kernel may reach another device: no remote copies, remote signals or barrier semaphores. Data moves between devices by JAX's collectives and lax.ppermute only.
A program may use at most 64 MiB of HBM per device.

v0:
```python
import jax
import jax.numpy as jnp
from jax import lax
from jax.sharding import PartitionSpec as P

NOCC = 96
NVIR = 800
SLAB = 64


def per_device(amplitudes, slab_integrals, cycle_integrals, occ_irrep, vir_irrep):
    rows = amplitudes.shape[0]
    width = slab_integrals.shape[1]
    ladder = jnp.dot(
        amplitudes,
        lax.all_gather(slab_integrals, "int", axis=0, tiled=True),
        precision=lax.Precision.HIGHEST,
        preferred_element_type=jnp.float32,
    )
    i_local = rows // NOCC
    a_local = width // NVIR
    blocks = ladder.reshape(i_local, NOCC, a_local, NVIR)
    columns = cycle_integrals.shape[2]
    moved = lax.all_to_all(
        lax.all_to_all(blocks, "amp", split_axis=3, concat_axis=2, tiled=True),
        "int",
        split_axis=1,
        concat_axis=0,
        tiled=True,
    )
    partial_value = jnp.einsum(
        "ikac,kcn->ian", moved, cycle_integrals, precision=lax.Precision.HIGHEST
    )
    partial_value = partial_value.reshape(moved.shape[0] * SLAB, columns)
    narrowed = lax.psum_scatter(partial_value, "amp", scatter_dimension=1, tiled=True)
    sums = lax.psum_scatter(narrowed, "int", scatter_dimension=0, tiled=True)
    col_local = sums.shape[1]
    row_start = lax.axis_index("int") * i_local
    batch_labels = lax.dynamic_slice_in_dim(occ_irrep, row_start, i_local, 0)
    slab_labels = vir_irrep[:SLAB]
    row_labels = jnp.bitwise_xor(batch_labels[:, None], slab_labels[None, :]).reshape(-1)
    col_ids = lax.axis_index("amp") * col_local + jnp.arange(col_local, dtype=jnp.int32)
    col_occ = col_ids // SLAB
    col_vir = col_ids % SLAB
    occ_match = col_occ[:, None] == jnp.arange(NOCC, dtype=jnp.int32)[None, :]
    vir_match = col_vir[:, None] == jnp.arange(SLAB, dtype=jnp.int32)[None, :]
    occ_lookup = jnp.sum(jnp.where(occ_match, occ_irrep[None, :], 0), axis=1)
    vir_lookup = jnp.sum(jnp.where(vir_match, slab_labels[None, :], 0), axis=1)
    col_labels = jnp.bitwise_xor(occ_lookup, vir_lookup)
    keep = row_labels[:, None] == col_labels[None, :]
    cycle = jnp.where(keep, sums, jnp.zeros_like(sums))
    return (ladder, cycle)


def solution(mesh):
    in_specs = (P("int", None), P("int", "amp"), P("int", "amp", None), P(), P())
    out_specs = (P("int", "amp"), P("int", "amp"))
    return jax.shard_map(
        per_device, mesh=mesh, in_specs=in_specs, out_specs=out_specs, check_vma=False
    )
```

profile of v0, /device:TPU:0, one launch (start us, length us, event | category | flops | bytes accessed | tf_op | source)
XLA Modules:
  0.0 589.0 jit_solution(9343251834261925868)
XLA Ops:
  7.2 0.7 all-gather.2.cloned.1.call-update
  7.9 0.0 reduce-scatter.3.cloned.1.call-start
  8.0 231.1 %all-gather.2.cloned.1.call-done = f32[512,6400]{1,0:T(8,128)} async-done(((f32[128,6400]{1,0:T(8,128)}), f32[512,6400]{1,0:T(8,128)}) %all-gather.2.cloned.1.call-update) | async-done | bytes 13107216 | tf_op jit(solution)/shard_map/all_gather | solution.py:16
  239.1 13.6 %fusion = f32[192,6400]{1,0:T(8,128)} fusion(f32[192,512]{1,0:T(8,128)S(1)} %copy-done, f32[512,6400]{1,0:T(8,128)} %all-gather.2.cloned.1.call-done), kind=kOutput, calls=%fused_computation.13 | convolution fusion | flops 7549747200 | bytes 18415616 | tf_op jit(solution)/shard_map/dot_general | solution.py:14
  252.7 7.9 %reshape.63 = f32[2,96,8,800]{3,2,1,0:T(8,128)} reshape(f32[192,6400]{1,0:T(8,128)} %fusion) | data formatting | bytes 9830400 | tf_op jit(solution)/shard_map/reshape | solution.py:22
  260.6 7.8 %copy.30 = f32[2,96,8,800]{1,2,0,3:T(8,128)} copy(f32[2,96,8,800]{3,2,1,0:T(8,128)} %reshape.63) | data formatting | bytes 9830400 | tf_op jit(solution)/shard_map/reshape | solution.py:22
  268.4 79.8 %all_to_all.36 = f32[2,96,8,800]{1,2,0,3:T(8,128)} all-to-all(f32[2,96,8,800]{1,2,0,3:T(8,128)} %copy.30), channel_id=1, replica_groups=mesh['amp'=8,'int'=4] {'amp'}, dimensions={3} | all-to-all | bytes 9830400 | tf_op jit(solution)/shard_map/all_to_all | solution.py:25
  348.1 7.6 %copy.32 = f32[2,96,8,8,100]{4,3,2,1,0:T(8,128)} copy(f32[2,96,8,8,100]{1,3,0,4,2:T(8,128)} %bitcast.18) | data formatting | bytes 9830400 | tf_op jit(solution)/shard_map/all_to_all | solution.py:25
  355.7 3.4 copy.33
  359.1 140.4 %all_to_all.37 = f32[2,96,64,100]{3,2,0,1:T(8,128)S(1)} all-to-all(f32[2,96,64,100]{3,2,0,1:T(8,128)S(1)} %copy.33), channel_id=1, replica_groups=mesh['amp'=8,'int'=4] {'int'}, dimensions={1} | all-to-all | bytes 9830400 | tf_op jit(solution)/shard_map/all_to_all | solution.py:24
  499.5 1.1 copy.35
  500.6 6.2 %copy.36 = f32[8,64,100,24]{2,3,1,0:T(8,128)} copy(f32[8,64,100,24]{2,1,3,0:T(8,128)S(1)} %bitcast.21) | data formatting | bytes 9830400 | tf_op jit(solution)/shard_map/ikac,kcn->ian/dot_general | solution.py:31
  506.8 6.5 %copy.37 = f32[512,100,24]{0,2,1:T(8,128)} copy(f32[512,100,24]{1,2,0:T(8,128)} %bitcast.22) | data formatting | bytes 9830400 | tf_op jit(solution)/shard_map/ikac,kcn->ian/dot_general | solution.py:31
  513.3 12.2 %convolution_bitcast_fusion = f32[512,512]{0,1:T(8,128)} fusion(f32[512,100,24]{0,2,1:T(8,128)} %copy.37, f32[24,100,512]{2,0,1:T(8,128)} %param.7), kind=kOutput, calls=%fused_computation | convolution fusion | flops 7549747200 | bytes 10878976 | tf_op jit(solution)/shard_map/ikac,kcn->ian/dot_general | solution.py:31
  525.5 0.0 reduce-scatter.5.cloned.1.call-start
  525.5 0.7 slice.3
  526.2 0.1 dynamic_slice.3
  526.3 0.1 broadcast_xor_fusion
  526.4 33.3 %reduce-scatter.3.cloned.1.call-done = f32[512,64]{0,1:T(8,128)} async-done(((f32[512,512]{0,1:T(8,128)}), f32[512,64]{0,1:T(8,128)}) %reduce-scatter.3.cloned.1.call-update) | async-done | bytes 131088 | tf_op jit(solution)/shard_map/reduce_scatter | solution.py:35
  559.7 0.1 xor.30
  559.8 0.2 select_reduce_fusion.1
  560.0 0.2 select_reduce_fusion
  560.1 20.8 %reduce-scatter.5.cloned.1.call-done = f32[128,64]{0,1:T(8,128)} async-done(((f32[512,64]{0,1:T(8,128)}), f32[128,64]{0,1:T(8,128)}) %reduce-scatter.5.cloned.1.call-update) | async-done | bytes 32784 | tf_op jit(solution)/shard_map/reduce_scatter | solution.py:36
  581.0 1.4 compare_select_fusion
  (11 shorter events, 0.1 us)
Async XLA Ops:
  7.2 231.9 %copy-start = (f32[192,512]{1,0:T(8,128)S(1)}, f32[192,512]{1,0:T(8,128)}, u32[]{:S(2)}) copy-start(f32[192,512]{1,0:T(8,128)} %param.5) | copy-start | bytes 1179652
  7.2 231.9 %all-gather.2.cloned.1.call-start = ((), (), s32[]{:S(2)}) async-start(), calls=%async_computation.4 | async-start | bytes 16384000 | tf_op jit(solution)/shard_map/all_gather | solution.py:16
  7.9 551.7 %reduce-scatter.3.cloned.1.call-start = ((), (), s32[]{:S(2)}) async-start(), calls=%async_computation.5 | async-start | bytes 1179648 | tf_op jit(solution)/shard_map/reduce_scatter | solution.py:35
  506.8 75.6 %copy-start.1 = (f32[192,512]{1,0:T(8,128)S(1)}, f32[192,512]{1,0:T(8,128)}, u32[]{:S(2)}) copy-start(f32[192,512]{1,0:T(8,128)} %param.5) | copy-start | bytes 1179652
  513.3 13.0 %copy-start.2 = (s32[96]{0:T(128)S(1)}, s32[96]{0:T(128)}, u32[]{:S(2)}) copy-start(s32[96]{0:T(128)} %param.8) | copy-start | bytes 1156
  525.5 55.5 %reduce-scatter.5.cloned.1.call-start = ((), (), s32[]{:S(2)}) async-start(), calls=%async_computation.6 | async-start | bytes 163840 | tf_op jit(solution)/shard_map/reduce_scatter | solution.py:36
Sparse Core Ops, SparseCore 0:
  9.6 229.4 all-gather.1
  525.6 33.9 reduce-scatter.2
  561.9 19.0 reduce-scatter.4
where the time goes:
time: 590 us; the launch traced here: 589 us
  waiting for transfers between devices  286 us (48%)
  blocking collectives  220 us (37%)
  local copies, waits for them, and re-layouts  41.3 us (7%)
  matrix products  25.8 us (4%)
  between operations  13.8 us (2%)
    all_gather x1, waiting for transfers between devices, per_device(): lax.all_gather(slab_integrals, 'int', axis=0, tiled=True)  231 us
    all_to_all x1, blocking collectives, per_device(): lax.all_to_all(lax.all_to_all(blocks, 'amp', split_axis=3, concat_axis=2,...  140 us
    all_to_all x1, blocking collectives, per_device(): lax.all_to_all(blocks, 'amp', split_axis=3, concat_axis=2, tiled=True)  79.8 us
    reduce_scatter x1, waiting for transfers between devices, per_device(): lax.psum_scatter(partial_value, 'amp', scatter_dimension=1, tiled=True)  33.3 us
    reduce_scatter x1, waiting for transfers between devices, per_device(): sums = lax.psum_scatter(narrowed, 'int', scatter_dimension=0, tiled=True)  20.8 us
    reshape x2, local copies, waits for them, and re-layouts, per_device(): blocks = ladder.reshape(i_local, NOCC, a_local, NVIR)  15.6 us
    dot_general x1, matrix products, per_device(): jnp.dot(amplitudes, lax.all_gather(slab_integrals, 'int', axis=0, tiled=T...  13.6 us
    dot_general x2, local copies, waits for them, and re-layouts, per_device(): jnp.einsum('ikac,kcn->ian', moved, cycle_integrals, precision=lax.Precisi...  12.7 us
  transfers between devices with their start and end apart: 3, of which 3 were waited for; matrix products, arithmetic and copies ran while one was open for 0% of the time, Pallas kernels for 0%

commit v1 on v0

v1 whole, which is shorter than its diff:
```python
import jax
import jax.numpy as jnp
from jax import lax
from jax.sharding import PartitionSpec as P

HIGHEST = lax.Precision.HIGHEST
CHUNKS = 4


def per_device(amplitudes, slab_integrals, cycle_integrals, occ_irrep, vir_irrep, n_amp, n_int):
    nocc = occ_irrep.shape[0]
    nvir = vir_irrep.shape[0]
    rows, pw = amplitudes.shape
    pw_local = slab_integrals.shape[0]
    i_local = rows // nocc
    ibat = i_local * n_int
    width = slab_integrals.shape[1]
    a_local = width // nvir
    slab = a_local * n_amp
    k_local, c_local, columns = cycle_integrals.shape
    chunks = CHUNKS
    while a_local % chunks:
        chunks -= 1
    a_chunk = a_local // chunks

    t_cyc = lax.all_to_all(
        amplitudes.reshape(i_local, nocc, pw), "int", split_axis=1, concat_axis=0, tiled=True
    ).reshape(ibat * k_local, pw)

    slab3 = slab_integrals.reshape(pw_local, a_local, nvir)
    ladder_chunks = []
    cycle_chunks = []
    for t in range(chunks):
        v = slab3[:, t * a_chunk:(t + 1) * a_chunk, :].reshape(pw_local, a_chunk * nvir)
        v_all = lax.all_gather(v, "int", axis=0, tiled=True)
        ladder_chunks.append(
            jnp.dot(amplitudes, v_all, precision=HIGHEST, preferred_element_type=jnp.float32)
        )
        l_cyc = jnp.dot(t_cyc, v_all, precision=HIGHEST, preferred_element_type=jnp.float32)
        l_cyc = l_cyc.reshape(ibat, k_local, a_chunk, nvir)
        moved = lax.all_to_all(l_cyc, "amp", split_axis=3, concat_axis=2, tiled=True)
        cycle_chunks.append(
            jnp.einsum("ikac,kcn->ian", moved, cycle_integrals, precision=HIGHEST)
        )
    ladder = jnp.concatenate(ladder_chunks, axis=1)

    parts = jnp.stack(cycle_chunks, 0).reshape(chunks, ibat, n_amp, a_chunk, columns)
    parts = parts.transpose(1, 2, 0, 3, 4).reshape(ibat * slab, columns)
    narrowed = lax.psum_scatter(parts, "amp", scatter_dimension=1, tiled=True)
    sums = lax.psum_scatter(narrowed, "int", scatter_dimension=0, tiled=True)

    col_local = sums.shape[1]
    row_start = lax.axis_index("int") * i_local
    batch_labels = lax.dynamic_slice_in_dim(occ_irrep, row_start, i_local, 0)
    slab_labels = vir_irrep[:slab]
    row_labels = jnp.bitwise_xor(batch_labels[:, None], slab_labels[None, :]).reshape(-1)
    col_ids = lax.axis_index("amp") * col_local + jnp.arange(col_local, dtype=jnp.int32)
    col_occ = col_ids // slab
    col_vir = col_ids % slab
    occ_match = col_occ[:, None] == jnp.arange(nocc, dtype=jnp.int32)[None, :]
    vir_match = col_vir[:, None] == jnp.arange(slab, dtype=jnp.int32)[None, :]
    occ_lookup = jnp.sum(jnp.where(occ_match, occ_irrep[None, :], 0), axis=1)
    vir_lookup = jnp.sum(jnp.where(vir_match, slab_labels[None, :], 0), axis=1)
    col_labels = jnp.bitwise_xor(occ_lookup, vir_lookup)
    keep = row_labels[:, None] == col_labels[None, :]
    cycle = jnp.where(keep, sums, jnp.zeros_like(sums))
    return (ladder, cycle)


def solution(mesh):
    n_amp = mesh.shape["amp"]
    n_int = mesh.shape["int"]
    in_specs = (P("int", None), P("int", "amp"), P("int", "amp", None), P(), P())
    out_specs = (P("int", "amp"), P("int", "amp"))

    def body(*args):
        return per_device(*args, n_amp=n_amp, n_int=n_int)

    return jax.shard_map(
        body, mesh=mesh, in_specs=in_specs, out_specs=out_specs, check_vma=False
    )
```

time: 590 us -> 528 us (0.89)
  blocking collectives: 220 us -> 30.3 us
  local copies, waits for them, and re-layouts: 41.3 us -> 162 us
  waiting for transfers between devices: 286 us -> 178 us
  matrix products: 25.8 us -> 98.3 us
  other arithmetic: 1.89 us -> 21.2 us
  starting transfers between devices: 0.12 us -> 17.6 us
    all_to_all x2 -> x1, blocking collectives: 220 us -> 30.3 us  [per_device(): lax.all_to_all(amplitudes.reshape(i_local, nocc, pw), 'int', split_axis=1...]
    unnamed x6 -> x38, local copies, waits for them, and re-layouts: 0.02 us -> 118 us
    all_gather x1 -> x4, waiting for transfers between devices: 231 us -> 149 us  [per_device(): v_all = lax.all_gather(v, 'int', axis=0, tiled=True)]
    dot_general x2 -> x12, matrix products: 25.8 us -> 98.3 us  [the longest x4 56.6 us: per_device(): jnp.einsum('ikac,kcn->ian', moved, cycle_integrals, precision=HIGHEST)]
    reduce_scatter x1 -> x0, waiting for transfers between devices: 33.3 us -> none  [per_device(): lax.psum_scatter(partial_value, 'amp', scatter_dimension=1, tiled=True)]
    unnamed x3 -> x7, waiting for transfers between devices: 0.71 us -> 21.1 us
    all_to_all x0 -> x4, other arithmetic: none -> 19.7 us  [per_device(): lax.all_to_all(l_cyc, 'amp', split_axis=3, concat_axis=2, tiled=True)]
    all_to_all x0 -> x4, starting transfers between devices: none -> 17.2 us  [per_device(): lax.all_to_all(l_cyc, 'amp', split_axis=3, concat_axis=2, tiled=True)]
  transfers between devices with their start and end apart: 3 -> 10, of which waited for: 3 -> 6; matrix products, arithmetic and copies ran while one was open for 0% -> 45% of each run, Pallas kernels for 0% -> 0%
where the time goes in v1:
time: 528 us; the launch traced here: 522 us
  waiting for transfers between devices  178 us (34%)
  local copies, waits for them, and re-layouts  162 us (31%)
  matrix products  98.3 us (19%)
  blocking collectives  30.3 us (6%)
  other arithmetic  21.2 us (4%)
  starting transfers between devices  17.6 us (3%)
  between operations  14.7 us (3%)
    all_gather x4, waiting for transfers between devices, per_device(): v_all = lax.all_gather(v, 'int', axis=0, tiled=True)  149 us
    unnamed x38, local copies, waits for them, and re-layouts  118 us
    dot_general x4, matrix products, per_device(): jnp.einsum('ikac,kcn->ian', moved, cycle_integrals, precision=HIGHEST)  56.6 us
    all_to_all x1, blocking collectives, per_device(): lax.all_to_all(amplitudes.reshape(i_local, nocc, pw), 'int', split_axis=1...  30.3 us
    dot_general x4, local copies, waits for them, and re-layouts, per_device(): jnp.dot(t_cyc, v_all, precision=HIGHEST, preferred_element_type=jnp.float32)  29.4 us
    dot_general x4, matrix products, per_device(): jnp.dot(t_cyc, v_all, precision=HIGHEST, preferred_element_type=jnp.float32)  21.3 us
    unnamed x7, waiting for transfers between devices  21.1 us
    dot_general x4, matrix products, per_device(): jnp.dot(amplitudes, v_all, precision=HIGHEST, preferred_element_type=jnp....  20.4 us
  transfers between devices with their start and end apart: 10, of which 6 were waited for; matrix products, arithmetic and copies ran while one was open for 45% of the time, Pallas kernels for 0%

profile of v1, /device:TPU:0, one launch (start us, length us, event | category | flops | bytes accessed | tf_op | source)
XLA Modules:
  0.0 522.0 jit_solution(12835926619351992455)
XLA Ops:
  14.9 30.3 %all_to_all.87 = f32[2,96,512]{2,0,1:T(2,128)S(1)} all-to-all(f32[2,96,512]{2,0,1:T(2,128)S(1)} %copy.67), channel_id=1, replica_groups=mesh['amp'=8,'int'=4] {'int'}, dimensions={1} | all-to-all | bytes 786432 | tf_op jit(solution)/shard_map/all_to_all | solution.py:26
  45.3 43.1 %all-gather.5.cloned.1.call-done = f32[512,1600]{0,1:T(8,128)} async-done(((f32[128,1600]{0,1:T(8,128)}), f32[512,1600]{0,1:T(8,128)}) %all-gather.5.cloned.1.call-update) | async-done | bytes 3276816 | tf_op jit(solution)/shard_map/all_gather | solution.py:35
  93.7 7.3 %copy.70 = f32[8,24,2,800]{1,2,0,3:T(2,128)} copy(f32[8,24,2,800]{3,1,2,0:T(8,128)S(1)} %fusion.41) | data formatting | bytes 2457600 | tf_op jit(solution)/shard_map/dot_general | solution.py:39
  101.1 13.5 %reshape.159 = f32[8,1,38400]{2,1,0:T(1,128)} reshape(f32[800,8,2,24]{3,2,1,0:T(2,128)} %bitcast.141) | data formatting | bytes 2457600
  118.8 37.3 %all-gather.7.cloned.1.call-done = f32[512,1600]{0,1:T(8,128)} async-done(((f32[128,1600]{0,1:T(8,128)}), f32[512,1600]{0,1:T(8,128)}) %all-gather.7.cloned.1.call-update) | async-done | bytes 3276816 | tf_op jit(solution)/shard_map/all_gather | solution.py:35
  161.5 7.3 %copy.74 = f32[8,24,2,800]{1,2,0,3:T(2,128)} copy(f32[8,24,2,800]{3,1,2,0:T(8,128)S(1)} %fusion.42) | data formatting | bytes 2457600 | tf_op jit(solution)/shard_map/dot_general | solution.py:39
  168.8 13.5 %reshape.157 = f32[8,1,38400]{2,1,0:T(1,128)} reshape(f32[800,8,2,24]{3,2,1,0:T(2,128)} %bitcast.142) | data formatting | bytes 2457600
  186.6 34.9 %all-gather.9.cloned.1.call-done = f32[512,1600]{0,1:T(8,128)} async-done(((f32[128,1600]{0,1:T(8,128)}), f32[512,1600]{0,1:T(8,128)}) %all-gather.9.cloned.1.call-update) | async-done | bytes 3276816 | tf_op jit(solution)/shard_map/all_gather | solution.py:35
  226.8 7.3 %copy.78 = f32[8,24,2,800]{1,2,0,3:T(2,128)} copy(f32[8,24,2,800]{3,1,2,0:T(8,128)S(1)} %fusion.43) | data formatting | bytes 2457600 | tf_op jit(solution)/shard_map/dot_general | solution.py:39
  234.2 13.5 %reshape.155 = f32[8,1,38400]{2,1,0:T(1,128)} reshape(f32[800,8,2,24]{3,2,1,0:T(2,128)} %bitcast.143) | data formatting | bytes 2457600
  252.9 33.8 %all-gather.11.cloned.1.call-done = f32[512,1600]{0,1:T(8,128)} async-done(((f32[128,1600]{0,1:T(8,128)}), f32[512,1600]{0,1:T(8,128)}) %all-gather.11.cloned.1.call-update) | async-done | bytes 3276816 | tf_op jit(solution)/shard_map/all_gather | solution.py:35
  292.0 7.3 %copy.82 = f32[8,24,2,800]{1,2,0,3:T(2,128)} copy(f32[8,24,2,800]{3,1,2,0:T(8,128)S(1)} %fusion.44) | data formatting | bytes 2457600 | tf_op jit(solution)/shard_map/dot_general | solution.py:39
  299.3 13.5 %reshape.153 = f32[8,1,38400]{2,1,0:T(1,128)} reshape(f32[800,8,2,24]{3,2,1,0:T(2,128)} %bitcast.144) | data formatting | bytes 2457600
  316.9 13.4 %reshape.160 = f32[800,8,2,24]{3,2,1,0:T(2,128)} reshape(f32[8,38400]{1,0:T(8,128)S(1)} %reduce.3) | data formatting | bytes 2457600
  335.6 13.5 %reshape.158 = f32[800,8,2,24]{3,2,1,0:T(2,128)} reshape(f32[8,38400]{1,0:T(8,128)S(1)} %reduce.2) | data formatting | bytes 2457600
  359.3 14.8 %reshape.156 = f32[800,8,2,24]{3,2,1,0:T(2,128)} reshape(f32[8,38400]{1,0:T(8,128)} %reduce.1) | data formatting | bytes 2457600
  374.1 13.5 %fusion.16 = f32[1,8,8,2,512]{4,2,3,1,0:T(8,128)S(1)} fusion(f32[24,100,512]{2,0,1:T(8,128)} %param.7, f32[8,24,2,8,100]{1,2,0,4,3:T(2,128)} %bitcast.155), kind=kOutput, calls=%fused_computation.16 | convolution fusion | flops 1887436800 | bytes 6406144 | tf_op jit(solution)/shard_map/ikac,kcn->ian/dot_general | solution.py:43
  387.7 20.4 %fusion.21 = f32[1,8,8,2,512]{4,2,3,1,0:T(8,128)S(1)} fusion(f32[24,100,512]{2,0,1:T(8,128)} %param.7, f32[8,24,2,8,100]{1,2,0,4,3:T(2,128)S(1)} %bitcast.158), kind=kOutput, calls=%fused_computation.17 | convolution fusion | flops 1887436800 | bytes 6406144 | tf_op jit(solution)/shard_map/ikac,kcn->ian/dot_general | solution.py:43
  408.1 9.5 %fusion.26 = f32[1,8,8,2,512]{4,2,3,1,0:T(8,128)S(1)} fusion(f32[24,100,512]{2,0,1:T(8,128)S(1)} %bitcast.171, f32[8,24,2,8,100]{1,2,0,4,3:T(2,128)S(1)} %bitcast.161), kind=kOutput, calls=%fused_computation.18 | convolution fusion | flops 1887436800 | bytes 6406144 | tf_op jit(solution)/shard_map/ikac,kcn->ian/dot_general | solution.py:43
  422.7 13.4 %reshape.154 = f32[800,8,2,24]{3,2,1,0:T(2,128)} reshape(f32[8,38400]{1,0:T(8,128)S(1)} %reduce) | data formatting | bytes 2457600
  436.1 13.2 %fusion.31 = f32[1,8,8,2,512]{4,2,3,1,0:T(8,128)S(1)} fusion(f32[24,100,512]{2,0,1:T(8,128)} %param.7, f32[8,24,2,8,100]{1,2,0,4,3:T(2,128)} %bitcast.162), kind=kOutput, calls=%fused_computation.19 | convolution fusion | flops 1887436800 | bytes 6406144 | tf_op jit(solution)/shard_map/ikac,kcn->ian/dot_general | solution.py:43
  472.4 19.2 %reduce-scatter.7.cloned.1.call-done = f32[64,512]{1,0:T(8,128)} async-done(((f32[512,512]{1,0:T(8,128)}), f32[64,512]{1,0:T(8,128)}) %reduce-scatter.7.cloned.1.call-update) | async-done | bytes 131088
  498.9 6.6 %concatenate.4 = f32[192,6400]{1,0:T(8,128)} concatenate(f32[192,1600]{1,0:T(8,128)} %fusion.37, f32[192,1600]{1,0:T(8,128)} %fusion.38, f32[192,1600]{1,0:T(8,128)} %fusion.39, f32[192,1600]{1,0:T(8,128)} %fusion.40), dimensions={1} | concatenate | bytes 9830400 | tf_op jit(solution)/shard_map/concatenate | solution.py:45
  505.4 7.9 %reduce-scatter.5.cloned.1.call-done = f32[128,64]{1,0:T(8,128)} async-done(((f32[512,64]{1,0:T(8,128)}), f32[128,64]{1,0:T(8,128)}) %reduce-scatter.5.cloned.1.call-update) | async-done | bytes 32784 | tf_op jit(solution)/shard_map/reduce_scatter | solution.py:50
  (82 shorter events, 99.3 us)
Async XLA Ops:
  7.2 81.2 %all-gather.5.cloned.1.call-start = ((), (), s32[]{:S(2)}) async-start(), calls=%async_computation.7 | async-start | bytes 4096000 | tf_op jit(solution)/shard_map/all_gather | solution.py:35
  12.5 2.1 copy-start.4
  12.5 143.6 %all-gather.7.cloned.1.call-start = ((), (), s32[]{:S(2)}) async-start(), calls=%async_computation.8 | async-start | bytes 4096000 | tf_op jit(solution)/shard_map/all_gather | solution.py:35
  13.2 208.2 %all-gather.9.cloned.1.call-start = ((), (), s32[]{:S(2)}) async-start(), calls=%async_computation.9 | async-start | bytes 4096000 | tf_op jit(solution)/shard_map/all_gather | solution.py:35
  14.0 272.7 %all-gather.11.cloned.1.call-start = ((), (), s32[]{:S(2)}) async-start(), calls=%async_computation.10 | async-start | bytes 4096000 | tf_op jit(solution)/shard_map/all_gather | solution.py:35
  114.6 67.7 %all-to-all-start.1 = ((f32[8,1,38400]{2,1,0:T(1,128)}), f32[8,1,38400]{2,1,0:T(1,128)S(1)}, u32[]{:S(2)}, u32[]{:S(2)}) async-start(f32[8,1,38400]{2,1,0:T(1,128)} %reshape.159), calls=%async_computation.1 | async-start | bytes 2457600 | tf_op jit(solution)/shard_map/all_to_all | solution.py:41
  182.3 65.4 %all-to-all-start.2 = ((f32[8,1,38400]{2,1,0:T(1,128)}), f32[8,1,38400]{2,1,0:T(1,128)}, u32[]{:S(2)}, u32[]{:S(2)}) async-start(f32[8,1,38400]{2,1,0:T(1,128)} %reshape.157), calls=%async_computation.2 | async-start | bytes 2457600 | tf_op jit(solution)/shard_map/all_to_all | solution.py:41
  234.2 18.7 %copy-start.6 = (s32[96]{0:T(128)S(1)}, s32[96]{0:T(128)}, u32[]{:S(2)}) copy-start(s32[96]{0:T(128)} %param.8) | copy-start | bytes 1156
  247.7 101.4 %all-to-all-start.3 = ((f32[8,1,38400]{2,1,0:T(1,128)}), f32[8,1,38400]{2,1,0:T(1,128)}, u32[]{:S(2)}, u32[]{:S(2)}) async-start(f32[8,1,38400]{2,1,0:T(1,128)} %reshape.155), calls=%async_computation.3 | async-start | bytes 2457600 | tf_op jit(solution)/shard_map/all_to_all | solution.py:41
  349.1 68.5 %all-to-all-start.4 = ((f32[8,1,38400]{2,1,0:T(1,128)}), f32[8,1,38400]{2,1,0:T(1,128)}, u32[]{:S(2)}, u32[]{:S(2)}) async-start(f32[8,1,38400]{2,1,0:T(1,128)} %reshape.153), calls=%async_computation.4 | async-start | bytes 2457600 | tf_op jit(solution)/shard_map/all_to_all | solution.py:41
  353.3 138.2 %reduce-scatter.7.cloned.1.call-start = ((), (), s32[]{:S(2)}) async-start(), calls=%async_computation.12 | async-start | bytes 1179648
  359.3 28.3 %slice-start = ((s8[6553600]{0:T(1024)(128)(4,1)}), s8[2359296]{0:T(1024)(128)(4,1)S(1)}, s32[]{:S(2)}) async-start(s8[6553600]{0:T(1024)(128)(4,1)} %bitcast.156), calls=%async_computation.13 | async-start | bytes 4718592
  374.1 13.5 %slice-start.1 = ((s8[6553600]{0:T(1024)(128)(4,1)}), s8[4194304]{0:T(1024)(128)(4,1)S(1)}, s32[]{:S(2)}) async-start(s8[6553600]{0:T(1024)(128)(4,1)} %bitcast.156), calls=%async_computation.14 | async-start | bytes 8388608
  374.1 33.9 %slice-start.2 = ((s8[6553600]{0:T(1024)(128)(4,1)}), s8[4194304]{0:T(1024)(128)(4,1)S(1)}, s32[]{:S(2)}) async-start(s8[6553600]{0:T(1024)(128)(4,1)} %bitcast.159), calls=%async_computation.15 | async-start | bytes 8388608
  374.1 33.9 %slice-start.4 = ((s8[4915200]{0:T(1024)(128)(4,1)}), s8[4194304]{0:T(1024)(128)(4,1)S(1)}, s32[]{:S(2)}) async-start(s8[4915200]{0:T(1024)(128)(4,1)} %bitcast.170), calls=%async_computation.17 | async-start | bytes 8388608
  387.7 20.4 %slice-start.3 = ((s8[6553600]{0:T(1024)(128)(4,1)}), s8[2359296]{0:T(1024)(128)(4,1)S(1)}, s32[]{:S(2)}) async-start(s8[6553600]{0:T(1024)(128)(4,1)} %bitcast.159), calls=%async_computation.16 | async-start | bytes 4718592
  387.7 20.4 %slice-start.5 = ((s8[4915200]{0:T(1024)(128)(4,1)}), s8[720896]{0:T(1024)(128)(4,1)S(1)}, s32[]{:S(2)}) async-start(s8[4915200]{0:T(1024)(128)(4,1)} %bitcast.170), calls=%async_computation.18 | async-start | bytes 1441792
  449.4 8.1 %copy-start = (f32[512,1600]{0,1:T(8,128)S(1)}, f32[512,1600]{0,1:T(8,128)}, u32[]{:S(2)}) copy-start(f32[512,1600]{0,1:T(8,128)} %all-gather.5.cloned.1.call-done) | copy-start | bytes 9830404
  456.7 56.7 %reduce-scatter.5.cloned.1.call-start = ((), (), s32[]{:S(2)}) async-start(), calls=%async_computation.11 | async-start | bytes 327680 | tf_op jit(solution)/shard_map/reduce_scatter | solution.py:50
  457.1 6.1 %copy-start.1 = (f32[512,1600]{0,1:T(8,128)S(1)}, f32[512,1600]{0,1:T(8,128)}, u32[]{:S(2)}) copy-start(f32[512,1600]{0,1:T(8,128)} %all-gather.7.cloned.1.call-done) | copy-start | bytes 9830404
  457.1 6.1 %copy-start.5 = (f32[192,512]{1,0:T(8,128)S(1)}, f32[192,512]{1,0:T(8,128)}, u32[]{:S(2)}) copy-start(f32[192,512]{1,0:T(8,128)} %param.5) | copy-start | bytes 1179652
  463.2 4.6 copy-start.3
  467.8 25.5 %copy-start.2 = (f32[512,1600]{0,1:T(8,128)S(1)}, f32[512,1600]{0,1:T(8,128)}, u32[]{:S(2)}) copy-start(f32[512,1600]{0,1:T(8,128)} %all-gather.11.cloned.1.call-done) | copy-start | bytes 9830404
Sparse Core Ops, SparseCore 0:
  12.6 75.7 all-gather.4
  90.5 65.5 all-gather.6
  157.7 63.7 all-gather.8
  222.9 63.7 all-gather.10
  456.8 34.6 reduce-scatter.6
  493.6 19.6 reduce-scatter.4

commit v2 on v1

--- a/solution.py
+++ b/solution.py
@@ -4,7 +4,7 @@
 from jax.sharding import PartitionSpec as P
 
 HIGHEST = lax.Precision.HIGHEST
-CHUNKS = 4
+CHUNKS = 2
 
 
 def per_device(amplitudes, slab_integrals, cycle_integrals, occ_irrep, vir_irrep, n_amp, n_int):
@@ -26,6 +26,7 @@
     t_cyc = lax.all_to_all(
         amplitudes.reshape(i_local, nocc, pw), "int", split_axis=1, concat_axis=0, tiled=True
     ).reshape(ibat * k_local, pw)
+    w2 = cycle_integrals.reshape(k_local * c_local, columns)
 
     slab3 = slab_integrals.reshape(pw_local, a_local, nvir)
     ladder_chunks = []
@@ -37,15 +38,16 @@
             jnp.dot(amplitudes, v_all, precision=HIGHEST, preferred_element_type=jnp.float32)
         )
         l_cyc = jnp.dot(t_cyc, v_all, precision=HIGHEST, preferred_element_type=jnp.float32)
-        l_cyc = l_cyc.reshape(ibat, k_local, a_chunk, nvir)
-        moved = lax.all_to_all(l_cyc, "amp", split_axis=3, concat_axis=2, tiled=True)
+        l_cyc = l_cyc.reshape(ibat, k_local, a_chunk, n_amp, c_local).transpose(3, 0, 2, 1, 4)
+        moved = lax.all_to_all(l_cyc, "amp", split_axis=0, concat_axis=0, tiled=True)
+        moved = moved.reshape(n_amp * ibat * a_chunk, k_local * c_local)
         cycle_chunks.append(
-            jnp.einsum("ikac,kcn->ian", moved, cycle_integrals, precision=HIGHEST)
+            jnp.dot(moved, w2, precision=HIGHEST, preferred_element_type=jnp.float32)
         )
     ladder = jnp.concatenate(ladder_chunks, axis=1)
 
-    parts = jnp.stack(cycle_chunks, 0).reshape(chunks, ibat, n_amp, a_chunk, columns)
-    parts = parts.transpose(1, 2, 0, 3, 4).reshape(ibat * slab, columns)
+    parts = jnp.stack(cycle_chunks, 0).reshape(chunks, n_amp, ibat, a_chunk, columns)
+    parts = parts.transpose(2, 1, 0, 3, 4).reshape(ibat * slab, columns)
     narrowed = lax.psum_scatter(parts, "amp", scatter_dimension=1, tiled=True)
     sums = lax.psum_scatter(narrowed, "int", scatter_dimension=0, tiled=True)
 

time: 528 us -> 413 us (0.78); the launches traced: 522 us -> 412 us
  local copies, waits for them, and re-layouts: 162 us -> 48.4 us
  waiting for transfers between devices: 178 us -> 228 us
  matrix products: 98.3 us -> 68.9 us
  other arithmetic: 21.2 us -> 6.47 us
  starting transfers between devices: 17.6 us -> 8.72 us
  blocking collectives: 30.3 us -> 38.4 us
    unnamed x38 -> x12, local copies, waits for them, and re-layouts: 118 us -> 7.24 us
    all_gather x4 -> x2, waiting for transfers between devices: 149 us -> 185 us  [per_device(): v_all = lax.all_gather(v, 'int', axis=0, tiled=True)]
    dot_general x4 -> x2, matrix products: 56.6 us -> 29.9 us  [per_device(): jnp.dot(moved, w2, precision=HIGHEST, preferred_element_type=jnp.float32)]
    all_to_all x4 -> x0, other arithmetic: 19.7 us -> none  [per_device(): lax.all_to_all(l_cyc, 'amp', split_axis=3, concat_axis=2, tiled=True)]
    all_to_all x1 -> x2, local copies, waits for them, and re-layouts: 0.51 us -> 16.8 us  [per_device(): lax.all_to_all(l_cyc, 'amp', split_axis=0, concat_axis=0, tiled=True)]
    all_to_all x4 -> x2, waiting for transfers between devices: 0.01 us -> 15 us  [per_device(): lax.all_to_all(l_cyc, 'amp', split_axis=0, concat_axis=0, tiled=True)]
    dot_general x4 -> x2, local copies, waits for them, and re-layouts: 29.4 us -> 14.9 us  [per_device(): jnp.dot(t_cyc, v_all, precision=HIGHEST, preferred_element_type=jnp.float32)]
    all_to_all x4 -> x2, starting transfers between devices: 17.2 us -> 8.16 us  [per_device(): lax.all_to_all(l_cyc, 'amp', split_axis=0, concat_axis=0, tiled=True)]
  transfers between devices with their start and end apart: 10 -> 6, of which waited for: 6 -> 5; matrix products, arithmetic and copies ran while one was open for 45% -> 21% of each run, Pallas kernels for 0% -> 0%
where the time goes in v2:
time: 413 us; the launch traced here: 412 us
  waiting for transfers between devices  228 us (55%)
  matrix products  68.9 us (17%)
  local copies, waits for them, and re-layouts  48.4 us (12%)
  blocking collectives  38.4 us (9%)
  between operations  13.9 us (3%)
  starting transfers between devices  8.72 us (2%)
  other arithmetic  6.47 us (2%)
    all_gather x2, waiting for transfers between devices, per_device(): v_all = lax.all_gather(v, 'int', axis=0, tiled=True)  185 us
    all_to_all x1, blocking collectives, per_device(): lax.all_to_all(amplitudes.reshape(i_local, nocc, pw), 'int', split_axis=1...  38.4 us
    dot_general x2, matrix products, per_device(): jnp.dot(moved, w2, precision=HIGHEST, preferred_element_type=jnp.float32)  29.9 us
    dot_general x2, matrix products, per_device(): jnp.dot(t_cyc, v_all, precision=HIGHEST, preferred_element_type=jnp.float32)  19.9 us
    dot_general x2, matrix products, per_device(): jnp.dot(amplitudes, v_all, precision=HIGHEST, preferred_element_type=jnp....  19.1 us
    all_to_all x2, local copies, waits for them, and re-layouts, per_device(): lax.all_to_all(l_cyc, 'amp', split_axis=0, concat_axis=0, tiled=True)  16.8 us
    reduce_scatter x1, waiting for transfers between devices, per_device(): sums = lax.psum_scatter(narrowed, 'int', scatter_dimension=0, tiled=True)  15 us
    all_to_all x2, waiting for transfers between devices, per_device(): lax.all_to_all(l_cyc, 'amp', split_axis=0, concat_axis=0, tiled=True)  15 us
  transfers between devices with their start and end apart: 6, of which 5 were waited for; matrix products, arithmetic and copies ran while one was open for 21% of the time, Pallas kernels for 0%

profile of v2, /device:TPU:0, one launch (start us, length us, event | category | flops | bytes accessed | tf_op | source)
XLA Modules:
  0.0 412.5 jit_solution(8197419634028779381)
XLA Ops:
  7.2 3.5 copy.41
  10.7 1.9 fusion.10
  14.7 38.4 %all_to_all.25 = f32[2,96,512]{2,0,1:T(2,128)S(1)} all-to-all(f32[2,96,512]{2,0,1:T(2,128)S(1)} %copy.42), channel_id=1, replica_groups=mesh['amp'=8,'int'=4] {'int'}, dimensions={1} | all-to-all | bytes 786432 | tf_op jit(solution)/shard_map/all_to_all | solution.py:26
  53.2 87.7 %all-gather.5.cloned.1.call-done = f32[512,3200]{0,1:T(8,128)} async-done(((f32[128,3200]{0,1:T(8,128)}), f32[512,3200]{0,1:T(8,128)}) %all-gather.5.cloned.1.call-update) | async-done | bytes 6553616 | tf_op jit(solution)/shard_map/all_gather | solution.py:36
  140.9 7.5 %reshape.110 = f32[4,8,100,512,1]{3,2,1,0,4:T(8,128)} reshape(f32[3200,512]{1,0:T(8,128)} %bitcast.51) | data formatting | bytes 13107200 | tf_op jit(solution)/shard_map/dot_general | solution.py:40
  148.4 10.1 %convolution_bitcast_fusion = f32[8,8,4,24,100]{4,3,0,2,1:T(8,128)S(1)} fusion(f32[8,24,512,1,1]{2,1,4,3,0:T(8,128)S(1)} %bitcast.61, f32[4,8,100,512,1]{3,2,1,0,4:T(8,128)} %reshape.110), kind=kOutput, calls=%fused_computation.5 | convolution fusion | flops 3774873600 | bytes 9404416 | tf_op jit(solution)/shard_map/dot_general | solution.py:40
  158.5 2.1 copy.47
  160.6 3.7 all-to-all-start.2
  164.3 97.3 %all-gather.3.cloned.1.call-done = f32[512,3200]{0,1:T(8,128)} async-done(((f32[128,3200]{0,1:T(8,128)}), f32[512,3200]{0,1:T(8,128)}) %all-gather.3.cloned.1.call-update) | async-done | bytes 6553616 | tf_op jit(solution)/shard_map/all_gather | solution.py:36
  261.6 7.5 %reshape.107 = f32[4,8,100,512,1]{3,2,1,0,4:T(8,128)} reshape(f32[3200,512]{1,0:T(8,128)} %bitcast.54) | data formatting | bytes 13107200 | tf_op jit(solution)/shard_map/dot_general | solution.py:40
  269.1 9.7 %convolution_bitcast_fusion.1 = f32[8,8,4,24,100]{4,3,0,2,1:T(8,128)S(1)} fusion(f32[8,24,512,1,1]{2,1,4,3,0:T(8,128)S(1)} %bitcast.62, f32[4,8,100,512,1]{3,2,1,0,4:T(8,128)} %reshape.107), kind=kOutput, calls=%fused_computation.6 | convolution fusion | flops 3774873600 | bytes 9404416 | tf_op jit(solution)/shard_map/dot_general | solution.py:40
  278.8 2.1 copy.45
  280.9 4.4 %all-to-all-start.1 = ((f32[8,8,4,24,100]{4,3,2,1,0:T(8,128)}), f32[8,8,4,24,100]{4,3,2,1,0:T(8,128)}, u32[]{:S(2)}, u32[]{:S(2)}) async-start(f32[8,8,4,24,100]{4,3,2,1,0:T(8,128)} %copy.45), calls=%async_computation.1 | async-start | bytes 6291456 | tf_op jit(solution)/shard_map/all_to_all | solution.py:42
  285.6 7.7 %copy.48 = f32[8,8,4,24,100]{3,1,4,2,0:T(8,128)} copy(f32[8,8,4,24,100]{4,3,2,1,0:T(8,128)S(1)} %all-to-all-done.2) | data formatting | bytes 4915200 | tf_op jit(solution)/shard_map/all_to_all | solution.py:42
  293.3 14.9 %fusion.7 = f32[1,8,8,4,512]{4,2,3,1,0:T(8,128)S(1)} fusion(f32[8,8,4,24,100]{3,1,4,2,0:T(8,128)} %copy.48, f32[24,100,512]{2,0,1:T(8,128)} %param.7), kind=kOutput, calls=%fused_computation.8 | convolution fusion | flops 3774873600 | bytes 7897088 | tf_op jit(solution)/shard_map/dot_general | solution.py:45
  308.2 15.0 %all-to-all-done.1 = f32[8,8,4,24,100]{4,3,2,1,0:T(8,128)} async-done(((f32[8,8,4,24,100]{4,3,2,1,0:T(8,128)}), f32[8,8,4,24,100]{4,3,2,1,0:T(8,128)}, u32[]{:S(2)}, u32[]{:S(2)}) %all-to-all-start.1) | async-done | bytes 2457632 | tf_op jit(solution)/shard_map/all_to_all | solution.py:42
  323.2 9.1 %copy.46 = f32[8,8,4,24,100]{3,1,4,2,0:T(8,128)} copy(f32[8,8,4,24,100]{4,3,2,1,0:T(8,128)} %all-to-all-done.1) | data formatting | bytes 4915200 | tf_op jit(solution)/shard_map/all_to_all | solution.py:42
  332.4 15.0 %fusion.4 = f32[1,8,8,4,512]{4,2,3,1,0:T(8,128)S(1)} fusion(f32[8,8,4,24,100]{3,1,4,2,0:T(8,128)} %copy.46, f32[24,100,512]{2,0,1:T(8,128)} %param.7), kind=kOutput, calls=%fused_computation.7 | convolution fusion | flops 3774873600 | bytes 7897088 | tf_op jit(solution)/shard_map/dot_general | solution.py:45
  351.5 11.2 %fusion.11 = f32[192,3200]{1,0:T(8,128)} fusion(f32[192,512]{1,0:T(8,128)} %param.5, f32[512,3200]{0,1:T(8,128)} %all-gather.3.cloned.1.call-done), kind=kOutput, calls=%fused_computation.23 | convolution fusion | flops 3774873600 | bytes 9404416 | tf_op jit(solution)/shard_map/dot_general | solution.py:38
  362.7 8.0 %fusion.12 = f32[192,3200]{1,0:T(8,128)} fusion(f32[192,512]{1,0:T(8,128)S(1)} %copy-done, f32[512,3200]{0,1:T(8,128)S(1)} %bitcast.53), kind=kOutput, calls=%fused_computation.24 | convolution fusion | flops 3774873600 | bytes 9404416 | tf_op jit(solution)/shard_map/dot_general | solution.py:38
  370.6 11.9 %reduce-scatter.7.cloned.1.call-done = f32[64,512]{1,0:T(8,128)} async-done(((f32[512,512]{1,0:T(8,128)}), f32[64,512]{1,0:T(8,128)}) %reduce-scatter.7.cloned.1.call-update) | async-done | bytes 131088
  382.5 1.7 copy.56
  384.3 5.0 %pad_maximum_fusion = f32[192,6400]{1,0:T(8,128)} fusion(f32[192,3200]{1,0:T(8,128)} %fusion.12, f32[192,3200]{1,0:T(8,128)} %fusion.11), kind=kLoop, calls=%fused_computation | loop fusion | flops 1228800 | bytes 9830400 | tf_op jit(solution)/shard_map/concatenate | solution.py:47
  389.3 15.0 %reduce-scatter.5.cloned.1.call-done = f32[128,64]{1,0:T(8,128)} async-done(((f32[512,64]{1,0:T(8,128)}), f32[128,64]{1,0:T(8,128)}) %reduce-scatter.5.cloned.1.call-update) | async-done | bytes 32784 | tf_op jit(solution)/shard_map/reduce_scatter | solution.py:52
  (35 shorter events, 8.1 us)
Async XLA Ops:
  7.2 133.7 %all-gather.5.cloned.1.call-start = ((), (), s32[]{:S(2)}) async-start(), calls=%async_computation.6 | async-start | bytes 8192000 | tf_op jit(solution)/shard_map/all_gather | solution.py:36
  12.7 249.0 %all-gather.3.cloned.1.call-start = ((), (), s32[]{:S(2)}) async-start(), calls=%async_computation.5 | async-start | bytes 8192000 | tf_op jit(solution)/shard_map/all_gather | solution.py:36
  160.6 120.3 %all-to-all-start.2 = ((f32[8,8,4,24,100]{4,3,2,1,0:T(8,128)}), f32[8,8,4,24,100]{4,3,2,1,0:T(8,128)S(1)}, u32[]{:S(2)}, u32[]{:S(2)}) async-start(f32[8,8,4,24,100]{4,3,2,1,0:T(8,128)} %copy.47), calls=%async_computation.2 | async-start | bytes 6291456 | tf_op jit(solution)/shard_map/all_to_all | solution.py:42
  280.9 42.3 %all-to-all-start.1 = ((f32[8,8,4,24,100]{4,3,2,1,0:T(8,128)}), f32[8,8,4,24,100]{4,3,2,1,0:T(8,128)}, u32[]{:S(2)}, u32[]{:S(2)}) async-start(f32[8,8,4,24,100]{4,3,2,1,0:T(8,128)} %copy.45), calls=%async_computation.1 | async-start | bytes 6291456 | tf_op jit(solution)/shard_map/all_to_all | solution.py:42
  285.4 97.2 %reduce-scatter.7.cloned.1.call-start = ((), (), s32[]{:S(2)}) async-start(), calls=%async_computation.8 | async-start | bytes 1179648
  347.4 3.5 copy-start.1
  348.6 14.1 %slice-start = ((s8[6553600]{0:T(1024)(128)(4,1)}), s8[2359296]{0:T(1024)(128)(4,1)S(1)}, s32[]{:S(2)}) async-start(s8[6553600]{0:T(1024)(128)(4,1)} %bitcast.52), calls=%async_computation.9 | async-start | bytes 4718592
  349.9 12.8 %copy-start = (f32[192,512]{1,0:T(8,128)S(1)}, f32[192,512]{1,0:T(8,128)}, u32[]{:S(2)}) copy-start(f32[192,512]{1,0:T(8,128)} %param.5) | copy-start | bytes 1179652
  349.9 54.4 %reduce-scatter.5.cloned.1.call-start = ((), (), s32[]{:S(2)}) async-start(), calls=%async_computation.7 | async-start | bytes 327680 | tf_op jit(solution)/shard_map/reduce_scatter | solution.py:52
  351.5 11.2 %slice-start.1 = ((s8[6553600]{0:T(1024)(128)(4,1)}), s8[4194304]{0:T(1024)(128)(4,1)S(1)}, s32[]{:S(2)}) async-start(s8[6553600]{0:T(1024)(128)(4,1)} %bitcast.52), calls=%async_computation.10 | async-start | bytes 8388608
Sparse Core Ops, SparseCore 0:
  12.8 128.0 all-gather.4
  142.4 119.1 all-gather.2
  350.0 32.4 reduce-scatter.6
  384.6 19.6 reduce-scatter.4

commit v3 on v2

--- a/solution.py
+++ b/solution.py
@@ -26,7 +26,7 @@
     t_cyc = lax.all_to_all(
         amplitudes.reshape(i_local, nocc, pw), "int", split_axis=1, concat_axis=0, tiled=True
     ).reshape(ibat * k_local, pw)
-    w2 = cycle_integrals.reshape(k_local * c_local, columns)
+    w2 = cycle_integrals.transpose(1, 0, 2).reshape(c_local * k_local, columns)
 
     slab3 = slab_integrals.reshape(pw_local, a_local, nvir)
     ladder_chunks = []
@@ -34,24 +34,31 @@
     for t in range(chunks):
         v = slab3[:, t * a_chunk:(t + 1) * a_chunk, :].reshape(pw_local, a_chunk * nvir)
         v_all = lax.all_gather(v, "int", axis=0, tiled=True)
+        if t:
+            v_all, ladder_chunks[-1], cycle_chunks[-1] = lax.optimization_barrier(
+                (v_all, ladder_chunks[-1], cycle_chunks[-1])
+            )
         ladder_chunks.append(
             jnp.dot(amplitudes, v_all, precision=HIGHEST, preferred_element_type=jnp.float32)
         )
         l_cyc = jnp.dot(t_cyc, v_all, precision=HIGHEST, preferred_element_type=jnp.float32)
-        l_cyc = l_cyc.reshape(ibat, k_local, a_chunk, n_amp, c_local).transpose(3, 0, 2, 1, 4)
+        l_cyc = l_cyc.reshape(ibat, k_local, a_chunk, n_amp, c_local).transpose(3, 0, 2, 4, 1)
+        l_cyc = l_cyc.reshape(n_amp, ibat * a_chunk, c_local * k_local)
         moved = lax.all_to_all(l_cyc, "amp", split_axis=0, concat_axis=0, tiled=True)
-        moved = moved.reshape(n_amp * ibat * a_chunk, k_local * c_local)
+        moved = moved.reshape(n_amp * ibat * a_chunk, c_local * k_local)
         cycle_chunks.append(
             jnp.dot(moved, w2, precision=HIGHEST, preferred_element_type=jnp.float32)
         )
     ladder = jnp.concatenate(ladder_chunks, axis=1)
 
-    parts = jnp.stack(cycle_chunks, 0).reshape(chunks, n_amp, ibat, a_chunk, columns)
-    parts = parts.transpose(2, 1, 0, 3, 4).reshape(ibat * slab, columns)
-    narrowed = lax.psum_scatter(parts, "amp", scatter_dimension=1, tiled=True)
-    sums = lax.psum_scatter(narrowed, "int", scatter_dimension=0, tiled=True)
+    col_local = columns // n_amp
+    parts = jnp.stack(cycle_chunks, 0).reshape(
+        chunks, n_amp, n_int, i_local, a_chunk, n_amp, col_local
+    )
+    parts = parts.transpose(2, 5, 3, 1, 0, 4, 6).reshape(n_int * n_amp, i_local * slab * col_local)
+    sums = lax.psum_scatter(parts, ("int", "amp"), scatter_dimension=0, tiled=True)
+    sums = sums.reshape(i_local * slab, col_local)
 
-    col_local = sums.shape[1]
     row_start = lax.axis_index("int") * i_local
     batch_labels = lax.dynamic_slice_in_dim(occ_irrep, row_start, i_local, 0)
     slab_labels = vir_irrep[:slab]

time: 413 us -> 492 us (1.19); the launches traced: 412 us -> 485 us
  waiting for transfers between devices: 228 us -> 280 us
  local copies, waits for them, and re-layouts: 48.4 us -> 77.1 us
  matrix products: 68.9 us -> 62.9 us
    unnamed x5 -> x4, waiting for transfers between devices: 12.6 us -> 123 us
    all_gather x2, waiting for transfers between devices: 185 us -> 129 us  [per_device(): v_all = lax.all_gather(v, 'int', axis=0, tiled=True)]
    reshape x1 -> x6, local copies, waits for them, and re-layouts: 0.36 us -> 37.4 us  [the longest x2 19 us: per_device(): l_cyc = l_cyc.reshape(n_amp, ibat * a_chunk, c_local * k_local)]
    all_to_all x2 -> x1, local copies, waits for them, and re-layouts: 16.8 us -> 1.44 us  [per_device(): lax.all_to_all(l_cyc, 'amp', split_axis=0, concat_axis=0, tiled=True)]
    reduce_scatter x1 -> x0, waiting for transfers between devices: 15 us -> none  [per_device(): sums = lax.psum_scatter(narrowed, 'int', scatter_dimension=0, tiled=True)]
    all_to_all x2, waiting for transfers between devices: 15 us -> 28.8 us  [per_device(): lax.all_to_all(l_cyc, 'amp', split_axis=0, concat_axis=0, tiled=True)]
    dot_general x2, matrix products: 29.9 us -> 18.7 us  [per_device(): jnp.dot(moved, w2, precision=HIGHEST, preferred_element_type=jnp.float32)]
    dot_general x2 -> x1, local copies, waits for them, and re-layouts: 14.9 us -> 7.48 us  [per_device(): jnp.dot(t_cyc, v_all, precision=HIGHEST, preferred_element_type=jnp.float32)]
  transfers between devices with their start and end apart: 6 -> 5, of which waited for: 5 -> 5; matrix products, arithmetic and copies ran while one was open for 21% -> 17% of each run, Pallas kernels for 0% -> 0%
where the time goes in v3:
time: 492 us; the launch traced here: 485 us
  waiting for transfers between devices  280 us (57%)
  local copies, waits for them, and re-layouts  77.1 us (16%)
  matrix products  62.9 us (13%)
  blocking collectives  38 us (8%)
  between operations  14.2 us (3%)
  starting transfers between devices  7.99 us (2%)
  other arithmetic  5.07 us (1%)
    all_gather x2, waiting for transfers between devices, per_device(): v_all = lax.all_gather(v, 'int', axis=0, tiled=True)  129 us
    unnamed x4, waiting for transfers between devices  123 us
    all_to_all x1, blocking collectives, per_device(): lax.all_to_all(amplitudes.reshape(i_local, nocc, pw), 'int', split_axis=1...  38 us
    all_to_all x2, waiting for transfers between devices, per_device(): lax.all_to_all(l_cyc, 'amp', split_axis=0, concat_axis=0, tiled=True)  28.8 us
    dot_general x2, matrix products, per_device(): jnp.dot(t_cyc, v_all, precision=HIGHEST, preferred_element_type=jnp.float32)  22.6 us
    dot_general x2, matrix products, per_device(): jnp.dot(amplitudes, v_all, precision=HIGHEST, preferred_element_type=jnp....  21.6 us
    reshape x2, local copies, waits for them, and re-layouts, per_device(): l_cyc = l_cyc.reshape(n_amp, ibat * a_chunk, c_local * k_local)  19 us
    dot_general x2, matrix products, per_device(): jnp.dot(moved, w2, precision=HIGHEST, preferred_element_type=jnp.float32)  18.7 us
  transfers between devices with their start and end apart: 5, of which 5 were waited for; matrix products, arithmetic and copies ran while one was open for 17% of the time, Pallas kernels for 0%

profile of v3, /device:TPU:0, one launch (start us, length us, event | category | flops | bytes accessed | tf_op | source)
XLA Modules:
  0.0 485.5 jit_solution(4678103883053121813)
XLA Ops:
  7.2 3.5 copy.52
  14.0 38.0 %all_to_all.25 = f32[2,96,512]{2,0,1:T(2,128)S(1)} all-to-all(f32[2,96,512]{2,0,1:T(2,128)S(1)} %copy.53), channel_id=1, replica_groups=mesh['amp'=8,'int'=4] {'int'}, dimensions={1} | all-to-all | bytes 786432 | tf_op jit(solution)/shard_map/all_to_all | solution.py:26
  52.2 88.0 %all-gather.5.cloned.1.call-done = f32[512,3200]{0,1:T(8,128)} async-done(((f32[128,3200]{0,1:T(8,128)}), f32[512,3200]{0,1:T(8,128)}) %all-gather.5.cloned.1.call-update) | async-done | bytes 6553616 | tf_op jit(solution)/shard_map/all_gather | solution.py:36
  140.2 7.5 %reshape.127 = f32[4,8,100,512,1]{3,2,1,0,4:T(8,128)} reshape(f32[3200,512]{1,0:T(8,128)} %bitcast.55) | data formatting | bytes 13107200 | tf_op jit(solution)/shard_map/dot_general | solution.py:44
  147.7 11.6 %convolution_bitcast_fusion.2 = f32[8,8,4,100,24]{3,4,0,2,1:T(8,128)} fusion(f32[8,24,512,1,1]{2,1,4,3,0:T(8,128)S(1)} %bitcast.65, f32[4,8,100,512,1]{3,2,1,0,4:T(8,128)} %reshape.127), kind=kOutput, calls=%fused_computation.4 | convolution fusion | flops 3774873600 | bytes 9404416 | tf_op jit(solution)/shard_map/dot_general | solution.py:44
  159.3 9.3 %copy.56 = f32[8,8,4,100,24]{4,3,2,1,0:T(8,128)} copy(f32[8,8,4,100,24]{3,4,0,2,1:T(8,128)} %convolution_bitcast_fusion.2) | data formatting | bytes 4915200 | tf_op jit(solution)/shard_map/transpose | solution.py:45
  168.5 9.5 %reshape.117 = f32[8,32,2400]{2,1,0:T(8,128)} reshape(f32[8,8,4,100,24]{4,3,2,1,0:T(8,128)} %copy.56) | data formatting | bytes 4915200 | tf_op jit(solution)/shard_map/reshape | solution.py:46
  178.1 4.2 all-to-all-start.1
  182.3 10.7 %fusion.1 = f32[192,3200]{1,0:T(8,128)} fusion(f32[192,512]{1,0:T(8,128)S(1)} %copy-done.2, f32[512,3200]{0,1:T(8,128)} %all-gather.5.cloned.1.call-done), kind=kOutput, calls=%fused_computation.20 | convolution fusion | flops 3774873600 | bytes 9404416 | tf_op jit(solution)/shard_map/dot_general | solution.py:42
  193.0 19.7 %all-to-all-done.1 = f32[8,32,2400]{2,1,0:T(8,128)S(1)} async-done(((f32[8,32,2400]{2,1,0:T(8,128)}), f32[8,32,2400]{2,1,0:T(8,128)S(1)}, u32[]{:S(2)}, u32[]{:S(2)}) %all-to-all-start.1) | async-done | bytes 2457632 | tf_op jit(solution)/shard_map/all_to_all | solution.py:47
  212.6 7.7 %fusion.2 = f32[256,512]{1,0:T(8,128)} fusion(f32[256,2400]{1,0:T(8,128)S(1)} %bitcast.59, f32[2400,512]{1,0:T(8,128)} %bitcast.56), kind=kOutput, calls=%fused_computation.21 | convolution fusion | flops 3774873600 | bytes 7897088 | tf_op jit(solution)/shard_map/dot_general | solution.py:50
  220.4 40.5 %all-gather.3.cloned.1.call-done = f32[512,3200]{0,1:T(8,128)} async-done(((f32[128,3200]{0,1:T(8,128)}), f32[512,3200]{0,1:T(8,128)}) %all-gather.3.cloned.1.call-update) | async-done | bytes 6553616 | tf_op jit(solution)/shard_map/all_gather | solution.py:36
  260.9 11.0 %convolution_bitcast_fusion = f32[192,3200]{1,0:T(8,128)} fusion(f32[512,3200]{0,1:T(8,128)} %all-gather.3.cloned.1.call-done, f32[192,512]{1,0:T(8,128)S(1)} %bitcast.66), kind=kOutput, calls=%fused_computation | convolution fusion | flops 3774873600 | bytes 9404416 | tf_op jit(solution)/shard_map/dot_general | solution.py:44
  271.9 6.9 %reshape.121 = f32[8,24,4,8,100]{4,3,2,1,0:T(8,128)S(1)} reshape(f32[192,3200]{1,0:T(8,128)} %convolution_bitcast_fusion) | data formatting | bytes 4915200 | tf_op jit(solution)/shard_map/reshape | solution.py:45
  278.9 8.0 %copy.58 = f32[8,24,4,8,100]{1,4,2,0,3:T(8,128)} copy(f32[8,24,4,8,100]{4,3,2,1,0:T(8,128)S(1)} %reshape.121) | data formatting | bytes 4915200 | tf_op jit(solution)/shard_map/reshape | solution.py:45
  286.8 9.5 %reshape.122 = f32[8,32,2400]{2,1,0:T(8,128)} reshape(f32[8,8,4,100,24]{4,3,2,1,0:T(8,128)} %bitcast.54) | data formatting | bytes 4915200 | tf_op jit(solution)/shard_map/reshape | solution.py:46
  296.3 3.7 all-to-all-start.2
  300.0 6.0 %copy.60 = f32[512,2400]{1,0:T(8,128)} copy(f32[512,2400]{0,1:T(8,128)} %bitcast.57) | data formatting | bytes 9830400 | tf_op jit(solution)/shard_map/dot_general | solution.py:50
  310.7 10.9 %convolution_bitcast_fusion.1 = f32[192,3200]{1,0:T(8,128)} fusion(f32[512,3200]{0,1:T(8,128)} %all-gather.3.cloned.1.call-done, f32[192,512]{1,0:T(8,128)} %param.5), kind=kOutput, calls=%fused_computation.1 | convolution fusion | flops 3774873600 | bytes 9404416 | tf_op jit(solution)/shard_map/dot_general | solution.py:42
  321.6 9.2 %all-to-all-done.2 = f32[8,32,2400]{2,1,0:T(8,128)S(1)} async-done(((f32[8,32,2400]{2,1,0:T(8,128)}), f32[8,32,2400]{2,1,0:T(8,128)S(1)}, u32[]{:S(2)}, u32[]{:S(2)}) %all-to-all-start.2) | async-done | bytes 2457632 | tf_op jit(solution)/shard_map/all_to_all | solution.py:47
  332.3 10.9 %convolution_bitcast_fusion.3 = f32[1,8,4,2,4,8,64]{6,1,5,4,3,2,0:T(8,128)S(1)} fusion(f32[8,4,2,4,2400,1]{4,0,5,3,2,1:T(8,128)S(1)} %bitcast.64, f32[8,64,2400,1,1,1]{2,1,0,5,4,3:T(8,128)} %bitcast.62), kind=kOutput, calls=%fused_computation.5 | convolution fusion | flops 3774873600 | bytes 7897088 | tf_op jit(solution)/shard_map/dot_general | solution.py:50
  346.2 3.5 reshape.124
  349.7 4.3 pad_maximum_fusion
  354.0 122.1 %all-reduce.3.cloned.1.call-done = f32[32,8192]{1,0:T(8,128)} async-done(((f32[32,8192]{1,0:T(8,128)}), f32[32,8192]{1,0:T(8,128)}) %all-reduce.3.cloned.1.call-update) | async-done | bytes 1048592
  (38 shorter events, 15.2 us)
Async XLA Ops:
  7.2 133.0 %all-gather.5.cloned.1.call-start = ((), (), s32[]{:S(2)}) async-start(), calls=%async_computation.4 | async-start | bytes 8192000 | tf_op jit(solution)/shard_map/all_gather | solution.py:36
  12.7 1.0 copy-start.2
  12.7 248.2 %all-gather.3.cloned.1.call-start = ((), (), s32[]{:S(2)}) async-start(), calls=%async_computation.3 | async-start | bytes 8192000 | tf_op jit(solution)/shard_map/all_gather | solution.py:36
  178.1 34.6 %all-to-all-start.1 = ((f32[8,32,2400]{2,1,0:T(8,128)}), f32[8,32,2400]{2,1,0:T(8,128)S(1)}, u32[]{:S(2)}, u32[]{:S(2)}) async-start(f32[8,32,2400]{2,1,0:T(8,128)} %reshape.117), calls=%async_computation.1 | async-start | bytes 4980736 | tf_op jit(solution)/shard_map/all_to_all | solution.py:47
  296.3 34.5 %all-to-all-start.2 = ((f32[8,32,2400]{2,1,0:T(8,128)}), f32[8,32,2400]{2,1,0:T(8,128)S(1)}, u32[]{:S(2)}, u32[]{:S(2)}) async-start(f32[8,32,2400]{2,1,0:T(8,128)} %reshape.122), calls=%async_computation.2 | async-start | bytes 4980736 | tf_op jit(solution)/shard_map/all_to_all | solution.py:47
  299.9 176.2 %all-reduce.3.cloned.1.call-start = ((), (), s32[]{:S(2)}) async-start(), calls=%async_computation.5 | async-start | bytes 2097152
  300.0 6.7 %copy-start.3 = (s32[96]{0:T(128)S(1)}, s32[96]{0:T(128)}, u32[]{:S(2)}) copy-start(s32[96]{0:T(128)} %param.8) | copy-start | bytes 1156
  300.0 6.9 %copy-start.4 = (u32[32]{0:T(128)S(1)}, u32[32]{0:T(128)}, u32[]{:S(2)}) copy-start(u32[32]{0:T(128)} %constant.47) | copy-start | bytes 388
  332.2 11.0 %copy-start.1 = (f32[1,8,4,2,4,8,64]{6,1,5,4,3,2,0:T(8,128)S(1)}, f32[1,8,4,2,4,8,64]{6,1,5,4,3,2,0:T(8,128)}, u32[]{:S(2)}) copy-start(f32[1,8,4,2,4,8,64]{6,1,5,4,3,2,0:T(8,128)} %copy.61) | copy-start | bytes 1572868
  343.5 6.2 %copy-start = (f32[192,3200]{1,0:T(8,128)S(1)}, f32[192,3200]{1,0:T(8,128)}, u32[]{:S(2)}) copy-start(f32[192,3200]{1,0:T(8,128)} %fusion.1) | copy-start | bytes 7372804
Sparse Core Ops, SparseCore 0:
  12.9 127.2 all-gather.4
  141.7 119.1 all-gather.2
  349.8 126.2 all-reduce.2

commit v4 on v3

--- a/solution.py
+++ b/solution.py
@@ -4,7 +4,7 @@
 from jax.sharding import PartitionSpec as P
 
 HIGHEST = lax.Precision.HIGHEST
-CHUNKS = 2
+CHUNKS = 3
 
 
 def per_device(amplitudes, slab_integrals, cycle_integrals, occ_irrep, vir_irrep, n_amp, n_int):
@@ -18,10 +18,9 @@
     a_local = width // nvir
     slab = a_local * n_amp
     k_local, c_local, columns = cycle_integrals.shape
-    chunks = CHUNKS
-    while a_local % chunks:
-        chunks -= 1
-    a_chunk = a_local // chunks
+    chunks = min(CHUNKS, a_local)
+    sizes = [a_local // chunks + (1 if t < a_local % chunks else 0) for t in range(chunks)]
+    starts = [sum(sizes[:t]) for t in range(chunks)]
 
     t_cyc = lax.all_to_all(
         amplitudes.reshape(i_local, nocc, pw), "int", split_axis=1, concat_axis=0, tiled=True
@@ -32,7 +31,8 @@
     ladder_chunks = []
     cycle_chunks = []
     for t in range(chunks):
-        v = slab3[:, t * a_chunk:(t + 1) * a_chunk, :].reshape(pw_local, a_chunk * nvir)
+        a_chunk = sizes[t]
+        v = slab3[:, starts[t]:starts[t] + a_chunk, :].reshape(pw_local, a_chunk * nvir)
         v_all = lax.all_gather(v, "int", axis=0, tiled=True)
         if t:
             v_all, ladder_chunks[-1], cycle_chunks[-1] = lax.optimization_barrier(
@@ -51,13 +51,13 @@
         )
     ladder = jnp.concatenate(ladder_chunks, axis=1)
 
-    col_local = columns // n_amp
-    parts = jnp.stack(cycle_chunks, 0).reshape(
-        chunks, n_amp, n_int, i_local, a_chunk, n_amp, col_local
+    parts = jnp.concatenate(
+        [c.reshape(n_amp, ibat, sizes[t], columns) for t, c in enumerate(cycle_chunks)], axis=2
     )
-    parts = parts.transpose(2, 5, 3, 1, 0, 4, 6).reshape(n_int * n_amp, i_local * slab * col_local)
-    sums = lax.psum_scatter(parts, ("int", "amp"), scatter_dimension=0, tiled=True)
-    sums = sums.reshape(i_local * slab, col_local)
+    parts = parts.transpose(1, 0, 2, 3).reshape(ibat * slab, columns)
+    narrowed = lax.psum_scatter(parts, "amp", scatter_dimension=1, tiled=True)
+    sums = lax.psum_scatter(narrowed, "int", scatter_dimension=0, tiled=True)
+    col_local = sums.shape[1]
 
     row_start = lax.axis_index("int") * i_local
     batch_labels = lax.dynamic_slice_in_dim(occ_irrep, row_start, i_local, 0)

time: 492 us -> 392 us (0.80)
  waiting for transfers between devices: 280 us -> 219 us
  blocking collectives: 38 us -> 0 us
  starting transfers between devices: 7.99 us -> 18.5 us
  local copies, waits for them, and re-layouts: 77.1 us -> 69.8 us
    unnamed x4 -> x6, waiting for transfers between devices: 123 us -> 32 us
    all_to_all x1 -> x0, blocking collectives: 38 us -> none  [per_device(): lax.all_to_all(amplitudes.reshape(i_local, nocc, pw), 'int', split_axis=1...]
    all_to_all x0 -> x1, waiting for transfers between devices: none -> 27.4 us  [per_device(): lax.all_to_all(amplitudes.reshape(i_local, nocc, pw), 'int', split_axis=1...]
    all_gather x2 -> x3, waiting for transfers between devices: 129 us -> 104 us  [per_device(): v_all = lax.all_gather(v, 'int', axis=0, tiled=True)]
    all_to_all x2 -> x3, waiting for transfers between devices: 28.8 us -> 47.8 us  [per_device(): lax.all_to_all(l_cyc, 'amp', split_axis=0, concat_axis=0, tiled=True)]
    reduce_scatter x0 -> x1, waiting for transfers between devices: none -> 7.85 us  [per_device(): sums = lax.psum_scatter(narrowed, 'int', scatter_dimension=0, tiled=True)]
    concatenate x0 -> x1, local copies, waits for them, and re-layouts: none -> 6.58 us  [per_device(): ladder = jnp.concatenate(ladder_chunks, axis=1)]
    all_to_all x0 -> x1, starting transfers between devices: none -> 6.32 us  [per_device(): lax.all_to_all(amplitudes.reshape(i_local, nocc, pw), 'int', split_axis=1...]
  transfers between devices with their start and end apart: 5 -> 9, of which waited for: 5 -> 9; matrix products, arithmetic and copies ran while one was open for 17% -> 26% of each run, Pallas kernels for 0% -> 0%
where the time goes in v4:
time: 392 us; the launch traced here: 386 us
  waiting for transfers between devices  219 us (56%)
  local copies, waits for them, and re-layouts  69.8 us (18%)
  matrix products  62.8 us (16%)
  starting transfers between devices  18.5 us (5%)
  between operations  14.4 us (4%)
    all_gather x3, waiting for transfers between devices, per_device(): v_all = lax.all_gather(v, 'int', axis=0, tiled=True)  104 us
    all_to_all x3, waiting for transfers between devices, per_device(): lax.all_to_all(l_cyc, 'amp', split_axis=0, concat_axis=0, tiled=True)  47.8 us
    unnamed x6, waiting for transfers between devices  32 us
    all_to_all x1, waiting for transfers between devices, per_device(): lax.all_to_all(amplitudes.reshape(i_local, nocc, pw), 'int', split_axis=1...  27.4 us
    dot_general x3, matrix products, per_device(): jnp.dot(amplitudes, v_all, precision=HIGHEST, preferred_element_type=jnp....  22.9 us
    dot_general x3, matrix products, per_device(): jnp.dot(t_cyc, v_all, precision=HIGHEST, preferred_element_type=jnp.float32)  21.7 us
    reshape x3, local copies, waits for them, and re-layouts, per_device(): l_cyc = l_cyc.reshape(n_amp, ibat * a_chunk, c_local * k_local)  20.7 us
    dot_general x3, matrix products, per_device(): jnp.dot(moved, w2, precision=HIGHEST, preferred_element_type=jnp.float32)  18.2 us
  transfers between devices with their start and end apart: 9, of which 9 were waited for; matrix products, arithmetic and copies ran while one was open for 26% of the time, Pallas kernels for 0%

profile of v4, /device:TPU:0, one launch (start us, length us, event | category | flops | bytes accessed | tf_op | source)
XLA Modules:
  0.0 386.2 jit_solution(11603752438899405828)
XLA Ops:
  15.2 6.3 %all-to-all-start = ((f32[2,96,512]{2,0,1:T(2,128)}), f32[2,96,512]{2,0,1:T(2,128)}, u32[]{:S(2)}, u32[]{:S(2)}) async-start(f32[2,96,512]{2,0,1:T(2,128)} %copy.54), calls=%async_computation | async-start | bytes 786432 | tf_op jit(solution)/shard_map/all_to_all | solution.py:25
  22.5 27.4 %all-to-all-done = f32[2,96,512]{2,0,1:T(2,128)} async-done(((f32[2,96,512]{2,0,1:T(2,128)}), f32[2,96,512]{2,0,1:T(2,128)}, u32[]{:S(2)}, u32[]{:S(2)}) %all-to-all-start) | async-done | bytes 393248 | tf_op jit(solution)/shard_map/all_to_all | solution.py:25
  51.0 64.2 %all-gather.6.cloned.1.call-done = f32[512,2400]{0,1:T(8,128)} async-done(((f32[128,2400]{0,1:T(8,128)}), f32[512,2400]{0,1:T(8,128)}) %all-gather.6.cloned.1.call-update) | async-done | bytes 4915216 | tf_op jit(solution)/shard_map/all_gather | solution.py:36
  120.5 7.7 %convolution_bitcast_fusion.4 = f32[8,8,3,100,24]{3,4,0,2,1:T(8,128)S(1)} fusion(f32[8,24,512,1,1]{2,1,4,3,0:T(8,128)S(1)} %bitcast.75, f32[3,8,100,512,1]{3,2,1,0,4:T(8,128)} %reshape.136), kind=kOutput, calls=%fused_computation.4 | convolution fusion | flops 2831155200 | bytes 7151616 | tf_op jit(solution)/shard_map/dot_general | solution.py:44
  128.2 5.6 %copy.57 = f32[8,8,3,100,24]{4,3,2,1,0:T(8,128)} copy(f32[8,8,3,100,24]{3,4,0,2,1:T(8,128)S(1)} %convolution_bitcast_fusion.4) | data formatting | bytes 3686400 | tf_op jit(solution)/shard_map/transpose | solution.py:45
  133.8 7.5 %reshape.122 = f32[8,24,2400]{2,1,0:T(8,128)} reshape(f32[8,8,3,100,24]{4,3,2,1,0:T(8,128)} %copy.57) | data formatting | bytes 3686400 | tf_op jit(solution)/shard_map/reshape | solution.py:46
  145.4 8.6 %fusion.1 = f32[192,2400]{1,0:T(8,128)} fusion(f32[192,512]{1,0:T(8,128)S(1)} %copy-done.1, f32[512,2400]{0,1:T(8,128)} %all-gather.6.cloned.1.call-done), kind=kOutput, calls=%fused_computation.19 | convolution fusion | flops 2831155200 | bytes 7151616 | tf_op jit(solution)/shard_map/dot_general | solution.py:42
  154.0 15.5 %all-to-all-done.1 = f32[8,24,2400]{2,1,0:T(8,128)S(1)} async-done(((f32[8,24,2400]{2,1,0:T(8,128)}), f32[8,24,2400]{2,1,0:T(8,128)S(1)}, u32[]{:S(2)}, u32[]{:S(2)}) %all-to-all-start.1) | async-done | bytes 1843232 | tf_op jit(solution)/shard_map/all_to_all | solution.py:47
  169.6 6.4 %fusion.2 = f32[192,512]{1,0:T(8,128)} fusion(f32[192,2400]{1,0:T(8,128)S(1)} %bitcast.68, f32[2400,512]{1,0:T(8,128)} %bitcast.62), kind=kOutput, calls=%fused_computation.20 | convolution fusion | flops 2831155200 | bytes 7151616 | tf_op jit(solution)/shard_map/dot_general | solution.py:50
  176.0 33.3 %all-gather.4.cloned.1.call-done = f32[512,2400]{0,1:T(8,128)} async-done(((f32[128,2400]{0,1:T(8,128)}), f32[512,2400]{0,1:T(8,128)}) %all-gather.4.cloned.1.call-update) | async-done | bytes 4915216 | tf_op jit(solution)/shard_map/all_gather | solution.py:36
  209.2 8.7 %convolution_bitcast_fusion = f32[192,2400]{1,0:T(8,128)} fusion(f32[512,2400]{0,1:T(8,128)} %all-gather.4.cloned.1.call-done, f32[192,512]{1,0:T(8,128)S(1)} %bitcast.76), kind=kOutput, calls=%fused_computation | convolution fusion | flops 2831155200 | bytes 7151616 | tf_op jit(solution)/shard_map/dot_general | solution.py:44
  220.5 5.5 %copy.59 = f32[8,24,3,8,100]{1,4,2,0,3:T(8,128)} copy(f32[8,24,3,8,100]{4,3,2,1,0:T(8,128)S(1)} %reshape.127) | data formatting | bytes 3686400 | tf_op jit(solution)/shard_map/reshape | solution.py:45
  226.0 7.6 %reshape.128 = f32[8,24,2400]{2,1,0:T(8,128)} reshape(f32[8,8,3,100,24]{4,3,2,1,0:T(8,128)} %bitcast.60) | data formatting | bytes 3686400 | tf_op jit(solution)/shard_map/reshape | solution.py:46
  237.5 8.8 %convolution_bitcast_fusion.1 = f32[192,2400]{1,0:T(8,128)} fusion(f32[512,2400]{0,1:T(8,128)} %all-gather.4.cloned.1.call-done, f32[192,512]{1,0:T(8,128)S(1)} %copy-done.1), kind=kOutput, calls=%fused_computation.1 | convolution fusion | flops 2831155200 | bytes 7151616 | tf_op jit(solution)/shard_map/dot_general | solution.py:42
  246.3 15.4 %all-to-all-done.2 = f32[8,24,2400]{2,1,0:T(8,128)S(1)} async-done(((f32[8,24,2400]{2,1,0:T(8,128)}), f32[8,24,2400]{2,1,0:T(8,128)S(1)}, u32[]{:S(2)}, u32[]{:S(2)}) %all-to-all-start.2) | async-done | bytes 1843232 | tf_op jit(solution)/shard_map/all_to_all | solution.py:47
  261.6 6.4 %fusion.3 = f32[192,512]{1,0:T(8,128)} fusion(f32[192,2400]{1,0:T(8,128)S(1)} %bitcast.69, f32[2400,512]{1,0:T(8,128)} %bitcast.63), kind=kOutput, calls=%fused_computation.21 | convolution fusion | flops 2831155200 | bytes 7151616 | tf_op jit(solution)/shard_map/dot_general | solution.py:50
  268.1 6.5 %all-gather.8.cloned.1.call-done = f32[512,1600]{0,1:T(8,128)} async-done(((f32[128,1600]{0,1:T(8,128)}), f32[512,1600]{0,1:T(8,128)}) %all-gather.8.cloned.1.call-update) | async-done | bytes 3276816 | tf_op jit(solution)/shard_map/all_gather | solution.py:36
  274.6 5.4 %convolution_bitcast_fusion.2 = f32[192,1600]{1,0:T(8,128)S(1)} fusion(f32[512,1600]{0,1:T(8,128)} %all-gather.8.cloned.1.call-done, f32[192,512]{1,0:T(8,128)S(1)} %bitcast.77), kind=kOutput, calls=%fused_computation.2 | convolution fusion | flops 1887436800 | bytes 4898816 | tf_op jit(solution)/shard_map/dot_general | solution.py:44
  286.1 5.6 %reshape.133 = f32[8,16,2400]{2,1,0:T(8,128)} reshape(f32[8,8,2,100,24]{4,3,2,1,0:T(8,128)} %bitcast.61) | data formatting | bytes 2457600 | tf_op jit(solution)/shard_map/reshape | solution.py:46
  296.1 16.9 %all-to-all-done.3 = f32[8,16,2400]{2,1,0:T(8,128)S(1)} async-done(((f32[8,16,2400]{2,1,0:T(8,128)}), f32[8,16,2400]{2,1,0:T(8,128)S(1)}, u32[]{:S(2)}, u32[]{:S(2)}) %all-to-all-start.3) | async-done | bytes 1228832 | tf_op jit(solution)/shard_map/all_to_all | solution.py:47
  324.6 31.3 %reduce-scatter.7.cloned.1.call-done = f32[64,512]{1,0:T(8,128)} async-done(((f32[512,512]{1,0:T(8,128)}), f32[64,512]{1,0:T(8,128)}) %reduce-scatter.7.cloned.1.call-update) | async-done | bytes 131088
  357.7 5.5 %convolution_bitcast_fusion.3 = f32[192,1600]{1,0:T(8,128)} fusion(f32[512,1600]{0,1:T(8,128)S(1)} %copy-done, f32[192,512]{1,0:T(8,128)} %param.5), kind=kOutput, calls=%fused_computation.3 | convolution fusion | flops 1887436800 | bytes 4898816 | tf_op jit(solution)/shard_map/dot_general | solution.py:42
  363.2 6.6 %concatenate.6 = f32[192,6400]{1,0:T(8,128)} concatenate(f32[192,2400]{1,0:T(8,128)} %fusion.1, f32[192,2400]{1,0:T(8,128)} %convolution_bitcast_fusion.1, f32[192,1600]{1,0:T(8,128)} %convolution_bitcast_fusion.3), dimensions={1} | concatenate | bytes 9830400 | tf_op jit(solution)/shard_map/concatenate | solution.py:52
  369.8 7.9 %reduce-scatter.5.cloned.1.call-done = f32[128,64]{1,0:T(8,128)} async-done(((f32[512,64]{1,0:T(8,128)}), f32[128,64]{1,0:T(8,128)}) %reduce-scatter.5.cloned.1.call-update) | async-done | bytes 32784 | tf_op jit(solution)/shard_map/reduce_scatter | solution.py:59
  (52 shorter events, 51.4 us)
Async XLA Ops:
  7.2 108.1 %all-gather.6.cloned.1.call-start = ((), (), s32[]{:S(2)}) async-start(), calls=%async_computation.7 | async-start | bytes 6144000 | tf_op jit(solution)/shard_map/all_gather | solution.py:36
  12.4 196.8 %all-gather.4.cloned.1.call-start = ((), (), s32[]{:S(2)}) async-start(), calls=%async_computation.6 | async-start | bytes 6144000 | tf_op jit(solution)/shard_map/all_gather | solution.py:36
  15.2 34.7 %all-to-all-start = ((f32[2,96,512]{2,0,1:T(2,128)}), f32[2,96,512]{2,0,1:T(2,128)}, u32[]{:S(2)}, u32[]{:S(2)}) async-start(f32[2,96,512]{2,0,1:T(2,128)} %copy.54), calls=%async_computation | async-start | bytes 786432 | tf_op jit(solution)/shard_map/all_to_all | solution.py:25
  21.5 253.1 %all-gather.8.cloned.1.call-start = ((), (), s32[]{:S(2)}) async-start(), calls=%async_computation.8 | async-start | bytes 4096000 | tf_op jit(solution)/shard_map/all_gather | solution.py:36
  141.3 4.1 %copy-start.1 = (f32[192,512]{1,0:T(8,128)S(1)}, f32[192,512]{1,0:T(8,128)}, u32[]{:S(2)}) copy-start(f32[192,512]{1,0:T(8,128)} %param.5) | copy-start | bytes 1179652
  141.3 28.2 %all-to-all-start.1 = ((f32[8,24,2400]{2,1,0:T(8,128)}), f32[8,24,2400]{2,1,0:T(8,128)S(1)}, u32[]{:S(2)}, u32[]{:S(2)}) async-start(f32[8,24,2400]{2,1,0:T(8,128)} %reshape.122), calls=%async_computation.1 | async-start | bytes 3735552 | tf_op jit(solution)/shard_map/all_to_all | solution.py:47
  233.6 28.1 %all-to-all-start.2 = ((f32[8,24,2400]{2,1,0:T(8,128)}), f32[8,24,2400]{2,1,0:T(8,128)S(1)}, u32[]{:S(2)}, u32[]{:S(2)}) async-start(f32[8,24,2400]{2,1,0:T(8,128)} %reshape.128), calls=%async_computation.2 | async-start | bytes 3735552 | tf_op jit(solution)/shard_map/all_to_all | solution.py:47
  286.1 9.7 %copy-start.2 = (f32[192,512]{1,0:T(8,128)S(1)}, f32[192,512]{1,0:T(8,128)}, u32[]{:S(2)}) copy-start(f32[192,512]{1,0:T(8,128)} %fusion.2) | copy-start | bytes 1179652
  291.7 4.3 %copy-start.3 = (f32[192,512]{1,0:T(8,128)S(1)}, f32[192,512]{1,0:T(8,128)}, u32[]{:S(2)}) copy-start(f32[192,512]{1,0:T(8,128)} %fusion.3) | copy-start | bytes 1179652
  291.7 21.3 %all-to-all-start.3 = ((f32[8,16,2400]{2,1,0:T(8,128)}), f32[8,16,2400]{2,1,0:T(8,128)S(1)}, u32[]{:S(2)}, u32[]{:S(2)}) async-start(f32[8,16,2400]{2,1,0:T(8,128)} %reshape.133), calls=%async_computation.3 | async-start | bytes 2490368 | tf_op jit(solution)/shard_map/all_to_all | solution.py:47
  295.4 60.4 %reduce-scatter.7.cloned.1.call-start = ((), (), s32[]{:S(2)}) async-start(), calls=%async_computation.10 | async-start | bytes 1179648
  318.9 5.0 %copy-start.4 = (s32[96]{0:T(128)S(1)}, s32[96]{0:T(128)}, u32[]{:S(2)}) copy-start(s32[96]{0:T(128)} %param.8) | copy-start | bytes 1156
  319.3 38.4 %copy-start = (f32[512,1600]{0,1:T(8,128)S(1)}, f32[512,1600]{0,1:T(8,128)}, u32[]{:S(2)}) copy-start(f32[512,1600]{0,1:T(8,128)} %all-gather.8.cloned.1.call-done) | copy-start | bytes 9830404
  323.2 54.4 %reduce-scatter.5.cloned.1.call-start = ((), (), s32[]{:S(2)}) async-start(), calls=%async_computation.9 | async-start | bytes 327680 | tf_op jit(solution)/shard_map/reduce_scatter | solution.py:59
Sparse Core Ops, SparseCore 0:
  12.5 102.6 all-gather.5
  116.8 92.3 all-gather.3
  210.8 63.7 all-gather.7
  323.4 32.4 reduce-scatter.6
  358.0 19.6 reduce-scatter.4

commit v5 on v4

--- a/solution.py
+++ b/solution.py
@@ -4,7 +4,6 @@
 from jax.sharding import PartitionSpec as P
 
 HIGHEST = lax.Precision.HIGHEST
-CHUNKS = 3
 
 
 def per_device(amplitudes, slab_integrals, cycle_integrals, occ_irrep, vir_irrep, n_amp, n_int):
@@ -18,8 +17,13 @@
     a_local = width // nvir
     slab = a_local * n_amp
     k_local, c_local, columns = cycle_integrals.shape
-    chunks = min(CHUNKS, a_local)
-    sizes = [a_local // chunks + (1 if t < a_local % chunks else 0) for t in range(chunks)]
+    if a_local >= 4:
+        sizes = [a_local // 2, a_local - a_local // 2 - 1, 1]
+    elif a_local >= 2:
+        sizes = [a_local - 1, 1]
+    else:
+        sizes = [a_local]
+    chunks = len(sizes)
     starts = [sum(sizes[:t]) for t in range(chunks)]
 
     t_cyc = lax.all_to_all(
@@ -38,26 +42,31 @@
             v_all, ladder_chunks[-1], cycle_chunks[-1] = lax.optimization_barrier(
                 (v_all, ladder_chunks[-1], cycle_chunks[-1])
             )
-        ladder_chunks.append(
-            jnp.dot(amplitudes, v_all, precision=HIGHEST, preferred_element_type=jnp.float32)
-        )
+        ladder_chunks.append(None)
+        if t < chunks - 1:
+            ladder_chunks[-1] = jnp.dot(
+                amplitudes, v_all, precision=HIGHEST, preferred_element_type=jnp.float32
+            )
         l_cyc = jnp.dot(t_cyc, v_all, precision=HIGHEST, preferred_element_type=jnp.float32)
         l_cyc = l_cyc.reshape(ibat, k_local, a_chunk, n_amp, c_local).transpose(3, 0, 2, 4, 1)
         l_cyc = l_cyc.reshape(n_amp, ibat * a_chunk, c_local * k_local)
         moved = lax.all_to_all(l_cyc, "amp", split_axis=0, concat_axis=0, tiled=True)
+        if t == chunks - 1:
+            ladder_chunks[-1] = jnp.dot(
+                amplitudes, v_all, precision=HIGHEST, preferred_element_type=jnp.float32
+            )
+            ladder = jnp.concatenate(ladder_chunks, axis=1)
+            moved, ladder = lax.optimization_barrier((moved, ladder))
         moved = moved.reshape(n_amp * ibat * a_chunk, c_local * k_local)
-        cycle_chunks.append(
-            jnp.dot(moved, w2, precision=HIGHEST, preferred_element_type=jnp.float32)
-        )
-    ladder = jnp.concatenate(ladder_chunks, axis=1)
+        partial_sums = jnp.dot(moved, w2, precision=HIGHEST, preferred_element_type=jnp.float32)
+        cycle_chunks.append(lax.psum_scatter(partial_sums, "amp", scatter_dimension=1, tiled=True))
 
+    col_local = columns // n_amp
     parts = jnp.concatenate(
-        [c.reshape(n_amp, ibat, sizes[t], columns) for t, c in enumerate(cycle_chunks)], axis=2
+        [c.reshape(n_amp, ibat, sizes[t], col_local) for t, c in enumerate(cycle_chunks)], axis=2
     )
-    parts = parts.transpose(1, 0, 2, 3).reshape(ibat * slab, columns)
-    narrowed = lax.psum_scatter(parts, "amp", scatter_dimension=1, tiled=True)
-    sums = lax.psum_scatter(narrowed, "int", scatter_dimension=0, tiled=True)
-    col_local = sums.shape[1]
+    parts = parts.transpose(1, 0, 2, 3).reshape(ibat * slab, col_local)
+    sums = lax.psum_scatter(parts, "int", scatter_dimension=0, tiled=True)
 
     row_start = lax.axis_index("int") * i_local
     batch_labels = lax.dynamic_slice_in_dim(occ_irrep, row_start, i_local, 0)

time: 392 us -> 470 us (1.20)
  blocking collectives: 0 us -> 100 us
  waiting for transfers between devices: 219 us -> 199 us
  matrix products: 62.8 us -> 80.5 us
  starting transfers between devices: 18.5 us -> 4.8 us
  local copies, waits for them, and re-layouts: 69.8 us -> 63.4 us
    all_to_all x0 -> x3, blocking collectives: none -> 100 us  [the longest x2 61.7 us: per_device(): lax.all_to_all(l_cyc, 'amp', split_axis=0, concat_axis=0, tiled=True)]
    reduce_scatter x1 -> x3, waiting for transfers between devices: 7.85 us -> 77.6 us  [the longest x2 57.8 us: per_device(): lax.psum_scatter(partial_sums, 'amp', scatter_dimension=1, tiled=True)]
    all_to_all x3 -> x1, waiting for transfers between devices: 47.8 us -> 1.65 us  [per_device(): lax.all_to_all(l_cyc, 'amp', split_axis=0, concat_axis=0, tiled=True)]
    all_to_all x1 -> x0, waiting for transfers between devices: 27.4 us -> none  [per_device(): lax.all_to_all(amplitudes.reshape(i_local, nocc, pw), 'int', split_axis=1...]
    all_gather x3, waiting for transfers between devices: 104 us -> 86.6 us  [per_device(): v_all = lax.all_gather(v, 'int', axis=0, tiled=True)]
    unnamed x0 -> x1, matrix products: none -> 11.2 us
    all_to_all x3 -> x1, starting transfers between devices: 11.7 us -> 4.33 us  [per_device(): lax.all_to_all(l_cyc, 'amp', split_axis=0, concat_axis=0, tiled=True)]
    all_to_all x1 -> x0, starting transfers between devices: 6.32 us -> none  [per_device(): lax.all_to_all(amplitudes.reshape(i_local, nocc, pw), 'int', split_axis=1...]
  transfers between devices with their start and end apart: 9 -> 8, of which waited for: 9 -> 6; matrix products, arithmetic and copies ran while one was open for 26% -> 25% of each run, Pallas kernels for 0% -> 0%
where the time goes in v5:
time: 470 us; the launch traced here: 464 us
  waiting for transfers between devices  199 us (42%)
  blocking collectives  100 us (21%)
  matrix products  80.5 us (17%)
  local copies, waits for them, and re-layouts  63.4 us (13%)
  between operations  14.5 us (3%)
  starting transfers between devices  4.8 us (1%)
    all_gather x3, waiting for transfers between devices, per_device(): v_all = lax.all_gather(v, 'int', axis=0, tiled=True)  86.6 us
    all_to_all x2, blocking collectives, per_device(): lax.all_to_all(l_cyc, 'amp', split_axis=0, concat_axis=0, tiled=True)  61.7 us
    reduce_scatter x2, waiting for transfers between devices, per_device(): lax.psum_scatter(partial_sums, 'amp', scatter_dimension=1, tiled=True)  57.8 us
    all_to_all x1, blocking collectives, per_device(): lax.all_to_all(amplitudes.reshape(i_local, nocc, pw), 'int', split_axis=1...  38.6 us
    unnamed x8, waiting for transfers between devices  33.2 us
    dot_general x3, matrix products, per_device(): jnp.dot(t_cyc, v_all, precision=HIGHEST, preferred_element_type=jnp.float32)  23.7 us
    dot_general x3, matrix products, per_device(): jnp.dot(amplitudes, v_all, precision=HIGHEST, preferred_element_type=jnp....  23.2 us
    dot_general x2, matrix products, per_device(): jnp.dot(moved, w2, precision=HIGHEST, preferred_element_type=jnp.float32)  22.4 us
  transfers between devices with their start and end apart: 8, of which 6 were waited for; matrix products, arithmetic and copies ran while one was open for 25% of the time, Pallas kernels for 0%

profile of v5, /device:TPU:0, one launch (start us, length us, event | category | flops | bytes accessed | tf_op | source)
XLA Modules:
  0.0 464.0 jit_solution(5637210452625345350)
XLA Ops:
  7.2 3.5 copy.54
  14.6 38.6 %all_to_all.30 = f32[2,96,512]{2,0,1:T(2,128)S(1)} all-to-all(f32[2,96,512]{2,0,1:T(2,128)S(1)} %copy.55), channel_id=1, replica_groups=mesh['amp'=8,'int'=4] {'int'}, dimensions={1} | all-to-all | bytes 786432 | tf_op jit(solution)/shard_map/all_to_all | solution.py:29
  54.1 86.6 %all-gather.7.cloned.1.call-done = f32[512,3200]{0,1:T(8,128)} async-done(((f32[128,3200]{0,1:T(8,128)}), f32[512,3200]{0,1:T(8,128)}) %all-gather.7.cloned.1.call-update) | async-done | bytes 6553616 | tf_op jit(solution)/shard_map/all_gather | solution.py:40
  140.8 7.5 %reshape.141 = f32[4,8,100,512,1]{3,2,1,0,4:T(8,128)} reshape(f32[3200,512]{1,0:T(8,128)} %bitcast.66) | data formatting | bytes 13107200 | tf_op jit(solution)/shard_map/dot_general | solution.py:50
  148.3 11.7 %convolution_bitcast_fusion.2 = f32[8,8,4,100,24]{3,4,0,2,1:T(8,128)} fusion(f32[8,24,512,1,1]{2,1,4,3,0:T(8,128)} %bitcast.78, f32[4,8,100,512,1]{3,2,1,0,4:T(8,128)} %reshape.141), kind=kOutput, calls=%fused_computation.2 | convolution fusion | flops 3774873600 | bytes 9404416 | tf_op jit(solution)/shard_map/dot_general | solution.py:50
  159.9 9.3 %copy.58 = f32[8,8,4,100,24]{4,3,2,1,0:T(8,128)} copy(f32[8,8,4,100,24]{3,4,0,2,1:T(8,128)} %convolution_bitcast_fusion.2) | data formatting | bytes 4915200 | tf_op jit(solution)/shard_map/transpose | solution.py:51
  169.2 9.5 %reshape.125 = f32[8,32,2400]{2,1,0:T(8,128)} reshape(f32[8,8,4,100,24]{4,3,2,1,0:T(8,128)} %copy.58) | data formatting | bytes 4915200 | tf_op jit(solution)/shard_map/reshape | solution.py:52
  178.7 35.0 %all_to_all.31 = f32[8,32,2400]{2,1,0:T(8,128)S(1)} all-to-all(f32[8,32,2400]{2,1,0:T(8,128)} %reshape.125), channel_id=1, replica_groups=mesh['amp'=8,'int'=4] {'amp'}, dimensions={0} | all-to-all | bytes 4915200 | tf_op jit(solution)/shard_map/all_to_all | solution.py:53
  213.7 11.2 %fusion.2 = f32[256,512]{0,1:T(8,128)} fusion(f32[256,2400]{1,0:T(8,128)S(1)} %bitcast.71, f32[2400,512]{1,0:T(8,128)} %bitcast.62), kind=kOutput, calls=%fused_computation.21 | convolution fusion | flops 3774873600 | bytes 7897088 | tf_op jit(solution)/shard_map/dot_general | solution.py:61
  226.1 10.9 %fusion.1 = f32[192,3200]{1,0:T(8,128)} fusion(f32[192,512]{1,0:T(8,128)} %param.5, f32[512,3200]{0,1:T(8,128)} %all-gather.7.cloned.1.call-done), kind=kOutput, calls=%fused_computation.20 | convolution fusion | flops 3774873600 | bytes 9404416 | tf_op jit(solution)/shard_map/dot_general | solution.py:47
  236.9 33.2 %reduce-scatter.7.cloned.1.call-done = f32[256,64]{0,1:T(8,128)} async-done(((f32[256,512]{0,1:T(8,128)}), f32[256,64]{0,1:T(8,128)}) %reduce-scatter.7.cloned.1.call-update) | async-done | bytes 65552 | tf_op jit(solution)/shard_map/reduce_scatter | solution.py:62
  270.2 8.7 %convolution_bitcast_fusion = f32[192,2400]{1,0:T(8,128)} fusion(f32[512,2400]{0,1:T(8,128)} %all-gather.5.cloned.1.call-done, f32[192,512]{1,0:T(8,128)S(1)} %bitcast.79), kind=kOutput, calls=%fused_computation | convolution fusion | flops 2831155200 | bytes 7151616 | tf_op jit(solution)/shard_map/dot_general | solution.py:50
  281.5 5.6 %copy.60 = f32[8,24,3,8,100]{1,4,2,0,3:T(8,128)} copy(f32[8,24,3,8,100]{4,3,2,1,0:T(8,128)S(1)} %reshape.129) | data formatting | bytes 3686400 | tf_op jit(solution)/shard_map/reshape | solution.py:51
  287.1 6.4 %reshape.130 = f32[8,24,2400]{2,1,0:T(8,128)S(1)} reshape(f32[8,8,3,100,24]{4,3,2,1,0:T(8,128)} %bitcast.65) | data formatting | bytes 3686400 | tf_op jit(solution)/shard_map/reshape | solution.py:52
  293.6 26.7 %all_to_all.32 = f32[8,24,2400]{2,1,0:T(8,128)S(1)} all-to-all(f32[8,24,2400]{2,1,0:T(8,128)S(1)} %reshape.130), channel_id=1, replica_groups=mesh['amp'=8,'int'=4] {'amp'}, dimensions={0} | all-to-all | bytes 3686400 | tf_op jit(solution)/shard_map/all_to_all | solution.py:53
  320.3 11.2 %fusion.3 = f32[192,512]{0,1:T(8,128)} fusion(f32[192,2400]{1,0:T(8,128)S(1)} %bitcast.72, f32[2400,512]{1,0:T(8,128)} %bitcast.63), kind=kOutput, calls=%fused_computation.22 | convolution fusion | flops 2831155200 | bytes 7151616 | tf_op jit(solution)/shard_map/dot_general | solution.py:61
  331.5 8.9 %convolution_bitcast_fusion.1 = f32[192,2400]{1,0:T(8,128)} fusion(f32[512,2400]{0,1:T(8,128)} %all-gather.5.cloned.1.call-done, f32[192,512]{1,0:T(8,128)S(1)} %copy-done.1), kind=kOutput, calls=%fused_computation.1 | convolution fusion | flops 2831155200 | bytes 7151616 | tf_op jit(solution)/shard_map/dot_general | solution.py:47
  340.4 24.5 %reduce-scatter.9.cloned.1.call-done = f32[192,64]{0,1:T(8,128)} async-done(((f32[192,512]{0,1:T(8,128)}), f32[192,64]{0,1:T(8,128)}) %reduce-scatter.9.cloned.1.call-update) | async-done | bytes 49168 | tf_op jit(solution)/shard_map/reduce_scatter | solution.py:62
  373.6 4.3 all-to-all-start.3
  378.7 3.4 convolution_bitcast_fusion.3
  382.1 4.9 %concatenate.6 = f32[192,6400]{1,0:T(8,128)} concatenate(f32[192,3200]{1,0:T(8,128)S(1)} %copy-done, f32[192,2400]{1,0:T(8,128)} %convolution_bitcast_fusion.1, f32[192,800]{1,0:T(8,128)S(1)} %convolution_bitcast_fusion.3), dimensions={1} | concatenate | bytes 9830400 | tf_op jit(solution)/shard_map/concatenate | solution.py:58
  388.7 11.2 %convolution_bitcast_fusion.5 = f32[512,64]{1,0:T(8,128)} fusion(f32[2400,512]{1,0:T(8,128)} %bitcast.64, f32[8,8,2400]{2,1,0:T(8,128)} %all-to-all-done.3), kind=kOutput, calls=%fused_computation.5 | convolution fusion | flops 943718400 | bytes 5660672
  400.3 33.1 %reduce-scatter.13.cloned.1.call-done = f32[64,64]{1,0:T(8,128)} async-done(((f32[512,64]{1,0:T(8,128)}), f32[64,64]{1,0:T(8,128)}) %reduce-scatter.13.cloned.1.call-update) | async-done | bytes 16400
  435.6 19.8 %reduce-scatter.11.cloned.1.call-done = f32[128,64]{1,0:T(8,128)} async-done(((f32[512,64]{1,0:T(8,128)}), f32[128,64]{1,0:T(8,128)}) %reduce-scatter.11.cloned.1.call-update) | async-done | bytes 32784 | tf_op jit(solution)/shard_map/reduce_scatter | solution.py:69
  (56 shorter events, 23.7 us)
Async XLA Ops:
  7.2 133.6 %all-gather.7.cloned.1.call-start = ((), (), s32[]{:S(2)}) async-start(), calls=%async_computation.9 | async-start | bytes 8192000 | tf_op jit(solution)/shard_map/all_gather | solution.py:40
  12.0 224.9 %all-gather.5.cloned.1.call-start = ((), (), s32[]{:S(2)}) async-start(), calls=%async_computation.8 | async-start | bytes 6144000 | tf_op jit(solution)/shard_map/all_gather | solution.py:40
  13.3 256.9 %reduce-scatter.7.cloned.1.call-start = ((), (), s32[]{:S(2)}) async-start(), calls=%async_computation.10 | async-start | bytes 589824 | tf_op jit(solution)/shard_map/reduce_scatter | solution.py:62
  224.9 115.4 %all-gather.9.cloned.1.call-start = ((), (), s32[]{:S(2)}) async-start(), calls=%async_computation.13 | async-start | bytes 2048000 | tf_op jit(solution)/shard_map/all_gather | solution.py:40
  225.8 44.4 %copy-start.2 = (f32[4,2,24,512]{3,2,1,0:T(8,128)S(1)}, f32[4,2,24,512]{3,2,1,0:T(8,128)}, u32[]{:S(2)}) copy-start(f32[4,2,24,512]{3,2,1,0:T(8,128)} %copy.57) | copy-start | bytes 1179652
  225.8 139.1 %reduce-scatter.9.cloned.1.call-start = ((), (), s32[]{:S(2)}) async-start(), calls=%async_computation.11 | async-start | bytes 589824 | tf_op jit(solution)/shard_map/reduce_scatter | solution.py:62
  320.3 11.2 %copy-start.1 = (f32[192,512]{1,0:T(8,128)S(1)}, f32[192,512]{1,0:T(8,128)}, u32[]{:S(2)}) copy-start(f32[192,512]{1,0:T(8,128)} %param.5) | copy-start | bytes 1179652
  371.8 6.9 %copy-start.5 = (s32[96]{0:T(128)S(1)}, s32[96]{0:T(128)}, u32[]{:S(2)}) copy-start(s32[96]{0:T(128)} %param.8) | copy-start | bytes 1156
  373.5 8.6 %copy-start = (f32[192,3200]{1,0:T(8,128)S(1)}, f32[192,3200]{1,0:T(8,128)}, u32[]{:S(2)}) copy-start(f32[192,3200]{1,0:T(8,128)} %fusion.1) | copy-start | bytes 7372804
  373.6 15.1 %all-to-all-start.3 = ((f32[8,8,2400]{2,1,0:T(8,128)}), f32[8,8,2400]{2,1,0:T(8,128)}, u32[]{:S(2)}, u32[]{:S(2)}) async-start(f32[8,8,2400]{2,1,0:T(8,128)} %reshape.133), calls=%async_computation.5 | async-start | bytes 1245184 | tf_op jit(solution)/shard_map/all_to_all | solution.py:53
  377.9 55.5 %reduce-scatter.13.cloned.1.call-start = ((), (), s32[]{:S(2)}) async-start(), calls=%async_computation.14 | async-start | bytes 294912
  387.0 13.0 %copy-start.3 = (f32[256,64]{0,1:T(8,128)S(1)}, f32[256,64]{0,1:T(8,128)}, u32[]{:S(2)}) copy-start(f32[256,64]{0,1:T(8,128)} %reduce-scatter.7.cloned.1.call-done) | copy-start | bytes 196612
  387.0 13.1 %copy-start.4 = (f32[192,64]{0,1:T(8,128)S(1)}, f32[192,64]{0,1:T(8,128)}, u32[]{:S(2)}) copy-start(f32[192,64]{0,1:T(8,128)} %reduce-scatter.9.cloned.1.call-done) | copy-start | bytes 147460
  399.9 55.4 %reduce-scatter.11.cloned.1.call-start = ((), (), s32[]{:S(2)}) async-start(), calls=%async_computation.12 | async-start | bytes 327680 | tf_op jit(solution)/shard_map/reduce_scatter | solution.py:69
Sparse Core Ops, SparseCore 0:
  12.1 128.6 all-gather.6
  142.3 92.3 all-gather.4
  237.8 32.3 reduce-scatter.6
  271.7 38.7 all-gather.8
  331.6 33.2 reduce-scatter.8
  400.1 33.2 reduce-scatter.12
  435.8 19.5 reduce-scatter.10

commit v6 on v4

--- a/solution.py
+++ b/solution.py
@@ -54,10 +54,11 @@
     parts = jnp.concatenate(
         [c.reshape(n_amp, ibat, sizes[t], columns) for t, c in enumerate(cycle_chunks)], axis=2
     )
-    parts = parts.transpose(1, 0, 2, 3).reshape(ibat * slab, columns)
-    narrowed = lax.psum_scatter(parts, "amp", scatter_dimension=1, tiled=True)
-    sums = lax.psum_scatter(narrowed, "int", scatter_dimension=0, tiled=True)
-    col_local = sums.shape[1]
+    col_local = columns // n_amp
+    parts = parts.transpose(1, 0, 2, 3).reshape(n_int, i_local * slab, n_amp, col_local)
+    parts = parts.transpose(0, 2, 1, 3).reshape(n_int * n_amp, i_local * slab, col_local)
+    gathered = lax.all_to_all(parts, ("int", "amp"), split_axis=0, concat_axis=0, tiled=True)
+    sums = jnp.sum(gathered, axis=0)
 
     row_start = lax.axis_index("int") * i_local
     batch_labels = lax.dynamic_slice_in_dim(occ_irrep, row_start, i_local, 0)

time: 392 us -> 369 us (0.941)
  waiting for transfers between devices: 219 us -> 193 us
    unnamed x6 -> x3, waiting for transfers between devices: 32 us -> 0.73 us
    all_to_all x0 -> x1, waiting for transfers between devices: none -> 12.7 us  [per_device(): lax.all_to_all(parts, ('int', 'amp'), split_axis=0, concat_axis=0, tiled=...]
    reduce_scatter x1 -> x0, waiting for transfers between devices: 7.85 us -> none  [per_device(): sums = lax.psum_scatter(narrowed, 'int', scatter_dimension=0, tiled=True)]
    unnamed x14 -> x11, local copies, waits for them, and re-layouts: 8.77 us -> 3.5 us
  transfers between devices with their start and end apart: 9 -> 8, of which waited for: 9 -> 8; matrix products, arithmetic and copies ran while one was open for 26% -> 27% of each run, Pallas kernels for 0% -> 0%
where the time goes in v6:
time: 369 us; the launch traced here: 363 us
  waiting for transfers between devices  193 us (52%)
  local copies, waits for them, and re-layouts  68.6 us (19%)
  matrix products  62.9 us (17%)
  starting transfers between devices  21.8 us (6%)
  between operations  14.4 us (4%)
    all_gather x3, waiting for transfers between devices, per_device(): v_all = lax.all_gather(v, 'int', axis=0, tiled=True)  104 us
    all_to_all x3, waiting for transfers between devices, per_device(): lax.all_to_all(l_cyc, 'amp', split_axis=0, concat_axis=0, tiled=True)  48 us
    all_to_all x1, waiting for transfers between devices, per_device(): lax.all_to_all(amplitudes.reshape(i_local, nocc, pw), 'int', split_axis=1...  27.4 us
    dot_general x3, matrix products, per_device(): jnp.dot(amplitudes, v_all, precision=HIGHEST, preferred_element_type=jnp....  22.9 us
    dot_general x3, matrix products, per_device(): jnp.dot(t_cyc, v_all, precision=HIGHEST, preferred_element_type=jnp.float32)  21.7 us
    reshape x3, local copies, waits for them, and re-layouts, per_device(): l_cyc = l_cyc.reshape(n_amp, ibat * a_chunk, c_local * k_local)  20.7 us
    dot_general x3, matrix products, per_device(): jnp.dot(moved, w2, precision=HIGHEST, preferred_element_type=jnp.float32)  18.2 us
    reshape x4, local copies, waits for them, and re-layouts, per_device(): l_cyc.reshape(ibat, k_local, a_chunk, n_amp, c_local)  14.3 us
  transfers between devices with their start and end apart: 8, of which 8 were waited for; matrix products, arithmetic and copies ran while one was open for 27% of the time, Pallas kernels for 0%

profile of v6, /device:TPU:0, one launch (start us, length us, event | category | flops | bytes accessed | tf_op | source)
XLA Modules:
  0.0 363.2 jit_solution(1282037852631214703)
XLA Ops:
  15.2 6.3 %all-to-all-start = ((f32[2,96,512]{2,0,1:T(2,128)}), f32[2,96,512]{2,0,1:T(2,128)}, u32[]{:S(2)}, u32[]{:S(2)}) async-start(f32[2,96,512]{2,0,1:T(2,128)} %copy.53), calls=%async_computation | async-start | bytes 786432 | tf_op jit(solution)/shard_map/all_to_all | solution.py:25
  22.5 27.4 %all-to-all-done = f32[2,96,512]{2,0,1:T(2,128)} async-done(((f32[2,96,512]{2,0,1:T(2,128)}), f32[2,96,512]{2,0,1:T(2,128)}, u32[]{:S(2)}, u32[]{:S(2)}) %all-to-all-start) | async-done | bytes 393248 | tf_op jit(solution)/shard_map/all_to_all | solution.py:25
  51.0 64.2 %all-gather.6.cloned.1.call-done = f32[512,2400]{0,1:T(8,128)} async-done(((f32[128,2400]{0,1:T(8,128)}), f32[512,2400]{0,1:T(8,128)}) %all-gather.6.cloned.1.call-update) | async-done | bytes 4915216 | tf_op jit(solution)/shard_map/all_gather | solution.py:36
  120.5 7.7 %convolution_bitcast_fusion.4 = f32[8,8,3,100,24]{3,4,0,2,1:T(8,128)S(1)} fusion(f32[8,24,512,1,1]{2,1,4,3,0:T(8,128)S(1)} %bitcast.76, f32[3,8,100,512,1]{3,2,1,0,4:T(8,128)} %reshape.140), kind=kOutput, calls=%fused_computation.4 | convolution fusion | flops 2831155200 | bytes 7151616 | tf_op jit(solution)/shard_map/dot_general | solution.py:44
  128.2 5.6 %copy.56 = f32[8,8,3,100,24]{4,3,2,1,0:T(8,128)} copy(f32[8,8,3,100,24]{3,4,0,2,1:T(8,128)S(1)} %convolution_bitcast_fusion.4) | data formatting | bytes 3686400 | tf_op jit(solution)/shard_map/transpose | solution.py:45
  133.8 7.5 %reshape.125 = f32[8,24,2400]{2,1,0:T(8,128)} reshape(f32[8,8,3,100,24]{4,3,2,1,0:T(8,128)} %copy.56) | data formatting | bytes 3686400 | tf_op jit(solution)/shard_map/reshape | solution.py:46
  145.4 8.6 %fusion.1 = f32[192,2400]{1,0:T(8,128)} fusion(f32[192,512]{1,0:T(8,128)S(1)} %copy-done.1, f32[512,2400]{0,1:T(8,128)} %all-gather.6.cloned.1.call-done), kind=kOutput, calls=%fused_computation.19 | convolution fusion | flops 2831155200 | bytes 7151616 | tf_op jit(solution)/shard_map/dot_general | solution.py:42
  154.1 15.5 %all-to-all-done.1 = f32[8,24,2400]{2,1,0:T(8,128)S(1)} async-done(((f32[8,24,2400]{2,1,0:T(8,128)}), f32[8,24,2400]{2,1,0:T(8,128)S(1)}, u32[]{:S(2)}, u32[]{:S(2)}) %all-to-all-start.1) | async-done | bytes 1843232 | tf_op jit(solution)/shard_map/all_to_all | solution.py:47
  169.6 6.4 %fusion.2 = f32[192,512]{1,0:T(8,128)} fusion(f32[192,2400]{1,0:T(8,128)S(1)} %bitcast.70, f32[2400,512]{1,0:T(8,128)} %bitcast.63), kind=kOutput, calls=%fused_computation.20 | convolution fusion | flops 2831155200 | bytes 7151616 | tf_op jit(solution)/shard_map/dot_general | solution.py:50
  176.0 33.2 %all-gather.4.cloned.1.call-done = f32[512,2400]{0,1:T(8,128)} async-done(((f32[128,2400]{0,1:T(8,128)}), f32[512,2400]{0,1:T(8,128)}) %all-gather.4.cloned.1.call-update) | async-done | bytes 4915216 | tf_op jit(solution)/shard_map/all_gather | solution.py:36
  209.2 8.7 %convolution_bitcast_fusion = f32[192,2400]{1,0:T(8,128)} fusion(f32[512,2400]{0,1:T(8,128)} %all-gather.4.cloned.1.call-done, f32[192,512]{1,0:T(8,128)S(1)} %bitcast.77), kind=kOutput, calls=%fused_computation | convolution fusion | flops 2831155200 | bytes 7151616 | tf_op jit(solution)/shard_map/dot_general | solution.py:44
  220.5 5.6 %copy.58 = f32[8,24,3,8,100]{1,4,2,0,3:T(8,128)} copy(f32[8,24,3,8,100]{4,3,2,1,0:T(8,128)S(1)} %reshape.130) | data formatting | bytes 3686400 | tf_op jit(solution)/shard_map/reshape | solution.py:45
  226.1 7.6 %reshape.131 = f32[8,24,2400]{2,1,0:T(8,128)} reshape(f32[8,8,3,100,24]{4,3,2,1,0:T(8,128)} %bitcast.61) | data formatting | bytes 3686400 | tf_op jit(solution)/shard_map/reshape | solution.py:46
  237.5 8.8 %convolution_bitcast_fusion.1 = f32[192,2400]{1,0:T(8,128)} fusion(f32[512,2400]{0,1:T(8,128)} %all-gather.4.cloned.1.call-done, f32[192,512]{1,0:T(8,128)S(1)} %copy-done.1), kind=kOutput, calls=%fused_computation.1 | convolution fusion | flops 2831155200 | bytes 7151616 | tf_op jit(solution)/shard_map/dot_general | solution.py:42
  246.3 15.4 %all-to-all-done.2 = f32[8,24,2400]{2,1,0:T(8,128)S(1)} async-done(((f32[8,24,2400]{2,1,0:T(8,128)}), f32[8,24,2400]{2,1,0:T(8,128)S(1)}, u32[]{:S(2)}, u32[]{:S(2)}) %all-to-all-start.2) | async-done | bytes 1843232 | tf_op jit(solution)/shard_map/all_to_all | solution.py:47
  261.7 6.4 %fusion.3 = f32[192,512]{1,0:T(8,128)} fusion(f32[192,2400]{1,0:T(8,128)S(1)} %bitcast.71, f32[2400,512]{1,0:T(8,128)} %bitcast.64), kind=kOutput, calls=%fused_computation.21 | convolution fusion | flops 2831155200 | bytes 7151616 | tf_op jit(solution)/shard_map/dot_general | solution.py:50
  268.1 6.5 %all-gather.8.cloned.1.call-done = f32[512,1600]{0,1:T(8,128)} async-done(((f32[128,1600]{0,1:T(8,128)}), f32[512,1600]{0,1:T(8,128)}) %all-gather.8.cloned.1.call-update) | async-done | bytes 3276816 | tf_op jit(solution)/shard_map/all_gather | solution.py:36
  274.6 5.4 %convolution_bitcast_fusion.2 = f32[192,1600]{1,0:T(8,128)S(1)} fusion(f32[512,1600]{0,1:T(8,128)} %all-gather.8.cloned.1.call-done, f32[192,512]{1,0:T(8,128)S(1)} %bitcast.78), kind=kOutput, calls=%fused_computation.2 | convolution fusion | flops 1887436800 | bytes 4898816 | tf_op jit(solution)/shard_map/dot_general | solution.py:44
  286.1 5.6 %reshape.136 = f32[8,16,2400]{2,1,0:T(8,128)} reshape(f32[8,8,2,100,24]{4,3,2,1,0:T(8,128)} %bitcast.62) | data formatting | bytes 2457600 | tf_op jit(solution)/shard_map/reshape | solution.py:46
  296.1 17.1 %all-to-all-done.3 = f32[8,16,2400]{2,1,0:T(8,128)S(1)} async-done(((f32[8,16,2400]{2,1,0:T(8,128)}), f32[8,16,2400]{2,1,0:T(8,128)S(1)}, u32[]{:S(2)}, u32[]{:S(2)}) %all-to-all-start.3) | async-done | bytes 1228832 | tf_op jit(solution)/shard_map/all_to_all | solution.py:47
  313.6 5.4 %fusion.4 = f32[8,8,2,512]{3,0,2,1:T(8,128)S(1)} fusion(f32[8,8,2,2400]{3,0,2,1:T(8,128)S(1)} %bitcast.81, f32[2400,512,1,1]{1,0,3,2:T(8,128)} %bitcast.65), kind=kOutput, calls=%fused_computation.22 | convolution fusion | flops 1887436800 | bytes 6406144 | tf_op jit(solution)/shard_map/dot_general | solution.py:50
  329.4 5.6 %convolution_bitcast_fusion.3 = f32[192,1600]{1,0:T(8,128)} fusion(f32[512,1600]{0,1:T(8,128)S(1)} %copy-done, f32[192,512]{1,0:T(8,128)} %param.5), kind=kOutput, calls=%fused_computation.3 | convolution fusion | flops 1887436800 | bytes 4898816 | tf_op jit(solution)/shard_map/dot_general | solution.py:42
  335.0 6.6 %concatenate.6 = f32[192,6400]{1,0:T(8,128)} concatenate(f32[192,2400]{1,0:T(8,128)} %fusion.1, f32[192,2400]{1,0:T(8,128)} %convolution_bitcast_fusion.1, f32[192,1600]{1,0:T(8,128)} %convolution_bitcast_fusion.3), dimensions={1} | concatenate | bytes 9830400 | tf_op jit(solution)/shard_map/concatenate | solution.py:52
  341.6 12.7 %all-to-all-done.4 = f32[32,128,64]{1,2,0:T(8,128)} async-done(((f32[32,128,64]{1,2,0:T(8,128)}), f32[32,128,64]{1,2,0:T(8,128)}, u32[]{:S(2)}, u32[]{:S(2)}) %all-to-all-start.4) | async-done | bytes 1048608 | tf_op jit(solution)/shard_map/all_to_all | solution.py:60
  (48 shorter events, 49.2 us)
Async XLA Ops:
  7.2 108.1 %all-gather.6.cloned.1.call-start = ((), (), s32[]{:S(2)}) async-start(), calls=%async_computation.6 | async-start | bytes 6144000 | tf_op jit(solution)/shard_map/all_gather | solution.py:36
  12.4 196.8 %all-gather.4.cloned.1.call-start = ((), (), s32[]{:S(2)}) async-start(), calls=%async_computation.5 | async-start | bytes 6144000 | tf_op jit(solution)/shard_map/all_gather | solution.py:36
  15.2 34.7 %all-to-all-start = ((f32[2,96,512]{2,0,1:T(2,128)}), f32[2,96,512]{2,0,1:T(2,128)}, u32[]{:S(2)}, u32[]{:S(2)}) async-start(f32[2,96,512]{2,0,1:T(2,128)} %copy.53), calls=%async_computation | async-start | bytes 786432 | tf_op jit(solution)/shard_map/all_to_all | solution.py:25
  21.5 253.1 %all-gather.8.cloned.1.call-start = ((), (), s32[]{:S(2)}) async-start(), calls=%async_computation.7 | async-start | bytes 4096000 | tf_op jit(solution)/shard_map/all_gather | solution.py:36
  141.4 4.1 %copy-start.1 = (f32[192,512]{1,0:T(8,128)S(1)}, f32[192,512]{1,0:T(8,128)}, u32[]{:S(2)}) copy-start(f32[192,512]{1,0:T(8,128)} %param.5) | copy-start | bytes 1179652
  141.4 28.2 %all-to-all-start.1 = ((f32[8,24,2400]{2,1,0:T(8,128)}), f32[8,24,2400]{2,1,0:T(8,128)S(1)}, u32[]{:S(2)}, u32[]{:S(2)}) async-start(f32[8,24,2400]{2,1,0:T(8,128)} %reshape.125), calls=%async_computation.1 | async-start | bytes 3735552 | tf_op jit(solution)/shard_map/all_to_all | solution.py:47
  233.6 28.0 %all-to-all-start.2 = ((f32[8,24,2400]{2,1,0:T(8,128)}), f32[8,24,2400]{2,1,0:T(8,128)S(1)}, u32[]{:S(2)}, u32[]{:S(2)}) async-start(f32[8,24,2400]{2,1,0:T(8,128)} %reshape.131), calls=%async_computation.2 | async-start | bytes 3735552 | tf_op jit(solution)/shard_map/all_to_all | solution.py:47
  286.1 9.7 %copy-start.2 = (f32[192,512]{1,0:T(8,128)S(1)}, f32[192,512]{1,0:T(8,128)}, u32[]{:S(2)}) copy-start(f32[192,512]{1,0:T(8,128)} %fusion.2) | copy-start | bytes 1179652
  291.7 4.3 %copy-start.3 = (f32[192,512]{1,0:T(8,128)S(1)}, f32[192,512]{1,0:T(8,128)}, u32[]{:S(2)}) copy-start(f32[192,512]{1,0:T(8,128)} %fusion.3) | copy-start | bytes 1179652
  291.7 21.5 %all-to-all-start.3 = ((f32[8,16,2400]{2,1,0:T(8,128)}), f32[8,16,2400]{2,1,0:T(8,128)S(1)}, u32[]{:S(2)}, u32[]{:S(2)}) async-start(f32[8,16,2400]{2,1,0:T(8,128)} %reshape.136), calls=%async_computation.3 | async-start | bytes 2490368 | tf_op jit(solution)/shard_map/all_to_all | solution.py:47
  321.4 7.4 %copy-start.4 = (s32[96]{0:T(128)S(1)}, s32[96]{0:T(128)}, u32[]{:S(2)}) copy-start(s32[96]{0:T(128)} %param.8) | copy-start | bytes 1156
  321.4 8.0 %copy-start = (f32[512,1600]{0,1:T(8,128)S(1)}, f32[512,1600]{0,1:T(8,128)}, u32[]{:S(2)}) copy-start(f32[512,1600]{0,1:T(8,128)} %all-gather.8.cloned.1.call-done) | copy-start | bytes 9830404
  324.7 29.6 %all-to-all-start.4 = ((f32[32,128,64]{1,2,0:T(8,128)}), f32[32,128,64]{1,2,0:T(8,128)}, u32[]{:S(2)}, u32[]{:S(2)}) async-start(f32[32,128,64]{1,2,0:T(8,128)} %bitcast.75), calls=%async_computation.4 | async-start | bytes 2097152 | tf_op jit(solution)/shard_map/all_to_all | solution.py:60
Sparse Core Ops, SparseCore 0:
  12.5 102.6 all-gather.5
  116.8 92.3 all-gather.3
  210.8 63.7 all-gather.7

commit v7 on v6

--- a/solution.py
+++ b/solution.py
@@ -4,7 +4,6 @@
 from jax.sharding import PartitionSpec as P
 
 HIGHEST = lax.Precision.HIGHEST
-CHUNKS = 3
 
 
 def per_device(amplitudes, slab_integrals, cycle_integrals, occ_irrep, vir_irrep, n_amp, n_int):
@@ -18,8 +17,13 @@
     a_local = width // nvir
     slab = a_local * n_amp
     k_local, c_local, columns = cycle_integrals.shape
-    chunks = min(CHUNKS, a_local)
-    sizes = [a_local // chunks + (1 if t < a_local % chunks else 0) for t in range(chunks)]
+    if a_local >= 4:
+        sizes = [a_local // 2, a_local - a_local // 2 - 1, 1]
+    elif a_local >= 2:
+        sizes = [a_local - 1, 1]
+    else:
+        sizes = [a_local]
+    chunks = len(sizes)
     starts = [sum(sizes[:t]) for t in range(chunks)]
 
     t_cyc = lax.all_to_all(
@@ -27,12 +31,11 @@
     ).reshape(ibat * k_local, pw)
     w2 = cycle_integrals.transpose(1, 0, 2).reshape(c_local * k_local, columns)
 
-    slab3 = slab_integrals.reshape(pw_local, a_local, nvir)
     ladder_chunks = []
     cycle_chunks = []
     for t in range(chunks):
         a_chunk = sizes[t]
-        v = slab3[:, starts[t]:starts[t] + a_chunk, :].reshape(pw_local, a_chunk * nvir)
+        v = lax.slice_in_dim(slab_integrals, starts[t] * nvir, (starts[t] + a_chunk) * nvir, axis=1)
         v_all = lax.all_gather(v, "int", axis=0, tiled=True)
         if t:
             v_all, ladder_chunks[-1], cycle_chunks[-1] = lax.optimization_barrier(

time: 369 us -> 368 us (level)
  waiting for transfers between devices: 193 us -> 166 us
  blocking collectives: 0 us -> 25.5 us
  local copies, waits for them, and re-layouts: 68.6 us -> 76.8 us
  starting transfers between devices: 21.8 us -> 14.8 us
    all_to_all x1 -> x0, waiting for transfers between devices: 27.4 us -> none  [per_device(): lax.all_to_all(amplitudes.reshape(i_local, nocc, pw), 'int', split_axis=1...]
    all_to_all x0 -> x1, blocking collectives: none -> 25.5 us  [per_device(): lax.all_to_all(amplitudes.reshape(i_local, nocc, pw), 'int', split_axis=1...]
    dot_general x1 -> x2, local copies, waits for them, and re-layouts: 5.26 us -> 15.9 us  [per_device(): jnp.dot(t_cyc, v_all, precision=HIGHEST, preferred_element_type=jnp.float32)]
    all_to_all x1 -> x0, starting transfers between devices: 6.32 us -> none  [per_device(): lax.all_to_all(amplitudes.reshape(i_local, nocc, pw), 'int', split_axis=1...]
    slice x2 -> x3, local copies, waits for them, and re-layouts: 2.64 us -> 7.12 us  [per_device(): lax.slice_in_dim(slab_integrals, starts[t] * nvir, (starts[t] + a_chunk)...]
    all_to_all x1, waiting for transfers between devices: 12.7 us -> 16.9 us  [per_device(): lax.all_to_all(parts, ('int', 'amp'), split_axis=0, concat_axis=0, tiled=...]
    transpose x1, local copies, waits for them, and re-layouts: 5.63 us -> 9.35 us  [per_device(): l_cyc.reshape(ibat, k_local, a_chunk, n_amp, c_local)]
  transfers between devices with their start and end apart: 8 -> 7, of which waited for: 8 -> 6; matrix products, arithmetic and copies ran while one was open for 27% -> 32% of each run, Pallas kernels for 0% -> 0%
where the time goes in v7:
time: 368 us; the launch traced here: 361 us
  waiting for transfers between devices  166 us (45%)
  local copies, waits for them, and re-layouts  76.8 us (21%)
  matrix products  61.2 us (17%)
  blocking collectives  25.5 us (7%)
  starting transfers between devices  14.8 us (4%)
  between operations  14.3 us (4%)
    all_gather x3, waiting for transfers between devices, per_device(): v_all = lax.all_gather(v, 'int', axis=0, tiled=True)  104 us
    all_to_all x3, waiting for transfers between devices, per_device(): lax.all_to_all(l_cyc, 'amp', split_axis=0, concat_axis=0, tiled=True)  44.7 us
    all_to_all x1, blocking collectives, per_device(): lax.all_to_all(amplitudes.reshape(i_local, nocc, pw), 'int', split_axis=1...  25.5 us
    dot_general x3, matrix products, per_device(): jnp.dot(t_cyc, v_all, precision=HIGHEST, preferred_element_type=jnp.float32)  22 us
    dot_general x3, matrix products, per_device(): jnp.dot(moved, w2, precision=HIGHEST, preferred_element_type=jnp.float32)  19.6 us
    dot_general x3, matrix products, per_device(): jnp.dot(amplitudes, v_all, precision=HIGHEST, preferred_element_type=jnp....  19.6 us
    reshape x3, local copies, waits for them, and re-layouts, per_device(): l_cyc = l_cyc.reshape(n_amp, ibat * a_chunk, c_local * k_local)  18.9 us
    all_to_all x1, waiting for transfers between devices, per_device(): lax.all_to_all(parts, ('int', 'amp'), split_axis=0, concat_axis=0, tiled=...  16.9 us
  transfers between devices with their start and end apart: 7, of which 6 were waited for; matrix products, arithmetic and copies ran while one was open for 32% of the time, Pallas kernels for 0%

profile of v7, /device:TPU:0, one launch (start us, length us, event | category | flops | bytes accessed | tf_op | source)
XLA Modules:
  0.0 361.4 jit_solution(6253134383679959750)
XLA Ops:
  12.8 25.5 %all_to_all.35 = f32[2,96,512]{2,0,1:T(2,128)S(1)} all-to-all(f32[2,96,512]{2,0,1:T(2,128)S(1)} %copy.52), channel_id=1, replica_groups=mesh['amp'=8,'int'=4] {'int'}, dimensions={1} | all-to-all | bytes 786432 | tf_op jit(solution)/shard_map/all_to_all | solution.py:29
  38.4 98.3 %all-gather.6.cloned.1.call-done = f32[512,3200]{1,0:T(8,128)} async-done(((f32[128,3200]{1,0:T(8,128)}), f32[512,3200]{1,0:T(8,128)}) %all-gather.6.cloned.1.call-update) | async-done | bytes 6553616 | tf_op jit(solution)/shard_map/all_gather | solution.py:39
  136.7 8.2 %copy.55 = f32[3200,512]{1,0:T(8,128)} copy(f32[3200,512]{0,1:T(8,128)} %bitcast.62) | data formatting | bytes 13107200 | tf_op jit(solution)/shard_map/dot_general | solution.py:47
  144.9 7.7 %reshape.128 = f32[4,8,100,512,1]{3,2,1,0,4:T(8,128)} reshape(f32[3200,512]{1,0:T(8,128)} %copy.55) | data formatting | bytes 13107200 | tf_op jit(solution)/shard_map/dot_general | solution.py:47
  152.6 11.2 %convolution_bitcast_fusion.2 = f32[8,8,4,100,24]{3,4,0,2,1:T(8,128)} fusion(f32[8,24,512,1,1]{2,1,4,3,0:T(8,128)S(1)} %bitcast.69, f32[4,8,100,512,1]{3,2,1,0,4:T(8,128)} %reshape.128), kind=kOutput, calls=%fused_computation.2 | convolution fusion | flops 3774873600 | bytes 9404416 | tf_op jit(solution)/shard_map/dot_general | solution.py:47
  163.8 9.4 %copy.56 = f32[8,8,4,100,24]{4,3,2,1,0:T(8,128)} copy(f32[8,8,4,100,24]{3,4,0,2,1:T(8,128)} %convolution_bitcast_fusion.2) | data formatting | bytes 4915200 | tf_op jit(solution)/shard_map/transpose | solution.py:48
  173.2 9.6 %reshape.114 = f32[8,32,2400]{2,1,0:T(8,128)} reshape(f32[8,8,4,100,24]{4,3,2,1,0:T(8,128)} %copy.56) | data formatting | bytes 4915200 | tf_op jit(solution)/shard_map/reshape | solution.py:49
  182.8 3.7 %all-to-all-start.1 = ((f32[8,32,2400]{2,1,0:T(8,128)}), f32[8,32,2400]{2,1,0:T(8,128)S(1)}, u32[]{:S(2)}, u32[]{:S(2)}) async-start(f32[8,32,2400]{2,1,0:T(8,128)} %reshape.114), calls=%async_computation.1 | async-start | bytes 4980736 | tf_op jit(solution)/shard_map/all_to_all | solution.py:50
  188.7 8.9 %fusion = f32[192,3200]{1,0:T(8,128)} fusion(f32[192,512]{1,0:T(8,128)S(1)} %copy-done.1, f32[512,3200]{1,0:T(8,128)} %all-gather.6.cloned.1.call-done), kind=kOutput, calls=%fused_computation.19 | convolution fusion | flops 3774873600 | bytes 9404416 | tf_op jit(solution)/shard_map/dot_general | solution.py:45
  197.6 19.7 %all-to-all-done.1 = f32[8,32,2400]{2,1,0:T(8,128)S(1)} async-done(((f32[8,32,2400]{2,1,0:T(8,128)}), f32[8,32,2400]{2,1,0:T(8,128)S(1)}, u32[]{:S(2)}, u32[]{:S(2)}) %all-to-all-start.1) | async-done | bytes 2457632 | tf_op jit(solution)/shard_map/all_to_all | solution.py:50
  217.3 7.7 %fusion.1 = f32[256,512]{1,0:T(8,128)} fusion(f32[256,2400]{1,0:T(8,128)S(1)} %bitcast.64, f32[2400,512]{1,0:T(8,128)} %bitcast.58), kind=kOutput, calls=%fused_computation.20 | convolution fusion | flops 3774873600 | bytes 7897088 | tf_op jit(solution)/shard_map/dot_general | solution.py:53
  225.0 6.1 %all-gather.4.cloned.1.call-done = f32[512,2400]{1,0:T(8,128)} async-done(((f32[128,2400]{1,0:T(8,128)}), f32[512,2400]{1,0:T(8,128)}) %all-gather.4.cloned.1.call-update) | async-done | bytes 4915216 | tf_op jit(solution)/shard_map/all_gather | solution.py:39
  231.1 7.7 %convolution_bitcast_fusion = f32[192,2400]{1,0:T(8,128)} fusion(f32[512,2400]{1,0:T(8,128)} %all-gather.4.cloned.1.call-done, f32[192,512]{1,0:T(8,128)S(1)} %bitcast.70), kind=kOutput, calls=%fused_computation | convolution fusion | flops 2831155200 | bytes 7151616 | tf_op jit(solution)/shard_map/dot_general | solution.py:47
  241.5 5.7 %copy.58 = f32[8,24,3,8,100]{1,4,2,0,3:T(8,128)} copy(f32[8,24,3,8,100]{4,3,2,1,0:T(8,128)S(1)} %reshape.118) | data formatting | bytes 3686400 | tf_op jit(solution)/shard_map/reshape | solution.py:48
  247.2 7.6 %reshape.119 = f32[8,24,2400]{2,1,0:T(8,128)} reshape(f32[8,8,3,100,24]{4,3,2,1,0:T(8,128)} %bitcast.61) | data formatting | bytes 3686400 | tf_op jit(solution)/shard_map/reshape | solution.py:49
  254.7 3.6 all-to-all-start.2
  258.3 7.5 %convolution_bitcast_fusion.1 = f32[192,2400]{1,0:T(8,128)} fusion(f32[512,2400]{1,0:T(8,128)} %all-gather.4.cloned.1.call-done, f32[192,512]{1,0:T(8,128)S(1)} %copy-done.1), kind=kOutput, calls=%fused_computation.1 | convolution fusion | flops 2831155200 | bytes 7151616 | tf_op jit(solution)/shard_map/dot_general | solution.py:45
  265.9 16.6 %all-to-all-done.2 = f32[8,24,2400]{2,1,0:T(8,128)S(1)} async-done(((f32[8,24,2400]{2,1,0:T(8,128)}), f32[8,24,2400]{2,1,0:T(8,128)S(1)}, u32[]{:S(2)}, u32[]{:S(2)}) %all-to-all-start.2) | async-done | bytes 1843232 | tf_op jit(solution)/shard_map/all_to_all | solution.py:50
  282.5 6.4 %fusion.2 = f32[192,512]{1,0:T(8,128)} fusion(f32[192,2400]{1,0:T(8,128)S(1)} %bitcast.66, f32[2400,512]{1,0:T(8,128)} %bitcast.59), kind=kOutput, calls=%fused_computation.21 | convolution fusion | flops 2831155200 | bytes 7151616 | tf_op jit(solution)/shard_map/dot_general | solution.py:53
  297.3 3.8 %all-to-all-start.3 = ((f32[8,8,2400]{2,1,0:T(8,128)}), f32[8,8,2400]{2,1,0:T(8,128)S(1)}, u32[]{:S(2)}, u32[]{:S(2)}) async-start(f32[8,8,2400]{2,1,0:T(8,128)} %reshape.124), calls=%async_computation.3 | async-start | bytes 1245184 | tf_op jit(solution)/shard_map/all_to_all | solution.py:50
  303.4 8.4 %all-to-all-done.3 = f32[8,8,2400]{2,1,0:T(8,128)S(1)} async-done(((f32[8,8,2400]{2,1,0:T(8,128)}), f32[8,8,2400]{2,1,0:T(8,128)S(1)}, u32[]{:S(2)}, u32[]{:S(2)}) %all-to-all-start.3) | async-done | bytes 614432 | tf_op jit(solution)/shard_map/all_to_all | solution.py:50
  311.8 5.5 %convolution_bitcast_fusion.5 = f32[8,8,1,512]{3,1,0,2:T(8,128)S(1)} fusion(f32[8,8,2400]{2,1,0:T(8,128)S(1)} %all-to-all-done.3, f32[2400,512,1]{1,0,2:T(8,128)} %bitcast.60), kind=kOutput, calls=%fused_computation.5 | convolution fusion | flops 943718400 | bytes 5660672 | tf_op jit(solution)/shard_map/dot_general | solution.py:53
  330.7 4.9 %concatenate.6 = f32[192,6400]{1,0:T(8,128)} concatenate(f32[192,3200]{1,0:T(8,128)S(1)} %copy-done, f32[192,2400]{1,0:T(8,128)} %convolution_bitcast_fusion.1, f32[192,800]{1,0:T(8,128)S(1)} %convolution_bitcast_fusion.4), dimensions={1} | concatenate | bytes 9830400 | tf_op jit(solution)/shard_map/concatenate | solution.py:55
  335.6 16.9 %all-to-all-done.4 = f32[32,128,64]{1,2,0:T(8,128)} async-done(((f32[32,128,64]{1,2,0:T(8,128)}), f32[32,128,64]{1,2,0:T(8,128)}, u32[]{:S(2)}, u32[]{:S(2)}) %all-to-all-start.4) | async-done | bytes 1048608 | tf_op jit(solution)/shard_map/all_to_all | solution.py:63
  (44 shorter events, 36.5 us)
Async XLA Ops:
  7.2 129.5 %all-gather.6.cloned.1.call-start = ((), (), s32[]{:S(2)}) async-start(), calls=%async_computation.6 | async-start | bytes 8192000 | tf_op jit(solution)/shard_map/all_gather | solution.py:39
  9.9 2.5 copy-start.1
  9.9 221.2 %all-gather.4.cloned.1.call-start = ((), (), s32[]{:S(2)}) async-start(), calls=%async_computation.5 | async-start | bytes 6225920 | tf_op jit(solution)/shard_map/all_gather | solution.py:39
  182.8 34.6 %all-to-all-start.1 = ((f32[8,32,2400]{2,1,0:T(8,128)}), f32[8,32,2400]{2,1,0:T(8,128)S(1)}, u32[]{:S(2)}, u32[]{:S(2)}) async-start(f32[8,32,2400]{2,1,0:T(8,128)} %reshape.114), calls=%async_computation.1 | async-start | bytes 4980736 | tf_op jit(solution)/shard_map/all_to_all | solution.py:50
  186.5 102.5 %all-gather.8.cloned.1.call-start = ((), (), s32[]{:S(2)}) async-start(), calls=%async_computation.7 | async-start | bytes 2293760 | tf_op jit(solution)/shard_map/all_gather | solution.py:39
  254.7 27.8 %all-to-all-start.2 = ((f32[8,24,2400]{2,1,0:T(8,128)}), f32[8,24,2400]{2,1,0:T(8,128)S(1)}, u32[]{:S(2)}, u32[]{:S(2)}) async-start(f32[8,24,2400]{2,1,0:T(8,128)} %reshape.119), calls=%async_computation.2 | async-start | bytes 3735552 | tf_op jit(solution)/shard_map/all_to_all | solution.py:50
  297.3 14.5 %all-to-all-start.3 = ((f32[8,8,2400]{2,1,0:T(8,128)}), f32[8,8,2400]{2,1,0:T(8,128)S(1)}, u32[]{:S(2)}, u32[]{:S(2)}) async-start(f32[8,8,2400]{2,1,0:T(8,128)} %reshape.124), calls=%async_computation.3 | async-start | bytes 1245184 | tf_op jit(solution)/shard_map/all_to_all | solution.py:50
  319.5 7.4 %copy-start.3 = (s32[96]{0:T(128)S(1)}, s32[96]{0:T(128)}, u32[]{:S(2)}) copy-start(s32[96]{0:T(128)} %param.8) | copy-start | bytes 1156
  319.5 8.0 %copy-start.2 = (f32[192,512]{1,0:T(8,128)S(1)}, f32[192,512]{1,0:T(8,128)}, u32[]{:S(2)}) copy-start(f32[192,512]{1,0:T(8,128)} %param.5) | copy-start | bytes 1179652
  319.5 11.2 %copy-start = (f32[192,3200]{1,0:T(8,128)S(1)}, f32[192,3200]{1,0:T(8,128)}, u32[]{:S(2)}) copy-start(f32[192,3200]{1,0:T(8,128)} %fusion) | copy-start | bytes 7372804
  322.9 29.6 %all-to-all-start.4 = ((f32[32,128,64]{1,2,0:T(8,128)}), f32[32,128,64]{1,2,0:T(8,128)}, u32[]{:S(2)}, u32[]{:S(2)}) async-start(f32[32,128,64]{1,2,0:T(8,128)} %bitcast.68), calls=%async_computation.4 | async-start | bytes 2097152 | tf_op jit(solution)/shard_map/all_to_all | solution.py:63
Sparse Core Ops, SparseCore 0:
  10.1 126.4 all-gather.5
  138.3 92.8 all-gather.3
  232.7 39.7 all-gather.7

commit v8 on v7

--- a/solution.py
+++ b/solution.py
@@ -31,37 +31,38 @@
     ).reshape(ibat * k_local, pw)
     w2 = cycle_integrals.transpose(1, 0, 2).reshape(c_local * k_local, columns)
 
+    def contract(moved, a_chunk):
+        part = jnp.dot(moved, w2, precision=HIGHEST, preferred_element_type=jnp.float32)
+        part = part.reshape(n_amp, n_int, i_local, a_chunk, n_amp, col_local)
+        part = part.transpose(1, 4, 2, 0, 3, 5).reshape(n_int * n_amp, i_local * n_amp * a_chunk, col_local)
+        got = lax.all_to_all(part, ("int", "amp"), split_axis=0, concat_axis=0, tiled=True)
+        return jnp.sum(got, axis=0).reshape(i_local, n_amp, a_chunk, col_local)
+
+    col_local = columns // n_amp
     ladder_chunks = []
     cycle_chunks = []
+    moved = None
     for t in range(chunks):
         a_chunk = sizes[t]
         v = lax.slice_in_dim(slab_integrals, starts[t] * nvir, (starts[t] + a_chunk) * nvir, axis=1)
         v_all = lax.all_gather(v, "int", axis=0, tiled=True)
         if t:
-            v_all, ladder_chunks[-1], cycle_chunks[-1] = lax.optimization_barrier(
-                (v_all, ladder_chunks[-1], cycle_chunks[-1])
-            )
+            v_all, ladder_chunks[-1], moved = lax.optimization_barrier((v_all, ladder_chunks[-1], moved))
+        l_cyc = jnp.dot(t_cyc, v_all, precision=HIGHEST, preferred_element_type=jnp.float32)
+        l_cyc = l_cyc.reshape(ibat, k_local, a_chunk, n_amp, c_local).transpose(3, 0, 2, 4, 1)
+        l_cyc = l_cyc.reshape(n_amp, ibat * a_chunk, c_local * k_local)
+        moved_next = lax.all_to_all(l_cyc, "amp", split_axis=0, concat_axis=0, tiled=True)
+        moved_next = moved_next.reshape(n_amp * ibat * a_chunk, c_local * k_local)
+        if t:
+            cycle_chunks.append(contract(moved, sizes[t - 1]))
         ladder_chunks.append(
             jnp.dot(amplitudes, v_all, precision=HIGHEST, preferred_element_type=jnp.float32)
         )
-        l_cyc = jnp.dot(t_cyc, v_all, precision=HIGHEST, preferred_element_type=jnp.float32)
-        l_cyc = l_cyc.reshape(ibat, k_local, a_chunk, n_amp, c_local).transpose(3, 0, 2, 4, 1)
-        l_cyc = l_cyc.reshape(n_amp, ibat * a_chunk, c_local * k_local)
-        moved = lax.all_to_all(l_cyc, "amp", split_axis=0, concat_axis=0, tiled=True)
-        moved = moved.reshape(n_amp * ibat * a_chunk, c_local * k_local)
-        cycle_chunks.append(
-            jnp.dot(moved, w2, precision=HIGHEST, preferred_element_type=jnp.float32)
-        )
+        moved = moved_next
+    cycle_chunks.append(contract(moved, sizes[-1]))
     ladder = jnp.concatenate(ladder_chunks, axis=1)
 
-    parts = jnp.concatenate(
-        [c.reshape(n_amp, ibat, sizes[t], columns) for t, c in enumerate(cycle_chunks)], axis=2
-    )
-    col_local = columns // n_amp
-    parts = parts.transpose(1, 0, 2, 3).reshape(n_int, i_local * slab, n_amp, col_local)
-    parts = parts.transpose(0, 2, 1, 3).reshape(n_int * n_amp, i_local * slab, col_local)
-    gathered = lax.all_to_all(parts, ("int", "amp"), split_axis=0, concat_axis=0, tiled=True)
-    sums = jnp.sum(gathered, axis=0)
+    sums = jnp.concatenate(cycle_chunks, axis=2).reshape(i_local * slab, col_local)
 
     row_start = lax.axis_index("int") * i_local
     batch_labels = lax.dynamic_slice_in_dim(occ_irrep, row_start, i_local, 0)

time: 368 us -> 387 us (1.052)
  waiting for transfers between devices: 166 us -> 132 us
  matrix products: 61.2 us -> 80.8 us
  starting transfers between devices: 14.8 us -> 29.3 us
  local copies, waits for them, and re-layouts: 76.8 us -> 91 us
  other arithmetic: 2.77 us -> 7.45 us
    all_to_all x3, waiting for transfers between devices: 44.7 us -> 0.01 us  [per_device(): lax.all_to_all(l_cyc, 'amp', split_axis=0, concat_axis=0, tiled=True)]
    all_gather x3, waiting for transfers between devices: 104 us -> 132 us  [per_device(): v_all = lax.all_gather(v, 'int', axis=0, tiled=True)]
    dot_general x3, matrix products: 19.6 us -> 39.4 us  [contract(): jnp.dot(moved, w2, precision=HIGHEST, preferred_element_type=jnp.float32)]
    all_to_all x1 -> x3, waiting for transfers between devices: 16.9 us -> 0.01 us  [contract(): lax.all_to_all(part, ('int', 'amp'), split_axis=0, concat_axis=0, tiled=T...]
    all_to_all x1 -> x3, starting transfers between devices: 3.38 us -> 16.4 us  [contract(): lax.all_to_all(part, ('int', 'amp'), split_axis=0, concat_axis=0, tiled=T...]
    dot_general x1 -> x3, local copies, waits for them, and re-layouts: 0.14 us -> 11.4 us  [contract(): jnp.dot(moved, w2, precision=HIGHEST, preferred_element_type=jnp.float32)]
    all_to_all x0 -> x3, other arithmetic: none -> 6.08 us  [contract(): lax.all_to_all(part, ('int', 'amp'), split_axis=0, concat_axis=0, tiled=T...]
    unnamed x8 -> x21, local copies, waits for them, and re-layouts: 0.01 us -> 5.72 us
  transfers between devices with their start and end apart: 7 -> 9, of which waited for: 6 -> 2; matrix products, arithmetic and copies ran while one was open for 32% -> 46% of each run, Pallas kernels for 0% -> 0%
where the time goes in v8:
time: 387 us; the launch traced here: 380 us
  waiting for transfers between devices  132 us (34%)
  local copies, waits for them, and re-layouts  91 us (24%)
  matrix products  80.8 us (21%)
  starting transfers between devices  29.3 us (8%)
  blocking collectives  25.5 us (7%)
  between operations  14.3 us (4%)
  other arithmetic  7.45 us (2%)
    all_gather x3, waiting for transfers between devices, per_device(): v_all = lax.all_gather(v, 'int', axis=0, tiled=True)  132 us
    dot_general x3, matrix products, contract(): jnp.dot(moved, w2, precision=HIGHEST, preferred_element_type=jnp.float32)  39.4 us
    all_to_all x1, blocking collectives, per_device(): lax.all_to_all(amplitudes.reshape(i_local, nocc, pw), 'int', split_axis=1...  25.5 us
    dot_general x3, matrix products, per_device(): jnp.dot(t_cyc, v_all, precision=HIGHEST, preferred_element_type=jnp.float32)  21.8 us
    dot_general x3, matrix products, per_device(): jnp.dot(amplitudes, v_all, precision=HIGHEST, preferred_element_type=jnp....  19.6 us
    reshape x3, local copies, waits for them, and re-layouts, per_device(): l_cyc = l_cyc.reshape(n_amp, ibat * a_chunk, c_local * k_local)  19 us
    all_to_all x3, starting transfers between devices, contract(): lax.all_to_all(part, ('int', 'amp'), split_axis=0, concat_axis=0, tiled=T...  16.4 us
    dot_general x2, local copies, waits for them, and re-layouts, per_device(): jnp.dot(t_cyc, v_all, precision=HIGHEST, preferred_element_type=jnp.float32)  15.9 us
  transfers between devices with their start and end apart: 9, of which 2 were waited for; matrix products, arithmetic and copies ran while one was open for 46% of the time, Pallas kernels for 0%

profile of v8, /device:TPU:0, one launch (start us, length us, event | category | flops | bytes accessed | tf_op | source)
XLA Modules:
  0.0 380.2 jit_solution(7212597677535091195)
XLA Ops:
  12.8 25.5 %all_to_all.45 = f32[2,96,512]{2,0,1:T(2,128)S(1)} all-to-all(f32[2,96,512]{2,0,1:T(2,128)S(1)} %copy.72), channel_id=1, replica_groups=mesh['amp'=8,'int'=4] {'int'}, dimensions={1} | all-to-all | bytes 786432 | tf_op jit(solution)/shard_map/all_to_all | solution.py:29
  38.4 98.3 %all-gather.6.cloned.1.call-done = f32[512,3200]{1,0:T(8,128)} async-done(((f32[128,3200]{1,0:T(8,128)}), f32[512,3200]{1,0:T(8,128)}) %all-gather.6.cloned.1.call-update) | async-done | bytes 6553616 | tf_op jit(solution)/shard_map/all_gather | solution.py:48
  136.7 8.2 %copy.75 = f32[3200,512]{1,0:T(8,128)} copy(f32[3200,512]{0,1:T(8,128)} %bitcast.86) | data formatting | bytes 13107200 | tf_op jit(solution)/shard_map/dot_general | solution.py:51
  144.9 7.7 %reshape.146 = f32[4,8,100,512,1]{3,2,1,0,4:T(8,128)} reshape(f32[3200,512]{1,0:T(8,128)} %copy.75) | data formatting | bytes 13107200 | tf_op jit(solution)/shard_map/dot_general | solution.py:51
  152.6 11.2 %convolution_bitcast_fusion.2 = f32[8,8,4,100,24]{3,4,0,2,1:T(8,128)} fusion(f32[8,24,512,1,1]{2,1,4,3,0:T(8,128)S(1)} %bitcast.95, f32[4,8,100,512,1]{3,2,1,0,4:T(8,128)} %reshape.146), kind=kOutput, calls=%fused_computation.4 | convolution fusion | flops 3774873600 | bytes 9404416 | tf_op jit(solution)/shard_map/dot_general | solution.py:51
  163.9 9.2 %copy.76 = f32[8,8,4,100,24]{4,3,2,1,0:T(8,128)} copy(f32[8,8,4,100,24]{3,4,0,2,1:T(8,128)} %convolution_bitcast_fusion.2) | data formatting | bytes 4915200 | tf_op jit(solution)/shard_map/transpose | solution.py:52
  173.1 9.6 %reshape.129 = f32[8,32,2400]{2,1,0:T(8,128)} reshape(f32[8,8,4,100,24]{4,3,2,1,0:T(8,128)} %copy.76) | data formatting | bytes 4915200 | tf_op jit(solution)/shard_map/reshape | solution.py:53
  188.7 8.9 %fusion.10 = f32[192,3200]{1,0:T(8,128)} fusion(f32[192,512]{1,0:T(8,128)S(1)} %copy-done.1, f32[512,3200]{1,0:T(8,128)} %all-gather.6.cloned.1.call-done), kind=kOutput, calls=%fused_computation.25 | convolution fusion | flops 3774873600 | bytes 9404416 | tf_op jit(solution)/shard_map/dot_general | solution.py:59
  197.6 33.6 %all-gather.4.cloned.1.call-done = f32[512,2400]{1,0:T(8,128)} async-done(((f32[128,2400]{1,0:T(8,128)}), f32[512,2400]{1,0:T(8,128)}) %all-gather.4.cloned.1.call-update) | async-done | bytes 4915216 | tf_op jit(solution)/shard_map/all_gather | solution.py:48
  231.1 7.5 %convolution_bitcast_fusion = f32[192,2400]{1,0:T(8,128)} fusion(f32[512,2400]{1,0:T(8,128)} %all-gather.4.cloned.1.call-done, f32[192,512]{1,0:T(8,128)S(1)} %bitcast.96), kind=kOutput, calls=%fused_computation | convolution fusion | flops 2831155200 | bytes 7151616 | tf_op jit(solution)/shard_map/dot_general | solution.py:51
  242.3 7.2 %copy.78 = f32[8,24,3,8,100]{1,4,2,0,3:T(8,128)} copy(f32[8,24,3,8,100]{4,3,2,1,0:T(8,128)} %reshape.132) | data formatting | bytes 3686400 | tf_op jit(solution)/shard_map/reshape | solution.py:52
  249.5 7.6 %reshape.133 = f32[8,24,2400]{2,1,0:T(8,128)} reshape(f32[8,8,3,100,24]{4,3,2,1,0:T(8,128)} %bitcast.85) | data formatting | bytes 3686400 | tf_op jit(solution)/shard_map/reshape | solution.py:53
  257.1 4.6 %all-to-all-start.2 = ((f32[8,24,2400]{2,1,0:T(8,128)}), f32[8,24,2400]{2,1,0:T(8,128)}, u32[]{:S(2)}, u32[]{:S(2)}) async-start(f32[8,24,2400]{2,1,0:T(8,128)} %reshape.133), calls=%async_computation.2 | async-start | bytes 3735552 | tf_op jit(solution)/shard_map/all_to_all | solution.py:54
  261.6 5.8 %copy.79 = f32[512,2400]{1,0:T(8,128)} copy(f32[512,2400]{0,1:T(8,128)} %bitcast.93) | data formatting | bytes 9830400 | tf_op jit(solution)/shard_map/dot_general | solution.py:35
  269.2 18.8 %fusion.4 = f32[4,8,2,8,4,64]{5,4,1,2,0,3:T(4,128)S(1)} fusion(f32[8,64,2400,1,1,1]{2,1,0,5,4,3:T(8,128)} %bitcast.87, f32[8,4,2,4,2400,1]{4,3,2,1,0,5:T(4,128)} %reshape.147), kind=kOutput, calls=%fused_computation.7 | convolution fusion | flops 3774873600 | bytes 7897088 | tf_op jit(solution)/shard_map/dot_general | solution.py:35
  290.2 4.1 %all-to-all-start.3 = ((f32[32,1,4096]{2,1,0:T(1,128)}), f32[32,1,4096]{2,1,0:T(1,128)}, u32[]{:S(2)}, u32[]{:S(2)}) async-start(f32[32,1,4096]{2,1,0:T(1,128)} %reshape.158), calls=%async_computation.3 | async-start | bytes 1048576 | tf_op jit(solution)/shard_map/all_to_all | solution.py:38
  294.4 7.6 %convolution_bitcast_fusion.1 = f32[192,2400]{1,0:T(8,128)} fusion(f32[512,2400]{1,0:T(8,128)} %all-gather.4.cloned.1.call-done, f32[192,512]{1,0:T(8,128)S(1)} %copy-done.1), kind=kOutput, calls=%fused_computation.1 | convolution fusion | flops 2831155200 | bytes 7151616 | tf_op jit(solution)/shard_map/dot_general | solution.py:59
  310.4 4.3 %all-to-all-start.5 = ((f32[8,8,2400]{2,1,0:T(8,128)}), f32[8,8,2400]{2,1,0:T(8,128)S(1)}, u32[]{:S(2)}, u32[]{:S(2)}) async-start(f32[8,8,2400]{2,1,0:T(8,128)} %reshape.141), calls=%async_computation.5 | async-start | bytes 1245184 | tf_op jit(solution)/shard_map/all_to_all | solution.py:54
  315.4 3.9 %dot_general.68 = f32[8,4,2,3,2400]{4,3,2,1,0:T(4,128)} reshape(f32[192,2400]{1,0:T(8,128)} %bitcast.14) | data formatting | bytes 3686400 | tf_op jit(solution)/shard_map/dot_general | solution.py:35
  319.3 11.0 %fusion.7 = f32[4,8,2,8,3,64]{5,3,1,4,2,0:T(8,128)S(1)} fusion(f32[8,64,2400,1,1,1]{2,1,0,5,4,3:T(8,128)} %bitcast.88, f32[8,4,2,3,2400,1]{4,3,2,1,0,5:T(4,128)} %bitcast.99), kind=kOutput, calls=%fused_computation.8 | convolution fusion | flops 2831155200 | bytes 7151616 | tf_op jit(solution)/shard_map/dot_general | solution.py:35
  332.1 6.1 %all-to-all-start.4 = ((f32[32,1,3072]{2,1,0:T(1,128)}), f32[32,1,3072]{2,1,0:T(1,128)S(1)}, u32[]{:S(2)}, u32[]{:S(2)}) async-start(f32[32,1,3072]{2,1,0:T(1,128)} %reshape.156), calls=%async_computation.4 | async-start | bytes 786432 | tf_op jit(solution)/shard_map/all_to_all | solution.py:38
  343.4 9.6 %convolution_bitcast_fusion.5 = f32[4,8,2,8,1,64]{5,3,1,2,0,4:T(8,128)S(1)} fusion(f32[8,4,2,2400,1]{3,0,4,2,1:T(8,128)S(1)} %bitcast.100, f32[8,64,2400,1,1]{2,1,0,4,3:T(8,128)} %bitcast.89), kind=kOutput, calls=%fused_computation.11 | convolution fusion | flops 943718400 | bytes 5660672 | tf_op jit(solution)/shard_map/dot_general | solution.py:35
  354.6 6.2 %all-to-all-start.6 = ((f32[32,1,1024]{2,1,0:T(1,128)}), f32[32,1,1024]{2,1,0:T(1,128)}, u32[]{:S(2)}, u32[]{:S(2)}) async-start(f32[32,1,1024]{2,1,0:T(1,128)} %reshape.154), calls=%async_computation.6 | async-start | bytes 262144 | tf_op jit(solution)/shard_map/all_to_all | solution.py:38
  363.9 4.9 %concatenate.6 = f32[192,6400]{1,0:T(8,128)} concatenate(f32[192,3200]{1,0:T(8,128)S(1)} %copy-done, f32[192,2400]{1,0:T(8,128)} %convolution_bitcast_fusion.1, f32[192,800]{1,0:T(8,128)S(1)} %convolution_bitcast_fusion.4), dimensions={1} | concatenate | bytes 9830400 | tf_op jit(solution)/shard_map/concatenate | solution.py:63
  (72 shorter events, 44.6 us)
Async XLA Ops:
  7.2 129.5 %all-gather.6.cloned.1.call-start = ((), (), s32[]{:S(2)}) async-start(), calls=%async_computation.8 | async-start | bytes 8192000 | tf_op jit(solution)/shard_map/all_gather | solution.py:48
  9.9 2.6 copy-start.1
  9.9 221.2 %all-gather.4.cloned.1.call-start = ((), (), s32[]{:S(2)}) async-start(), calls=%async_computation.7 | async-start | bytes 6225920 | tf_op jit(solution)/shard_map/all_gather | solution.py:48
  182.7 48.5 %all-to-all-start.1 = ((f32[8,32,2400]{2,1,0:T(8,128)}), f32[8,32,2400]{2,1,0:T(8,128)S(1)}, u32[]{:S(2)}, u32[]{:S(2)}) async-start(f32[8,32,2400]{2,1,0:T(8,128)} %reshape.129), calls=%async_computation.1 | async-start | bytes 4980736 | tf_op jit(solution)/shard_map/all_to_all | solution.py:54
  186.4 115.5 %all-gather.8.cloned.1.call-start = ((), (), s32[]{:S(2)}) async-start(), calls=%async_computation.9 | async-start | bytes 2293760 | tf_op jit(solution)/shard_map/all_gather | solution.py:48
  257.1 33.2 %all-to-all-start.2 = ((f32[8,24,2400]{2,1,0:T(8,128)}), f32[8,24,2400]{2,1,0:T(8,128)}, u32[]{:S(2)}, u32[]{:S(2)}) async-start(f32[8,24,2400]{2,1,0:T(8,128)} %reshape.133), calls=%async_computation.2 | async-start | bytes 3735552 | tf_op jit(solution)/shard_map/all_to_all | solution.py:54
  290.2 20.1 %all-to-all-start.3 = ((f32[32,1,4096]{2,1,0:T(1,128)}), f32[32,1,4096]{2,1,0:T(1,128)}, u32[]{:S(2)}, u32[]{:S(2)}) async-start(f32[32,1,4096]{2,1,0:T(1,128)} %reshape.158), calls=%async_computation.3 | async-start | bytes 1048576 | tf_op jit(solution)/shard_map/all_to_all | solution.py:38
  308.5 6.8 %copy-start.6 = (s32[96]{0:T(128)S(1)}, s32[96]{0:T(128)}, u32[]{:S(2)}) copy-start(s32[96]{0:T(128)} %param.8) | copy-start | bytes 1156
  310.4 21.8 %all-to-all-start.5 = ((f32[8,8,2400]{2,1,0:T(8,128)}), f32[8,8,2400]{2,1,0:T(8,128)S(1)}, u32[]{:S(2)}, u32[]{:S(2)}) async-start(f32[8,8,2400]{2,1,0:T(8,128)} %reshape.141), calls=%async_computation.5 | async-start | bytes 1245184 | tf_op jit(solution)/shard_map/all_to_all | solution.py:54
  332.1 21.7 %all-to-all-start.4 = ((f32[32,1,3072]{2,1,0:T(1,128)}), f32[32,1,3072]{2,1,0:T(1,128)S(1)}, u32[]{:S(2)}, u32[]{:S(2)}) async-start(f32[32,1,3072]{2,1,0:T(1,128)} %reshape.156), calls=%async_computation.4 | async-start | bytes 786432 | tf_op jit(solution)/shard_map/all_to_all | solution.py:38
  343.4 17.5 %copy-start.2 = (f32[192,512]{1,0:T(8,128)S(1)}, f32[192,512]{1,0:T(8,128)}, u32[]{:S(2)}) copy-start(f32[192,512]{1,0:T(8,128)} %param.5) | copy-start | bytes 1179652
  353.0 10.9 %copy-start = (f32[192,3200]{1,0:T(8,128)S(1)}, f32[192,3200]{1,0:T(8,128)}, u32[]{:S(2)}) copy-start(f32[192,3200]{1,0:T(8,128)} %fusion.10) | copy-start | bytes 7372804
  353.9 0.8 copy-start.3
  354.6 16.0 %all-to-all-start.6 = ((f32[32,1,1024]{2,1,0:T(1,128)}), f32[32,1,1024]{2,1,0:T(1,128)}, u32[]{:S(2)}, u32[]{:S(2)}) async-start(f32[32,1,1024]{2,1,0:T(1,128)} %reshape.154), calls=%async_computation.6 | async-start | bytes 262144 | tf_op jit(solution)/shard_map/all_to_all | solution.py:38
  363.9 4.9 %copy-start.4 = (f32[32,1,3072]{2,1,0:T(1,128)S(1)}, f32[32,1,3072]{2,1,0:T(1,128)}, u32[]{:S(2)}) copy-start(f32[32,1,3072]{2,1,0:T(1,128)} %copy-done.3) | copy-start | bytes 1179652
  368.9 3.7 copy-start.5
Sparse Core Ops, SparseCore 0:
  10.1 126.5 all-gather.5
  138.3 92.8 all-gather.3
  232.7 39.7 all-gather.7

commit v9 on v7

--- a/solution.py
+++ b/solution.py
@@ -3,7 +3,7 @@
 from jax import lax
 from jax.sharding import PartitionSpec as P
 
-HIGHEST = lax.Precision.HIGHEST
+PRECISION = lax.Precision.HIGH
 
 
 def per_device(amplitudes, slab_integrals, cycle_integrals, occ_irrep, vir_irrep, n_amp, n_int):
@@ -42,15 +42,15 @@
                 (v_all, ladder_chunks[-1], cycle_chunks[-1])
             )
         ladder_chunks.append(
-            jnp.dot(amplitudes, v_all, precision=HIGHEST, preferred_element_type=jnp.float32)
+            jnp.dot(amplitudes, v_all, precision=PRECISION, preferred_element_type=jnp.float32)
         )
-        l_cyc = jnp.dot(t_cyc, v_all, precision=HIGHEST, preferred_element_type=jnp.float32)
+        l_cyc = jnp.dot(t_cyc, v_all, precision=PRECISION, preferred_element_type=jnp.float32)
         l_cyc = l_cyc.reshape(ibat, k_local, a_chunk, n_amp, c_local).transpose(3, 0, 2, 4, 1)
         l_cyc = l_cyc.reshape(n_amp, ibat * a_chunk, c_local * k_local)
         moved = lax.all_to_all(l_cyc, "amp", split_axis=0, concat_axis=0, tiled=True)
         moved = moved.reshape(n_amp * ibat * a_chunk, c_local * k_local)
         cycle_chunks.append(
-            jnp.dot(moved, w2, precision=HIGHEST, preferred_element_type=jnp.float32)
+            jnp.dot(moved, w2, precision=PRECISION, preferred_element_type=jnp.float32)
         )
     ladder = jnp.concatenate(ladder_chunks, axis=1)
 

time: 368 us -> 357 us (0.970); the launches traced: 361 us -> 355 us
  matrix products: 61.2 us -> 44.3 us
  waiting for transfers between devices: 166 us -> 177 us
    dot_general x9, matrix products: 61.2 us -> 44.3 us  [the longest x3 14.9 us: per_device(): jnp.dot(t_cyc, v_all, precision=PRECISION, preferred_element_type=jnp.flo...]
    all_gather x3, waiting for transfers between devices: 104 us -> 111 us  [per_device(): v_all = lax.all_gather(v, 'int', axis=0, tiled=True)]
    all_to_all x3, waiting for transfers between devices: 44.7 us -> 48.7 us  [per_device(): lax.all_to_all(l_cyc, 'amp', split_axis=0, concat_axis=0, tiled=True)]
  transfers between devices with their start and end apart: 7 -> 7, of which waited for: 6 -> 6; matrix products, arithmetic and copies ran while one was open for 32% -> 29% of each run, Pallas kernels for 0% -> 0%
where the time goes in v9:
time: 357 us; the launch traced here: 355 us
  waiting for transfers between devices  177 us (50%)
  local copies, waits for them, and re-layouts  76.7 us (21%)
  matrix products  44.3 us (12%)
  blocking collectives  25.5 us (7%)
  starting transfers between devices  14.7 us (4%)
  between operations  13.9 us (4%)
    all_gather x3, waiting for transfers between devices, per_device(): v_all = lax.all_gather(v, 'int', axis=0, tiled=True)  111 us
    all_to_all x3, waiting for transfers between devices, per_device(): lax.all_to_all(l_cyc, 'amp', split_axis=0, concat_axis=0, tiled=True)  48.7 us
    all_to_all x1, blocking collectives, per_device(): lax.all_to_all(amplitudes.reshape(i_local, nocc, pw), 'int', split_axis=1...  25.5 us
    reshape x3, local copies, waits for them, and re-layouts, per_device(): l_cyc = l_cyc.reshape(n_amp, ibat * a_chunk, c_local * k_local)  18.8 us
    all_to_all x1, waiting for transfers between devices, per_device(): lax.all_to_all(parts, ('int', 'amp'), split_axis=0, concat_axis=0, tiled=...  17.7 us
    dot_general x2, local copies, waits for them, and re-layouts, per_device(): jnp.dot(t_cyc, v_all, precision=PRECISION, preferred_element_type=jnp.flo...  15.9 us
    dot_general x3, matrix products, per_device(): jnp.dot(t_cyc, v_all, precision=PRECISION, preferred_element_type=jnp.flo...  14.9 us
    dot_general x3, matrix products, per_device(): jnp.dot(moved, w2, precision=PRECISION, preferred_element_type=jnp.float32)  14.8 us
  transfers between devices with their start and end apart: 7, of which 6 were waited for; matrix products, arithmetic and copies ran while one was open for 29% of the time, Pallas kernels for 0%

profile of v9, /device:TPU:0, one launch (start us, length us, event | category | flops | bytes accessed | tf_op | source)
XLA Modules:
  0.0 354.8 jit_solution(15242090613368226702)
XLA Ops:
  12.8 25.5 %all_to_all.35 = f32[2,96,512]{2,0,1:T(2,128)S(1)} all-to-all(f32[2,96,512]{2,0,1:T(2,128)S(1)} %copy.52), channel_id=1, replica_groups=mesh['amp'=8,'int'=4] {'int'}, dimensions={1} | all-to-all | bytes 786432 | tf_op jit(solution)/shard_map/all_to_all | solution.py:29
  38.4 98.3 %all-gather.6.cloned.1.call-done = f32[512,3200]{1,0:T(8,128)} async-done(((f32[128,3200]{1,0:T(8,128)}), f32[512,3200]{1,0:T(8,128)}) %all-gather.6.cloned.1.call-update) | async-done | bytes 6553616 | tf_op jit(solution)/shard_map/all_gather | solution.py:39
  136.7 8.2 %copy.55 = f32[3200,512]{1,0:T(8,128)} copy(f32[3200,512]{0,1:T(8,128)} %bitcast.62) | data formatting | bytes 13107200 | tf_op jit(solution)/shard_map/dot_general | solution.py:47
  144.9 7.7 %reshape.128 = f32[4,8,100,512,1]{3,2,1,0,4:T(8,128)} reshape(f32[3200,512]{1,0:T(8,128)} %copy.55) | data formatting | bytes 13107200 | tf_op jit(solution)/shard_map/dot_general | solution.py:47
  152.6 7.2 %convolution_bitcast_fusion.2 = f32[8,8,4,100,24]{3,4,0,2,1:T(8,128)} fusion(f32[8,24,512,1,1]{2,1,4,3,0:T(8,128)S(1)} %bitcast.69, f32[4,8,100,512,1]{3,2,1,0,4:T(8,128)} %reshape.128), kind=kOutput, calls=%fused_computation.2 | convolution fusion | flops 1887436800 | bytes 9404416 | tf_op jit(solution)/shard_map/dot_general | solution.py:47
  159.8 9.3 %copy.56 = f32[8,8,4,100,24]{4,3,2,1,0:T(8,128)} copy(f32[8,8,4,100,24]{3,4,0,2,1:T(8,128)} %convolution_bitcast_fusion.2) | data formatting | bytes 4915200 | tf_op jit(solution)/shard_map/transpose | solution.py:48
  169.1 9.5 %reshape.114 = f32[8,32,2400]{2,1,0:T(8,128)} reshape(f32[8,8,4,100,24]{4,3,2,1,0:T(8,128)} %copy.56) | data formatting | bytes 4915200 | tf_op jit(solution)/shard_map/reshape | solution.py:49
  178.6 3.7 %all-to-all-start.1 = ((f32[8,32,2400]{2,1,0:T(8,128)}), f32[8,32,2400]{2,1,0:T(8,128)S(1)}, u32[]{:S(2)}, u32[]{:S(2)}) async-start(f32[8,32,2400]{2,1,0:T(8,128)} %reshape.114), calls=%async_computation.1 | async-start | bytes 4980736 | tf_op jit(solution)/shard_map/all_to_all | solution.py:50
  184.5 6.8 %fusion = f32[192,3200]{1,0:T(8,128)} fusion(f32[192,512]{1,0:T(8,128)S(1)} %copy-done.1, f32[512,3200]{1,0:T(8,128)} %all-gather.6.cloned.1.call-done), kind=kOutput, calls=%fused_computation.19 | convolution fusion | flops 1887436800 | bytes 9404416 | tf_op jit(solution)/shard_map/dot_general | solution.py:45
  191.4 21.8 %all-to-all-done.1 = f32[8,32,2400]{2,1,0:T(8,128)S(1)} async-done(((f32[8,32,2400]{2,1,0:T(8,128)}), f32[8,32,2400]{2,1,0:T(8,128)S(1)}, u32[]{:S(2)}, u32[]{:S(2)}) %all-to-all-start.1) | async-done | bytes 2457632 | tf_op jit(solution)/shard_map/all_to_all | solution.py:50
  213.2 5.6 %fusion.1 = f32[256,512]{1,0:T(8,128)} fusion(f32[256,2400]{1,0:T(8,128)S(1)} %bitcast.64, f32[2400,512]{1,0:T(8,128)} %bitcast.58), kind=kOutput, calls=%fused_computation.20 | convolution fusion | flops 1887436800 | bytes 7897088 | tf_op jit(solution)/shard_map/dot_general | solution.py:53
  218.8 12.3 %all-gather.4.cloned.1.call-done = f32[512,2400]{1,0:T(8,128)} async-done(((f32[128,2400]{1,0:T(8,128)}), f32[512,2400]{1,0:T(8,128)}) %all-gather.4.cloned.1.call-update) | async-done | bytes 4915216 | tf_op jit(solution)/shard_map/all_gather | solution.py:39
  231.1 5.4 %convolution_bitcast_fusion = f32[192,2400]{1,0:T(8,128)} fusion(f32[512,2400]{1,0:T(8,128)} %all-gather.4.cloned.1.call-done, f32[192,512]{1,0:T(8,128)S(1)} %bitcast.70), kind=kOutput, calls=%fused_computation | convolution fusion | flops 1415577600 | bytes 7151616 | tf_op jit(solution)/shard_map/dot_general | solution.py:47
  239.2 5.6 %copy.58 = f32[8,24,3,8,100]{1,4,2,0,3:T(8,128)} copy(f32[8,24,3,8,100]{4,3,2,1,0:T(8,128)S(1)} %reshape.118) | data formatting | bytes 3686400 | tf_op jit(solution)/shard_map/reshape | solution.py:48
  244.8 7.6 %reshape.119 = f32[8,24,2400]{2,1,0:T(8,128)} reshape(f32[8,8,3,100,24]{4,3,2,1,0:T(8,128)} %bitcast.61) | data formatting | bytes 3686400 | tf_op jit(solution)/shard_map/reshape | solution.py:49
  252.4 3.8 %all-to-all-start.2 = ((f32[8,24,2400]{2,1,0:T(8,128)}), f32[8,24,2400]{2,1,0:T(8,128)S(1)}, u32[]{:S(2)}, u32[]{:S(2)}) async-start(f32[8,24,2400]{2,1,0:T(8,128)} %reshape.119), calls=%async_computation.2 | async-start | bytes 3735552 | tf_op jit(solution)/shard_map/all_to_all | solution.py:50
  256.2 5.5 %convolution_bitcast_fusion.1 = f32[192,2400]{1,0:T(8,128)} fusion(f32[512,2400]{1,0:T(8,128)} %all-gather.4.cloned.1.call-done, f32[192,512]{1,0:T(8,128)S(1)} %copy-done.1), kind=kOutput, calls=%fused_computation.1 | convolution fusion | flops 1415577600 | bytes 7151616 | tf_op jit(solution)/shard_map/dot_general | solution.py:45
  261.7 18.5 %all-to-all-done.2 = f32[8,24,2400]{2,1,0:T(8,128)S(1)} async-done(((f32[8,24,2400]{2,1,0:T(8,128)}), f32[8,24,2400]{2,1,0:T(8,128)S(1)}, u32[]{:S(2)}, u32[]{:S(2)}) %all-to-all-start.2) | async-done | bytes 1843232 | tf_op jit(solution)/shard_map/all_to_all | solution.py:50
  280.2 5.1 %fusion.2 = f32[192,512]{1,0:T(8,128)} fusion(f32[192,2400]{1,0:T(8,128)S(1)} %bitcast.66, f32[2400,512]{1,0:T(8,128)} %bitcast.59), kind=kOutput, calls=%fused_computation.21 | convolution fusion | flops 1415577600 | bytes 7151616 | tf_op jit(solution)/shard_map/dot_general | solution.py:53
  292.9 3.5 all-to-all-start.3
  298.8 8.4 %all-to-all-done.3 = f32[8,8,2400]{2,1,0:T(8,128)S(1)} async-done(((f32[8,8,2400]{2,1,0:T(8,128)}), f32[8,8,2400]{2,1,0:T(8,128)S(1)}, u32[]{:S(2)}, u32[]{:S(2)}) %all-to-all-start.3) | async-done | bytes 614432 | tf_op jit(solution)/shard_map/all_to_all | solution.py:50
  307.1 4.0 %convolution_bitcast_fusion.5 = f32[8,8,1,512]{3,1,0,2:T(8,128)S(1)} fusion(f32[8,8,2400]{2,1,0:T(8,128)S(1)} %all-to-all-done.3, f32[2400,512,1]{1,0,2:T(8,128)} %bitcast.60), kind=kOutput, calls=%fused_computation.5 | convolution fusion | flops 471859200 | bytes 5660672 | tf_op jit(solution)/shard_map/dot_general | solution.py:53
  323.8 4.9 %concatenate.6 = f32[192,6400]{1,0:T(8,128)} concatenate(f32[192,3200]{1,0:T(8,128)S(1)} %copy-done, f32[192,2400]{1,0:T(8,128)} %convolution_bitcast_fusion.1, f32[192,800]{1,0:T(8,128)S(1)} %convolution_bitcast_fusion.4), dimensions={1} | concatenate | bytes 9830400 | tf_op jit(solution)/shard_map/concatenate | solution.py:55
  328.7 17.7 %all-to-all-done.4 = f32[32,128,64]{1,2,0:T(8,128)} async-done(((f32[32,128,64]{1,2,0:T(8,128)}), f32[32,128,64]{1,2,0:T(8,128)}, u32[]{:S(2)}, u32[]{:S(2)}) %all-to-all-start.4) | async-done | bytes 1048608 | tf_op jit(solution)/shard_map/all_to_all | solution.py:63
  (44 shorter events, 34.9 us)
Async XLA Ops:
  7.2 129.5 %all-gather.6.cloned.1.call-start = ((), (), s32[]{:S(2)}) async-start(), calls=%async_computation.6 | async-start | bytes 8192000 | tf_op jit(solution)/shard_map/all_gather | solution.py:39
  9.9 2.5 copy-start.1
  9.9 221.2 %all-gather.4.cloned.1.call-start = ((), (), s32[]{:S(2)}) async-start(), calls=%async_computation.5 | async-start | bytes 6225920 | tf_op jit(solution)/shard_map/all_gather | solution.py:39
  178.6 34.6 %all-to-all-start.1 = ((f32[8,32,2400]{2,1,0:T(8,128)}), f32[8,32,2400]{2,1,0:T(8,128)S(1)}, u32[]{:S(2)}, u32[]{:S(2)}) async-start(f32[8,32,2400]{2,1,0:T(8,128)} %reshape.114), calls=%async_computation.1 | async-start | bytes 4980736 | tf_op jit(solution)/shard_map/all_to_all | solution.py:50
  182.3 103.0 %all-gather.8.cloned.1.call-start = ((), (), s32[]{:S(2)}) async-start(), calls=%async_computation.7 | async-start | bytes 2293760 | tf_op jit(solution)/shard_map/all_gather | solution.py:39
  252.4 27.8 %all-to-all-start.2 = ((f32[8,24,2400]{2,1,0:T(8,128)}), f32[8,24,2400]{2,1,0:T(8,128)S(1)}, u32[]{:S(2)}, u32[]{:S(2)}) async-start(f32[8,24,2400]{2,1,0:T(8,128)} %reshape.119), calls=%async_computation.2 | async-start | bytes 3735552 | tf_op jit(solution)/shard_map/all_to_all | solution.py:50
  292.9 14.3 %all-to-all-start.3 = ((f32[8,8,2400]{2,1,0:T(8,128)}), f32[8,8,2400]{2,1,0:T(8,128)S(1)}, u32[]{:S(2)}, u32[]{:S(2)}) async-start(f32[8,8,2400]{2,1,0:T(8,128)} %reshape.124), calls=%async_computation.3 | async-start | bytes 1245184 | tf_op jit(solution)/shard_map/all_to_all | solution.py:50
  313.4 7.4 %copy-start.3 = (s32[96]{0:T(128)S(1)}, s32[96]{0:T(128)}, u32[]{:S(2)}) copy-start(s32[96]{0:T(128)} %param.8) | copy-start | bytes 1156
  313.4 8.0 %copy-start.2 = (f32[192,512]{1,0:T(8,128)S(1)}, f32[192,512]{1,0:T(8,128)}, u32[]{:S(2)}) copy-start(f32[192,512]{1,0:T(8,128)} %param.5) | copy-start | bytes 1179652
  313.4 10.4 %copy-start = (f32[192,3200]{1,0:T(8,128)S(1)}, f32[192,3200]{1,0:T(8,128)}, u32[]{:S(2)}) copy-start(f32[192,3200]{1,0:T(8,128)} %fusion) | copy-start | bytes 7372804
  316.8 29.6 %all-to-all-start.4 = ((f32[32,128,64]{1,2,0:T(8,128)}), f32[32,128,64]{1,2,0:T(8,128)}, u32[]{:S(2)}, u32[]{:S(2)}) async-start(f32[32,128,64]{1,2,0:T(8,128)} %bitcast.68), calls=%async_computation.4 | async-start | bytes 2097152 | tf_op jit(solution)/shard_map/all_to_all | solution.py:63
Sparse Core Ops, SparseCore 0:
  10.1 126.4 all-gather.5
  138.3 92.8 all-gather.3
  232.7 39.7 all-gather.7

commit v10 on v5

--- a/solution.py
+++ b/solution.py
@@ -3,7 +3,7 @@
 from jax import lax
 from jax.sharding import PartitionSpec as P
 
-HIGHEST = lax.Precision.HIGHEST
+PRECISION = lax.Precision.HIGH
 
 
 def per_device(amplitudes, slab_integrals, cycle_integrals, occ_irrep, vir_irrep, n_amp, n_int):
@@ -31,42 +31,54 @@
     ).reshape(ibat * k_local, pw)
     w2 = cycle_integrals.transpose(1, 0, 2).reshape(c_local * k_local, columns)
 
-    slab3 = slab_integrals.reshape(pw_local, a_local, nvir)
+    col_local = columns // n_amp
+
+    def reduce_block(part, a_chunk):
+        part = part.reshape(n_amp, n_int, i_local, a_chunk, n_amp, col_local)
+        part = part.transpose(1, 4, 2, 0, 3, 5).reshape(n_int * n_amp, i_local * n_amp * a_chunk, col_local)
+        got = lax.all_to_all(part, ("int", "amp"), split_axis=0, concat_axis=0, tiled=True)
+        return jnp.sum(got, axis=0).reshape(i_local, n_amp, a_chunk, col_local)
+
     ladder_chunks = []
     cycle_chunks = []
+    reduced = []
     for t in range(chunks):
         a_chunk = sizes[t]
-        v = slab3[:, starts[t]:starts[t] + a_chunk, :].reshape(pw_local, a_chunk * nvir)
+        v = lax.slice_in_dim(slab_integrals, starts[t] * nvir, (starts[t] + a_chunk) * nvir, axis=1)
         v_all = lax.all_gather(v, "int", axis=0, tiled=True)
-        if t:
+        if t == 1:
+            v_all, ladder_chunks[-1], reduced[0] = lax.optimization_barrier(
+                (v_all, ladder_chunks[-1], reduced[0])
+            )
+        elif t:
             v_all, ladder_chunks[-1], cycle_chunks[-1] = lax.optimization_barrier(
                 (v_all, ladder_chunks[-1], cycle_chunks[-1])
             )
         ladder_chunks.append(None)
         if t < chunks - 1:
             ladder_chunks[-1] = jnp.dot(
-                amplitudes, v_all, precision=HIGHEST, preferred_element_type=jnp.float32
+                amplitudes, v_all, precision=PRECISION, preferred_element_type=jnp.float32
             )
-        l_cyc = jnp.dot(t_cyc, v_all, precision=HIGHEST, preferred_element_type=jnp.float32)
+        l_cyc = jnp.dot(t_cyc, v_all, precision=PRECISION, preferred_element_type=jnp.float32)
         l_cyc = l_cyc.reshape(ibat, k_local, a_chunk, n_amp, c_local).transpose(3, 0, 2, 4, 1)
         l_cyc = l_cyc.reshape(n_amp, ibat * a_chunk, c_local * k_local)
         moved = lax.all_to_all(l_cyc, "amp", split_axis=0, concat_axis=0, tiled=True)
         if t == chunks - 1:
             ladder_chunks[-1] = jnp.dot(
-                amplitudes, v_all, precision=HIGHEST, preferred_element_type=jnp.float32
+                amplitudes, v_all, precision=PRECISION, preferred_element_type=jnp.float32
             )
             ladder = jnp.concatenate(ladder_chunks, axis=1)
             moved, ladder = lax.optimization_barrier((moved, ladder))
         moved = moved.reshape(n_amp * ibat * a_chunk, c_local * k_local)
-        partial_sums = jnp.dot(moved, w2, precision=HIGHEST, preferred_element_type=jnp.float32)
-        cycle_chunks.append(lax.psum_scatter(partial_sums, "amp", scatter_dimension=1, tiled=True))
+        part = jnp.dot(moved, w2, precision=PRECISION, preferred_element_type=jnp.float32)
+        if t == 0 and chunks > 1:
+            reduced.append(reduce_block(part, a_chunk))
+        else:
+            cycle_chunks.append(part.reshape(n_amp, ibat, a_chunk, columns))
+    rest = jnp.concatenate(cycle_chunks, axis=2)
+    reduced.append(reduce_block(rest, rest.shape[2]))
 
-    col_local = columns // n_amp
-    parts = jnp.concatenate(
-        [c.reshape(n_amp, ibat, sizes[t], col_local) for t, c in enumerate(cycle_chunks)], axis=2
-    )
-    parts = parts.transpose(1, 0, 2, 3).reshape(ibat * slab, col_local)
-    sums = lax.psum_scatter(parts, "int", scatter_dimension=0, tiled=True)
+    sums = jnp.concatenate(reduced, axis=2).reshape(i_local * slab, col_local)
 
     row_start = lax.axis_index("int") * i_local
     batch_labels = lax.dynamic_slice_in_dim(occ_irrep, row_start, i_local, 0)

time: 470 us -> 362 us (0.77)
  blocking collectives: 100 us -> 25.5 us
  matrix products: 80.5 us -> 46.2 us
  waiting for transfers between devices: 199 us -> 166 us
  local copies, waits for them, and re-layouts: 63.4 us -> 86.7 us
  starting transfers between devices: 4.8 us -> 17.7 us
    reduce_scatter x3 -> x0, waiting for transfers between devices: 77.6 us -> none  [the longest x2 57.8 us: per_device(): lax.psum_scatter(partial_sums, 'amp', scatter_dimension=1, tiled=True)]
    all_to_all x2 -> x0, blocking collectives: 61.7 us -> none  [per_device(): lax.all_to_all(l_cyc, 'amp', split_axis=0, concat_axis=0, tiled=True)]
    all_to_all x1 -> x3, waiting for transfers between devices: 1.65 us -> 44.6 us  [per_device(): lax.all_to_all(l_cyc, 'amp', split_axis=0, concat_axis=0, tiled=True)]
    unnamed x8 -> x3, waiting for transfers between devices: 33.2 us -> 0.05 us
    dot_general x8 -> x9, matrix products: 69.3 us -> 46.2 us  [the longest x3 15.9 us: per_device(): jnp.dot(moved, w2, precision=PRECISION, preferred_element_type=jnp.float32)]
    all_to_all x0 -> x2, waiting for transfers between devices: none -> 22.7 us  [reduce_block(): lax.all_to_all(part, ('int', 'amp'), split_axis=0, concat_axis=0, tiled=T...]
    dot_general x1 -> x5, local copies, waits for them, and re-layouts: 7.47 us -> 23 us  [the longest x2 15.9 us: per_device(): jnp.dot(t_cyc, v_all, precision=PRECISION, preferred_element_type=jnp.flo...]
    all_to_all x1, blocking collectives: 38.6 us -> 25.5 us  [per_device(): lax.all_to_all(amplitudes.reshape(i_local, nocc, pw), 'int', split_axis=1...]
  transfers between devices with their start and end apart: 8 -> 8, of which waited for: 6 -> 6; matrix products, arithmetic and copies ran while one was open for 25% -> 31% of each run, Pallas kernels for 0% -> 0%
where the time goes in v10:
time: 362 us; the launch traced here: 360 us
  waiting for transfers between devices  166 us (46%)
  local copies, waits for them, and re-layouts  86.7 us (24%)
  matrix products  46.2 us (13%)
  blocking collectives  25.5 us (7%)
  starting transfers between devices  17.7 us (5%)
  between operations  14 us (4%)
  other arithmetic  4.65 us (1%)
    all_gather x3, waiting for transfers between devices, per_device(): v_all = lax.all_gather(v, 'int', axis=0, tiled=True)  98.3 us
    all_to_all x3, waiting for transfers between devices, per_device(): lax.all_to_all(l_cyc, 'amp', split_axis=0, concat_axis=0, tiled=True)  44.6 us
    all_to_all x1, blocking collectives, per_device(): lax.all_to_all(amplitudes.reshape(i_local, nocc, pw), 'int', split_axis=1...  25.5 us
    all_to_all x2, waiting for transfers between devices, reduce_block(): lax.all_to_all(part, ('int', 'amp'), split_axis=0, concat_axis=0, tiled=T...  22.7 us
    reshape x3, local copies, waits for them, and re-layouts, per_device(): l_cyc = l_cyc.reshape(n_amp, ibat * a_chunk, c_local * k_local)  18.8 us
    dot_general x2, local copies, waits for them, and re-layouts, per_device(): jnp.dot(t_cyc, v_all, precision=PRECISION, preferred_element_type=jnp.flo...  15.9 us
    dot_general x3, matrix products, per_device(): jnp.dot(moved, w2, precision=PRECISION, preferred_element_type=jnp.float32)  15.9 us
    dot_general x3, matrix products, per_device(): jnp.dot(amplitudes, v_all, precision=PRECISION, preferred_element_type=jn...  15.4 us
  transfers between devices with their start and end apart: 8, of which 6 were waited for; matrix products, arithmetic and copies ran while one was open for 31% of the time, Pallas kernels for 0%

profile of v10, /device:TPU:0, one launch (start us, length us, event | category | flops | bytes accessed | tf_op | source)
XLA Modules:
  0.0 360.4 jit_solution(229527415505324260)
XLA Ops:
  12.8 25.5 %all_to_all.40 = f32[2,96,512]{2,0,1:T(2,128)S(1)} all-to-all(f32[2,96,512]{2,0,1:T(2,128)S(1)} %copy.73), channel_id=1, replica_groups=mesh['amp'=8,'int'=4] {'int'}, dimensions={1} | all-to-all | bytes 786432 | tf_op jit(solution)/shard_map/all_to_all | solution.py:29
  38.4 98.3 %all-gather.8.cloned.1.call-done = f32[512,3200]{1,0:T(8,128)} async-done(((f32[128,3200]{1,0:T(8,128)}), f32[512,3200]{1,0:T(8,128)}) %all-gather.8.cloned.1.call-update) | async-done | bytes 6553616 | tf_op jit(solution)/shard_map/all_gather | solution.py:48
  136.7 8.2 %copy.76 = f32[3200,512]{1,0:T(8,128)} copy(f32[3200,512]{0,1:T(8,128)} %bitcast.89) | data formatting | bytes 13107200 | tf_op jit(solution)/shard_map/dot_general | solution.py:62
  144.9 7.7 %reshape.142 = f32[4,8,100,512,1]{3,2,1,0,4:T(8,128)} reshape(f32[3200,512]{1,0:T(8,128)} %copy.76) | data formatting | bytes 13107200 | tf_op jit(solution)/shard_map/dot_general | solution.py:62
  152.6 7.1 %convolution_bitcast_fusion.2 = f32[8,8,4,100,24]{3,4,0,2,1:T(8,128)} fusion(f32[8,24,512,1,1]{2,1,4,3,0:T(8,128)S(1)} %bitcast.98, f32[4,8,100,512,1]{3,2,1,0,4:T(8,128)} %reshape.142), kind=kOutput, calls=%fused_computation.2 | convolution fusion | flops 1887436800 | bytes 9404416 | tf_op jit(solution)/shard_map/dot_general | solution.py:62
  159.8 9.3 %copy.77 = f32[8,8,4,100,24]{4,3,2,1,0:T(8,128)} copy(f32[8,8,4,100,24]{3,4,0,2,1:T(8,128)} %convolution_bitcast_fusion.2) | data formatting | bytes 4915200 | tf_op jit(solution)/shard_map/transpose | solution.py:63
  169.0 9.5 %reshape.129 = f32[8,32,2400]{2,1,0:T(8,128)} reshape(f32[8,8,4,100,24]{4,3,2,1,0:T(8,128)} %copy.77) | data formatting | bytes 4915200 | tf_op jit(solution)/shard_map/reshape | solution.py:64
  178.6 3.8 %all-to-all-start.1 = ((f32[8,32,2400]{2,1,0:T(8,128)}), f32[8,32,2400]{2,1,0:T(8,128)S(1)}, u32[]{:S(2)}, u32[]{:S(2)}) async-start(f32[8,32,2400]{2,1,0:T(8,128)} %reshape.129), calls=%async_computation.1 | async-start | bytes 4980736 | tf_op jit(solution)/shard_map/all_to_all | solution.py:65
  182.4 5.8 %copy.79 = f32[512,2400]{1,0:T(8,128)} copy(f32[512,2400]{0,1:T(8,128)} %bitcast.94) | data formatting | bytes 9830400 | tf_op jit(solution)/shard_map/dot_general | solution.py:73
  188.2 24.9 %all-to-all-done.1 = f32[8,32,2400]{2,1,0:T(8,128)S(1)} async-done(((f32[8,32,2400]{2,1,0:T(8,128)}), f32[8,32,2400]{2,1,0:T(8,128)S(1)}, u32[]{:S(2)}, u32[]{:S(2)}) %all-to-all-start.1) | async-done | bytes 2457632 | tf_op jit(solution)/shard_map/all_to_all | solution.py:65
  215.5 4.4 %convolution_bitcast_fusion.3 = f32[4,8,2,8,4,64]{5,3,1,4,2,0:T(8,128)S(1)} fusion(f32[8,4,2,4,2400,1]{4,0,5,3,2,1:T(8,128)S(1)} %bitcast.101, f32[8,64,2400,1,1,1]{2,1,0,5,4,3:T(8,128)S(1)} %bitcast.91), kind=kOutput, calls=%fused_computation.3 | convolution fusion | flops 1887436800 | bytes 7897088 | tf_op jit(solution)/shard_map/dot_general | solution.py:73
  227.1 6.8 %fusion = f32[192,3200]{1,0:T(8,128)} fusion(f32[192,512]{1,0:T(8,128)S(1)} %copy-done.2, f32[512,3200]{1,0:T(8,128)} %all-gather.8.cloned.1.call-done), kind=kOutput, calls=%fused_computation.21 | convolution fusion | flops 1887436800 | bytes 9404416 | tf_op jit(solution)/shard_map/dot_general | solution.py:59
  233.9 8.5 %all-to-all-done.2 = f32[32,1,4096]{2,1,0:T(1,128)S(1)} async-done(((f32[32,1,4096]{2,1,0:T(1,128)}), f32[32,1,4096]{2,1,0:T(1,128)S(1)}, u32[]{:S(2)}, u32[]{:S(2)}) %all-to-all-start.2) | async-done | bytes 524320 | tf_op jit(solution)/shard_map/all_to_all | solution.py:39
  245.3 5.5 %convolution_bitcast_fusion = f32[192,2400]{1,0:T(8,128)} fusion(f32[512,2400]{1,0:T(8,128)} %all-gather.6.cloned.1.call-done, f32[192,512]{1,0:T(8,128)S(1)} %bitcast.99), kind=kOutput, calls=%fused_computation | convolution fusion | flops 1415577600 | bytes 7151616 | tf_op jit(solution)/shard_map/dot_general | solution.py:62
  253.3 5.6 %copy.83 = f32[8,24,3,8,100]{1,4,2,0,3:T(8,128)} copy(f32[8,24,3,8,100]{4,3,2,1,0:T(8,128)S(1)} %reshape.134) | data formatting | bytes 3686400 | tf_op jit(solution)/shard_map/reshape | solution.py:63
  258.9 7.6 %reshape.135 = f32[8,24,2400]{2,1,0:T(8,128)} reshape(f32[8,8,3,100,24]{4,3,2,1,0:T(8,128)} %bitcast.88) | data formatting | bytes 3686400 | tf_op jit(solution)/shard_map/reshape | solution.py:64
  266.5 3.9 %all-to-all-start.3 = ((f32[8,24,2400]{2,1,0:T(8,128)}), f32[8,24,2400]{2,1,0:T(8,128)S(1)}, u32[]{:S(2)}, u32[]{:S(2)}) async-start(f32[8,24,2400]{2,1,0:T(8,128)} %reshape.135), calls=%async_computation.3 | async-start | bytes 3735552 | tf_op jit(solution)/shard_map/all_to_all | solution.py:65
  270.4 5.4 %convolution_bitcast_fusion.1 = f32[192,2400]{1,0:T(8,128)} fusion(f32[512,2400]{1,0:T(8,128)} %all-gather.6.cloned.1.call-done, f32[192,512]{1,0:T(8,128)S(1)} %copy-done.2), kind=kOutput, calls=%fused_computation.1 | convolution fusion | flops 1415577600 | bytes 7151616 | tf_op jit(solution)/shard_map/dot_general | solution.py:59
  275.8 18.4 %all-to-all-done.3 = f32[8,24,2400]{2,1,0:T(8,128)S(1)} async-done(((f32[8,24,2400]{2,1,0:T(8,128)}), f32[8,24,2400]{2,1,0:T(8,128)S(1)}, u32[]{:S(2)}, u32[]{:S(2)}) %all-to-all-start.3) | async-done | bytes 1843232 | tf_op jit(solution)/shard_map/all_to_all | solution.py:65
  294.6 5.2 %fusion.1 = f32[8,8,3,512]{3,0,2,1:T(8,128)} fusion(f32[8,8,3,2400]{3,0,2,1:T(8,128)S(1)} %bitcast.103, f32[2400,512,1,1]{1,0,3,2:T(8,128)} %bitcast.95), kind=kOutput, calls=%fused_computation.22 | convolution fusion | flops 1415577600 | bytes 7151616 | tf_op jit(solution)/shard_map/dot_general | solution.py:73
  307.4 4.3 %all-to-all-start.4 = ((f32[8,8,2400]{2,1,0:T(8,128)}), f32[8,8,2400]{2,1,0:T(8,128)}, u32[]{:S(2)}, u32[]{:S(2)}) async-start(f32[8,8,2400]{2,1,0:T(8,128)} %reshape.137), calls=%async_computation.4 | async-start | bytes 1245184 | tf_op jit(solution)/shard_map/all_to_all | solution.py:65
  316.2 5.2 %concatenate.12 = f32[192,6400]{1,0:T(8,128)} concatenate(f32[192,3200]{1,0:T(8,128)S(1)} %copy-done.1, f32[192,2400]{1,0:T(8,128)} %convolution_bitcast_fusion.1, f32[192,800]{1,0:T(8,128)} %convolution_bitcast_fusion.4), dimensions={1} | concatenate | bytes 9830400 | tf_op jit(solution)/shard_map/concatenate | solution.py:70
  323.8 6.3 %convolution_bitcast_fusion.6 = f32[8,4,2,1,8,64]{5,0,4,2,1,3:T(8,128)S(1)} fusion(f32[8,4,2,2400,1]{3,0,4,2,1:T(8,128)S(1)} %bitcast.102, f32[8,64,2400,1,1]{2,1,0,4,3:T(8,128)} %bitcast.90), kind=kOutput, calls=%fused_computation.6 | convolution fusion | flops 471859200 | bytes 5660672 | tf_op jit(solution)/shard_map/dot_general | solution.py:73
  336.4 14.2 %all-to-all-done.5 = f32[32,1,4096]{2,1,0:T(1,128)S(1)} async-done(((f32[32,1,4096]{2,1,0:T(1,128)}), f32[32,1,4096]{2,1,0:T(1,128)S(1)}, u32[]{:S(2)}, u32[]{:S(2)}) %all-to-all-start.5) | async-done | bytes 524320 | tf_op jit(solution)/shard_map/all_to_all | solution.py:39
  (60 shorter events, 45.0 us)
Async XLA Ops:
  7.2 129.5 %all-gather.8.cloned.1.call-start = ((), (), s32[]{:S(2)}) async-start(), calls=%async_computation.8 | async-start | bytes 8192000 | tf_op jit(solution)/shard_map/all_gather | solution.py:48
  9.9 2.6 copy-start.2
  9.9 235.3 %all-gather.6.cloned.1.call-start = ((), (), s32[]{:S(2)}) async-start(), calls=%async_computation.7 | async-start | bytes 6225920 | tf_op jit(solution)/shard_map/all_gather | solution.py:48
  178.6 34.5 %all-to-all-start.1 = ((f32[8,32,2400]{2,1,0:T(8,128)}), f32[8,32,2400]{2,1,0:T(8,128)S(1)}, u32[]{:S(2)}, u32[]{:S(2)}) async-start(f32[8,32,2400]{2,1,0:T(8,128)} %reshape.129), calls=%async_computation.1 | async-start | bytes 4980736 | tf_op jit(solution)/shard_map/all_to_all | solution.py:65
  213.1 2.4 copy-start
  222.2 20.1 %all-to-all-start.2 = ((f32[32,1,4096]{2,1,0:T(1,128)}), f32[32,1,4096]{2,1,0:T(1,128)S(1)}, u32[]{:S(2)}, u32[]{:S(2)}) async-start(f32[32,1,4096]{2,1,0:T(1,128)} %reshape.149), calls=%async_computation.2 | async-start | bytes 1048576 | tf_op jit(solution)/shard_map/all_to_all | solution.py:39
  224.8 75.0 %all-gather.4.cloned.1.call-start = ((), (), s32[]{:S(2)}) async-start(), calls=%async_computation.6 | async-start | bytes 2293760 | tf_op jit(solution)/shard_map/all_gather | solution.py:48
  266.5 27.7 %all-to-all-start.3 = ((f32[8,24,2400]{2,1,0:T(8,128)}), f32[8,24,2400]{2,1,0:T(8,128)S(1)}, u32[]{:S(2)}, u32[]{:S(2)}) async-start(f32[8,24,2400]{2,1,0:T(8,128)} %reshape.135), calls=%async_computation.3 | async-start | bytes 3735552 | tf_op jit(solution)/shard_map/all_to_all | solution.py:65
  307.4 8.8 %copy-start.1 = (f32[192,3200]{1,0:T(8,128)S(1)}, f32[192,3200]{1,0:T(8,128)}, u32[]{:S(2)}) copy-start(f32[192,3200]{1,0:T(8,128)} %fusion) | copy-start | bytes 7372804
  307.4 15.2 %all-to-all-start.4 = ((f32[8,8,2400]{2,1,0:T(8,128)}), f32[8,8,2400]{2,1,0:T(8,128)}, u32[]{:S(2)}, u32[]{:S(2)}) async-start(f32[8,8,2400]{2,1,0:T(8,128)} %reshape.137), calls=%async_computation.4 | async-start | bytes 1245184 | tf_op jit(solution)/shard_map/all_to_all | solution.py:65
  330.1 5.7 %copy-start.3 = (s32[96]{0:T(128)S(1)}, s32[96]{0:T(128)}, u32[]{:S(2)}) copy-start(s32[96]{0:T(128)} %param.8) | copy-start | bytes 1156
  332.3 18.3 %all-to-all-start.5 = ((f32[32,1,4096]{2,1,0:T(1,128)}), f32[32,1,4096]{2,1,0:T(1,128)S(1)}, u32[]{:S(2)}, u32[]{:S(2)}) async-start(f32[32,1,4096]{2,1,0:T(1,128)} %reshape.151), calls=%async_computation.5 | async-start | bytes 1048576 | tf_op jit(solution)/shard_map/all_to_all | solution.py:39
Sparse Core Ops, SparseCore 0:
  10.1 126.5 all-gather.7
  138.3 98.3 all-gather.5
  238.2 40.1 all-gather.3

commit v11 on v9

--- a/solution.py
+++ b/solution.py
@@ -29,7 +29,14 @@
     t_cyc = lax.all_to_all(
         amplitudes.reshape(i_local, nocc, pw), "int", split_axis=1, concat_axis=0, tiled=True
     ).reshape(ibat * k_local, pw)
-    w2 = cycle_integrals.transpose(1, 0, 2).reshape(c_local * k_local, columns)
+    c_pad = -(-c_local // 128) * 128
+    if c_pad * 10 > c_local * 13:
+        c_pad = c_local
+    if c_pad == c_local:
+        w2 = cycle_integrals.transpose(1, 0, 2).reshape(c_local * k_local, columns)
+    else:
+        w2 = jnp.pad(cycle_integrals, ((0, 0), (0, c_pad - c_local), (0, 0)))
+        w2 = w2.reshape(k_local * c_pad, columns)
 
     ladder_chunks = []
     cycle_chunks = []
@@ -44,11 +51,19 @@
         ladder_chunks.append(
             jnp.dot(amplitudes, v_all, precision=PRECISION, preferred_element_type=jnp.float32)
         )
-        l_cyc = jnp.dot(t_cyc, v_all, precision=PRECISION, preferred_element_type=jnp.float32)
-        l_cyc = l_cyc.reshape(ibat, k_local, a_chunk, n_amp, c_local).transpose(3, 0, 2, 4, 1)
-        l_cyc = l_cyc.reshape(n_amp, ibat * a_chunk, c_local * k_local)
+        if c_pad == c_local:
+            l_cyc = jnp.dot(t_cyc, v_all, precision=PRECISION, preferred_element_type=jnp.float32)
+            l_cyc = l_cyc.reshape(ibat, k_local, a_chunk, n_amp, c_local).transpose(3, 0, 2, 4, 1)
+        else:
+            v_pad = jnp.pad(
+                v_all.reshape(pw, a_chunk, n_amp, c_local),
+                ((0, 0), (0, 0), (0, 0), (0, c_pad - c_local)),
+            ).reshape(pw, a_chunk * n_amp * c_pad)
+            l_cyc = jnp.dot(t_cyc, v_pad, precision=PRECISION, preferred_element_type=jnp.float32)
+            l_cyc = l_cyc.reshape(ibat, k_local, a_chunk, n_amp, c_pad).transpose(3, 0, 2, 1, 4)
+        l_cyc = l_cyc.reshape(n_amp, ibat * a_chunk, c_pad * k_local)
         moved = lax.all_to_all(l_cyc, "amp", split_axis=0, concat_axis=0, tiled=True)
-        moved = moved.reshape(n_amp * ibat * a_chunk, c_local * k_local)
+        moved = moved.reshape(n_amp * ibat * a_chunk, c_pad * k_local)
         cycle_chunks.append(
             jnp.dot(moved, w2, precision=PRECISION, preferred_element_type=jnp.float32)
         )

time: 357 us -> 367 us (1.028)
  waiting for transfers between devices: 177 us -> 199 us
  local copies, waits for them, and re-layouts: 76.7 us -> 70.3 us
  matrix products: 44.3 us -> 38.1 us
    dot_general x2 -> x0, local copies, waits for them, and re-layouts: 15.9 us -> none  [per_device(): jnp.dot(t_cyc, v_all, precision=PRECISION, preferred_element_type=jnp.flo...]
    all_gather x3, waiting for transfers between devices: 111 us -> 123 us  [per_device(): v_all = lax.all_gather(v, 'int', axis=0, tiled=True)]
    reshape x7, local copies, waits for them, and re-layouts: 30.6 us -> 18.9 us  [the longest x3 13.1 us: per_device(): v_all.reshape(pw, a_chunk, n_amp, c_local)]
    pad x0 -> x4, local copies, waits for them, and re-layouts: none -> 11.3 us  [the longest x3 7.87 us: per_device(): jnp.pad(v_all.reshape(pw, a_chunk, n_amp, c_local), ((0, 0), (0, 0), (0,...]
    all_to_all x3, waiting for transfers between devices: 48.7 us -> 58.5 us  [per_device(): lax.all_to_all(l_cyc, 'amp', split_axis=0, concat_axis=0, tiled=True)]
    all_gather x0 -> x1, local copies, waits for them, and re-layouts: none -> 8.13 us  [per_device(): v_all = lax.all_gather(v, 'int', axis=0, tiled=True)]
    transpose x1, local copies, waits for them, and re-layouts: 9.33 us -> 1.34 us  [per_device(): l_cyc.reshape(ibat, k_local, a_chunk, n_amp, c_pad).transpose(3, 0, 2, 1, 4)]
    optimization_barrier x0 -> x2, local copies, waits for them, and re-layouts: none -> 7.46 us  [per_device(): lax.optimization_barrier((v_all, ladder_chunks[-1], cycle_chunks[-1]))]
  transfers between devices with their start and end apart: 7 -> 7, of which waited for: 6 -> 7; matrix products, arithmetic and copies ran while one was open for 29% -> 20% of each run, Pallas kernels for 0% -> 0%
where the time goes in v11:
time: 367 us; the launch traced here: 365 us
  waiting for transfers between devices  199 us (54%)
  local copies, waits for them, and re-layouts  70.3 us (19%)
  matrix products  38.1 us (10%)
  blocking collectives  25.5 us (7%)
  starting transfers between devices  15.1 us (4%)
  between operations  14.1 us (4%)
    all_gather x3, waiting for transfers between devices, per_device(): v_all = lax.all_gather(v, 'int', axis=0, tiled=True)  123 us
    all_to_all x3, waiting for transfers between devices, per_device(): lax.all_to_all(l_cyc, 'amp', split_axis=0, concat_axis=0, tiled=True)  58.5 us
    all_to_all x1, blocking collectives, per_device(): lax.all_to_all(amplitudes.reshape(i_local, nocc, pw), 'int', split_axis=1...  25.5 us
    all_to_all x1, waiting for transfers between devices, per_device(): lax.all_to_all(parts, ('int', 'amp'), split_axis=0, concat_axis=0, tiled=...  17.7 us
    dot_general x3, matrix products, per_device(): jnp.dot(moved, w2, precision=PRECISION, preferred_element_type=jnp.float32)  17.2 us
    reshape x3, local copies, waits for them, and re-layouts, per_device(): v_all.reshape(pw, a_chunk, n_amp, c_local)  13.1 us
    dot_general x3, matrix products, per_device(): jnp.dot(amplitudes, v_all, precision=PRECISION, preferred_element_type=jn...  12.1 us
    all_to_all x3, starting transfers between devices, per_device(): lax.all_to_all(l_cyc, 'amp', split_axis=0, concat_axis=0, tiled=True)  11.4 us
  transfers between devices with their start and end apart: 7, of which 7 were waited for; matrix products, arithmetic and copies ran while one was open for 20% of the time, Pallas kernels for 0%

profile of v11, /device:TPU:0, one launch (start us, length us, event | category | flops | bytes accessed | tf_op | source)
XLA Modules:
  0.0 365.2 jit_solution(1500313754116249793)
XLA Ops:
  12.9 25.5 %all_to_all.35 = f32[2,96,512]{2,0,1:T(2,128)S(1)} all-to-all(f32[2,96,512]{2,0,1:T(2,128)S(1)} %copy.61), channel_id=1, replica_groups=mesh['amp'=8,'int'=4] {'int'}, dimensions={1} | all-to-all | bytes 786432 | tf_op jit(solution)/shard_map/all_to_all | solution.py:29
  38.5 98.3 %all-gather.6.cloned.1.call-done = f32[512,3200]{1,0:T(8,128)} async-done(((f32[128,3200]{1,0:T(8,128)}), f32[512,3200]{1,0:T(8,128)}) %all-gather.6.cloned.1.call-update) | async-done | bytes 6553616 | tf_op jit(solution)/shard_map/all_gather | solution.py:46
  136.8 8.1 %copy.60 = f32[512,3200]{0,1:T(8,128)} copy(f32[512,3200]{1,0:T(8,128)} %all-gather.6.cloned.1.call-done) | data formatting | bytes 13107200 | tf_op jit(solution)/shard_map/all_gather | solution.py:46
  144.9 7.7 %reshape.130 = f32[512,4,8,100]{0,3,2,1:T(8,128)} reshape(f32[512,3200]{0,1:T(8,128)} %copy.60) | data formatting | bytes 13107200 | tf_op jit(solution)/shard_map/reshape | solution.py:59
  152.6 4.5 %pad.16 = f32[512,4,8,128]{0,3,2,1:T(8,128)S(1)} pad(f32[512,4,8,100]{0,3,2,1:T(8,128)} %reshape.130, f32[]{:T(128)} %constant.34.clone.1), padding=0_0x0_0x0_0x0_28 | pad | bytes 14942212 | tf_op jit(solution)/shard_map/jit(_pad)/pad | solution.py:58
  157.1 4.3 %convolution_bitcast_fusion.1 = f32[24,8,32,128]{3,1,2,0:T(8,128)S(1)} fusion(f32[512,4096]{0,1:T(8,128)S(1)} %bitcast.83, f32[192,512]{1,0:T(8,128)S(1)} %bitcast.95), kind=kOutput, calls=%fused_computation.3 | convolution fusion | flops 2415919104 | bytes 11927552 | tf_op jit(solution)/shard_map/dot_general | solution.py:62
  165.7 3.8 %all-to-all-start.1 = ((f32[8,32,3072]{2,1,0:T(8,128)}), f32[8,32,3072]{2,1,0:T(8,128)S(1)}, u32[]{:S(2)}, u32[]{:S(2)}) async-start(f32[8,32,3072]{2,1,0:T(8,128)} %reshape.135), calls=%async_computation.1 | async-start | bytes 6291456 | tf_op jit(solution)/shard_map/all_to_all | solution.py:65
  169.5 5.4 %copy.74 = f32[24,100,512]{2,1,0:T(8,128)S(1)} copy(f32[24,100,512]{2,0,1:T(8,128)} %param.7) | data formatting | bytes 9830400
  178.4 4.4 %fusion = f32[192,3200]{1,0:T(8,128)} fusion(f32[192,512]{1,0:T(8,128)S(1)} %copy-done.4, f32[512,3200]{1,0:T(8,128)S(1)} %bitcast.85), kind=kOutput, calls=%fused_computation.22 | convolution fusion | flops 1887436800 | bytes 9404416 | tf_op jit(solution)/shard_map/dot_general | solution.py:52
  182.8 24.5 %all-to-all-done.1 = f32[8,32,3072]{2,1,0:T(8,128)S(1)} async-done(((f32[8,32,3072]{2,1,0:T(8,128)}), f32[8,32,3072]{2,1,0:T(8,128)S(1)}, u32[]{:S(2)}, u32[]{:S(2)}) %all-to-all-start.1) | async-done | bytes 3145760 | tf_op jit(solution)/shard_map/all_to_all | solution.py:65
  207.2 6.5 %fusion.1 = f32[256,512]{1,0:T(8,128)} fusion(f32[256,3072]{1,0:T(8,128)S(1)} %bitcast.87, f32[3072,512]{1,0:T(8,128)} %bitcast.80), kind=kOutput, calls=%fused_computation.23 | convolution fusion | flops 2415919104 | bytes 9961472 | tf_op jit(solution)/shard_map/dot_general | solution.py:68
  213.7 17.5 %all-gather.4.cloned.1.call-done = f32[512,2400]{1,0:T(8,128)} async-done(((f32[128,2400]{1,0:T(8,128)}), f32[512,2400]{1,0:T(8,128)}) %all-gather.4.cloned.1.call-update) | async-done | bytes 4915216 | tf_op jit(solution)/shard_map/all_gather | solution.py:46
  231.2 5.7 %copy.66 = f32[512,2400]{0,1:T(8,128)} copy(f32[512,2400]{1,0:T(8,128)} %all-gather.4.cloned.1.call-done) | data formatting | bytes 9830400 | tf_op jit(solution)/shard_map/optimization_barrier | solution.py:48
  236.9 5.2 %reshape.138 = f32[512,3,8,100]{0,3,2,1:T(8,128)} reshape(f32[512,2400]{0,1:T(8,128)} %copy.66) | data formatting | bytes 9830400 | tf_op jit(solution)/shard_map/reshape | solution.py:59
  251.1 3.8 %all-to-all-start.2 = ((f32[8,24,3072]{2,1,0:T(8,128)}), f32[8,24,3072]{2,1,0:T(8,128)S(1)}, u32[]{:S(2)}, u32[]{:S(2)}) async-start(f32[8,24,3072]{2,1,0:T(8,128)} %reshape.141), calls=%async_computation.2 | async-start | bytes 4718592 | tf_op jit(solution)/shard_map/all_to_all | solution.py:65
  257.0 5.4 %convolution_bitcast_fusion = f32[192,2400]{1,0:T(8,128)} fusion(f32[512,2400]{1,0:T(8,128)} %all-gather.4.cloned.1.call-done, f32[192,512]{1,0:T(8,128)S(1)} %copy-done.5), kind=kOutput, calls=%fused_computation | convolution fusion | flops 1415577600 | bytes 7151616 | tf_op jit(solution)/shard_map/dot_general | solution.py:52
  262.4 21.9 %all-to-all-done.2 = f32[8,24,3072]{2,1,0:T(8,128)S(1)} async-done(((f32[8,24,3072]{2,1,0:T(8,128)}), f32[8,24,3072]{2,1,0:T(8,128)S(1)}, u32[]{:S(2)}, u32[]{:S(2)}) %all-to-all-start.2) | async-done | bytes 2359328 | tf_op jit(solution)/shard_map/all_to_all | solution.py:65
  284.3 5.9 %fusion.2 = f32[192,512]{1,0:T(8,128)} fusion(f32[192,3072]{1,0:T(8,128)S(1)} %bitcast.92, f32[3072,512]{1,0:T(8,128)} %bitcast.81), kind=kOutput, calls=%fused_computation.24 | convolution fusion | flops 1811939328 | bytes 9043968 | tf_op jit(solution)/shard_map/dot_general | solution.py:68
  290.3 7.4 %all-gather.8.cloned.1.call-done = f32[512,800]{1,0:T(8,128)} async-done(((f32[128,800]{1,0:T(8,128)}), f32[512,800]{1,0:T(8,128)}) %all-gather.8.cloned.1.call-update) | async-done | bytes 1638416 | tf_op jit(solution)/shard_map/all_gather | solution.py:46
  303.3 3.8 %all-to-all-start.3 = ((f32[8,8,3072]{2,1,0:T(8,128)}), f32[8,8,3072]{2,1,0:T(8,128)S(1)}, u32[]{:S(2)}, u32[]{:S(2)}) async-start(f32[8,8,3072]{2,1,0:T(8,128)} %bitcast.79), calls=%async_computation.3 | async-start | bytes 1572864 | tf_op jit(solution)/shard_map/all_to_all | solution.py:65
  307.5 12.1 %all-to-all-done.3 = f32[8,8,3072]{2,1,0:T(8,128)S(1)} async-done(((f32[8,8,3072]{2,1,0:T(8,128)}), f32[8,8,3072]{2,1,0:T(8,128)S(1)}, u32[]{:S(2)}, u32[]{:S(2)}) %all-to-all-start.3) | async-done | bytes 786464 | tf_op jit(solution)/shard_map/all_to_all | solution.py:65
  319.6 4.8 %convolution_bitcast_fusion.5 = f32[8,8,1,512]{3,1,0,2:T(8,128)S(1)} fusion(f32[8,8,3072]{2,1,0:T(8,128)S(1)} %all-to-all-done.3, f32[3072,512,1]{1,0,2:T(8,128)} %bitcast.82), kind=kOutput, calls=%fused_computation.7 | convolution fusion | flops 603979776 | bytes 7208960 | tf_op jit(solution)/shard_map/dot_general | solution.py:68
  334.1 4.9 %concatenate.6 = f32[192,6400]{1,0:T(8,128)} concatenate(f32[192,3200]{1,0:T(8,128)S(1)} %copy-done, f32[192,2400]{1,0:T(8,128)} %convolution_bitcast_fusion, f32[192,800]{1,0:T(8,128)S(1)} %convolution_bitcast_fusion.4), dimensions={1} | concatenate | bytes 9830400 | tf_op jit(solution)/shard_map/concatenate | solution.py:70
  339.0 17.7 %all-to-all-done.4 = f32[32,128,64]{1,2,0:T(8,128)} async-done(((f32[32,128,64]{1,2,0:T(8,128)}), f32[32,128,64]{1,2,0:T(8,128)}, u32[]{:S(2)}, u32[]{:S(2)}) %all-to-all-start.4) | async-done | bytes 1048608 | tf_op jit(solution)/shard_map/all_to_all | solution.py:78
  (70 shorter events, 42.0 us)
Async XLA Ops:
  7.2 129.6 %all-gather.6.cloned.1.call-start = ((), (), s32[]{:S(2)}) async-start(), calls=%async_computation.6 | async-start | bytes 8192000 | tf_op jit(solution)/shard_map/all_gather | solution.py:46
  9.9 2.6 copy-start.3
  9.9 221.3 %all-gather.4.cloned.1.call-start = ((), (), s32[]{:S(2)}) async-start(), calls=%async_computation.5 | async-start | bytes 6225920 | tf_op jit(solution)/shard_map/all_gather | solution.py:46
  38.5 206.9 %copy-start.1 = (f32[4,2,24,512]{3,2,1,0:T(8,128)}, f32[4,2,24,512]{3,2,1,0:T(8,128)S(1)}, u32[]{:S(2)}) copy-start(f32[4,2,24,512]{3,2,1,0:T(8,128)S(1)} %copy.63) | copy-start | bytes 1179652
  165.7 41.6 %all-to-all-start.1 = ((f32[8,32,3072]{2,1,0:T(8,128)}), f32[8,32,3072]{2,1,0:T(8,128)S(1)}, u32[]{:S(2)}, u32[]{:S(2)}) async-start(f32[8,32,3072]{2,1,0:T(8,128)} %reshape.135), calls=%async_computation.1 | async-start | bytes 6291456 | tf_op jit(solution)/shard_map/all_to_all | solution.py:65
  169.5 8.9 %slice-start = ((s8[6553600]{0:T(1024)(128)(4,1)}), s8[4194304]{0:T(1024)(128)(4,1)S(1)}, s32[]{:S(2)}) async-start(s8[6553600]{0:T(1024)(128)(4,1)} %bitcast.84), calls=%async_computation.8 | async-start | bytes 8388608
  174.9 3.5 slice-start.1
  174.9 3.4 copy-start.4
  251.1 5.9 %copy-start.5 = (f32[192,512]{1,0:T(8,128)S(1)}, f32[192,512]{1,0:T(8,128)}, u32[]{:S(2)}) copy-start(f32[192,512]{1,0:T(8,128)} %param.5) | copy-start | bytes 1179652
  251.1 33.2 %all-to-all-start.2 = ((f32[8,24,3072]{2,1,0:T(8,128)}), f32[8,24,3072]{2,1,0:T(8,128)S(1)}, u32[]{:S(2)}, u32[]{:S(2)}) async-start(f32[8,24,3072]{2,1,0:T(8,128)} %reshape.141), calls=%async_computation.2 | async-start | bytes 4718592 | tf_op jit(solution)/shard_map/all_to_all | solution.py:65
  254.9 42.8 %all-gather.8.cloned.1.call-start = ((), (), s32[]{:S(2)}) async-start(), calls=%async_computation.7 | async-start | bytes 2293760 | tf_op jit(solution)/shard_map/all_gather | solution.py:46
  299.6 1.0 copy-start.2
  301.8 5.3 %copy-start.7 = (f32[256,512]{1,0:T(8,128)S(1)}, f32[256,512]{1,0:T(8,128)}, u32[]{:S(2)}) copy-start(f32[256,512]{1,0:T(8,128)} %fusion.1) | copy-start | bytes 1572868
  301.8 5.5 %copy-start.8 = (f32[192,512]{1,0:T(8,128)S(1)}, f32[192,512]{1,0:T(8,128)}, u32[]{:S(2)}) copy-start(f32[192,512]{1,0:T(8,128)} %fusion.2) | copy-start | bytes 1179652
  303.3 16.3 %all-to-all-start.3 = ((f32[8,8,3072]{2,1,0:T(8,128)}), f32[8,8,3072]{2,1,0:T(8,128)S(1)}, u32[]{:S(2)}, u32[]{:S(2)}) async-start(f32[8,8,3072]{2,1,0:T(8,128)} %bitcast.79), calls=%async_computation.3 | async-start | bytes 1572864 | tf_op jit(solution)/shard_map/all_to_all | solution.py:65
  325.3 5.9 %copy-start.9 = (s32[96]{0:T(128)S(1)}, s32[96]{0:T(128)}, u32[]{:S(2)}) copy-start(s32[96]{0:T(128)} %param.8) | copy-start | bytes 1156
  325.3 6.5 %copy-start.6 = (f32[192,512]{1,0:T(8,128)S(1)}, f32[192,512]{1,0:T(8,128)}, u32[]{:S(2)}) copy-start(f32[192,512]{1,0:T(8,128)} %param.5) | copy-start | bytes 1179652
  326.9 7.2 %copy-start = (f32[192,3200]{1,0:T(8,128)S(1)}, f32[192,3200]{1,0:T(8,128)}, u32[]{:S(2)}) copy-start(f32[192,3200]{1,0:T(8,128)} %fusion) | copy-start | bytes 7372804
  326.9 29.7 %all-to-all-start.4 = ((f32[32,128,64]{1,2,0:T(8,128)}), f32[32,128,64]{1,2,0:T(8,128)}, u32[]{:S(2)}, u32[]{:S(2)}) async-start(f32[32,128,64]{1,2,0:T(8,128)} %bitcast.99), calls=%async_computation.4 | async-start | bytes 2097152 | tf_op jit(solution)/shard_map/all_to_all | solution.py:78
Sparse Core Ops, SparseCore 0:
  10.1 126.5 all-gather.5
  138.3 92.8 all-gather.3
  257.3 40.3 all-gather.7

commit v12 on v9

--- a/solution.py
+++ b/solution.py
@@ -18,7 +18,7 @@
     slab = a_local * n_amp
     k_local, c_local, columns = cycle_integrals.shape
     if a_local >= 4:
-        sizes = [a_local // 2, a_local - a_local // 2 - 1, 1]
+        sizes = [(a_local - 1) // 2, a_local - 2 - (a_local - 1) // 2, 1, 1]
     elif a_local >= 2:
         sizes = [a_local - 1, 1]
     else:

time: 357 us -> 355 us (level)
  local copies, waits for them, and re-layouts: 76.7 us -> 68 us
  matrix products: 44.3 us -> 50.8 us
  waiting for transfers between devices: 177 us -> 173 us
    dot_general x2, local copies, waits for them, and re-layouts: 15.9 us -> 11.1 us  [per_device(): jnp.dot(t_cyc, v_all, precision=PRECISION, preferred_element_type=jnp.flo...]
    all_gather x3 -> x4, waiting for transfers between devices: 111 us -> 106 us  [per_device(): v_all = lax.all_gather(v, 'int', axis=0, tiled=True)]
    all_to_all x3 -> x4, starting transfers between devices: 11.1 us -> 14.9 us  [per_device(): lax.all_to_all(l_cyc, 'amp', split_axis=0, concat_axis=0, tiled=True)]
    transpose x1, local copies, waits for them, and re-layouts: 9.33 us -> 5.63 us  [per_device(): l_cyc.reshape(ibat, k_local, a_chunk, n_amp, c_local)]
    dot_general x3 -> x4, matrix products: 14.8 us -> 18.4 us  [per_device(): jnp.dot(moved, w2, precision=PRECISION, preferred_element_type=jnp.float32)]
    reshape x4 -> x6, local copies, waits for them, and re-layouts: 11.8 us -> 15.3 us  [per_device(): l_cyc.reshape(ibat, k_local, a_chunk, n_amp, c_local)]
    dot_general x3 -> x4, matrix products: 14.6 us -> 17.4 us  [per_device(): jnp.dot(amplitudes, v_all, precision=PRECISION, preferred_element_type=jn...]
    all_to_all x3 -> x4, waiting for transfers between devices: 48.7 us -> 50.6 us  [per_device(): lax.all_to_all(l_cyc, 'amp', split_axis=0, concat_axis=0, tiled=True)]
  transfers between devices with their start and end apart: 7 -> 9, of which waited for: 6 -> 8; matrix products, arithmetic and copies ran while one was open for 29% -> 29% of each run, Pallas kernels for 0% -> 0%
where the time goes in v12:
time: 355 us; the launch traced here: 354 us
  waiting for transfers between devices  173 us (49%)
  local copies, waits for them, and re-layouts  68 us (19%)
  matrix products  50.8 us (14%)
  blocking collectives  27.5 us (8%)
  starting transfers between devices  18.2 us (5%)
  between operations  14 us (4%)
    all_gather x4, waiting for transfers between devices, per_device(): v_all = lax.all_gather(v, 'int', axis=0, tiled=True)  106 us
    all_to_all x4, waiting for transfers between devices, per_device(): lax.all_to_all(l_cyc, 'amp', split_axis=0, concat_axis=0, tiled=True)  50.6 us
    all_to_all x1, blocking collectives, per_device(): lax.all_to_all(amplitudes.reshape(i_local, nocc, pw), 'int', split_axis=1...  27.5 us
    reshape x4, local copies, waits for them, and re-layouts, per_device(): l_cyc = l_cyc.reshape(n_amp, ibat * a_chunk, c_local * k_local)  18.7 us
    dot_general x4, matrix products, per_device(): jnp.dot(moved, w2, precision=PRECISION, preferred_element_type=jnp.float32)  18.4 us
    dot_general x4, matrix products, per_device(): jnp.dot(amplitudes, v_all, precision=PRECISION, preferred_element_type=jn...  17.4 us
    all_to_all x1, waiting for transfers between devices, per_device(): lax.all_to_all(parts, ('int', 'amp'), split_axis=0, concat_axis=0, tiled=...  15.7 us
    reshape x6, local copies, waits for them, and re-layouts, per_device(): l_cyc.reshape(ibat, k_local, a_chunk, n_amp, c_local)  15.3 us
  transfers between devices with their start and end apart: 9, of which 8 were waited for; matrix products, arithmetic and copies ran while one was open for 29% of the time, Pallas kernels for 0%

profile of v12, /device:TPU:0, one launch (start us, length us, event | category | flops | bytes accessed | tf_op | source)
XLA Modules:
  0.0 353.6 jit_solution(3028213121475945152)
XLA Ops:
  12.1 27.5 %all_to_all.40 = f32[2,96,512]{2,0,1:T(2,128)S(1)} all-to-all(f32[2,96,512]{2,0,1:T(2,128)S(1)} %copy.57), channel_id=1, replica_groups=mesh['amp'=8,'int'=4] {'int'}, dimensions={1} | all-to-all | bytes 786432 | tf_op jit(solution)/shard_map/all_to_all | solution.py:29
  39.7 71.0 %all-gather.7.cloned.1.call-done = f32[512,2400]{1,0:T(8,128)} async-done(((f32[128,2400]{1,0:T(8,128)}), f32[512,2400]{1,0:T(8,128)}) %all-gather.7.cloned.1.call-update) | async-done | bytes 4915216 | tf_op jit(solution)/shard_map/all_gather | solution.py:39
  110.7 5.7 %copy.60 = f32[2400,512]{1,0:T(8,128)} copy(f32[2400,512]{0,1:T(8,128)} %bitcast.79) | data formatting | bytes 9830400 | tf_op jit(solution)/shard_map/dot_general | solution.py:47
  116.4 5.4 %reshape.144 = f32[3,8,100,512,1]{3,2,1,0,4:T(8,128)} reshape(f32[2400,512]{1,0:T(8,128)} %copy.60) | data formatting | bytes 9830400 | tf_op jit(solution)/shard_map/dot_general | solution.py:47
  121.9 4.9 %convolution_bitcast_fusion.2 = f32[8,8,3,100,24]{3,4,0,2,1:T(8,128)S(1)} fusion(f32[8,24,512,1,1]{2,1,4,3,0:T(8,128)S(1)} %bitcast.82, f32[3,8,100,512,1]{3,2,1,0,4:T(8,128)} %reshape.144), kind=kOutput, calls=%fused_computation.2 | convolution fusion | flops 1415577600 | bytes 7151616 | tf_op jit(solution)/shard_map/dot_general | solution.py:47
  126.8 5.6 %copy.61 = f32[8,8,3,100,24]{4,3,2,1,0:T(8,128)} copy(f32[8,8,3,100,24]{3,4,0,2,1:T(8,128)S(1)} %convolution_bitcast_fusion.2) | data formatting | bytes 3686400 | tf_op jit(solution)/shard_map/transpose | solution.py:48
  132.5 7.6 %reshape.126 = f32[8,24,2400]{2,1,0:T(8,128)} reshape(f32[8,8,3,100,24]{4,3,2,1,0:T(8,128)} %copy.61) | data formatting | bytes 3686400 | tf_op jit(solution)/shard_map/reshape | solution.py:49
  146.6 5.6 %fusion.4 = f32[192,2400]{1,0:T(8,128)} fusion(f32[192,512]{1,0:T(8,128)S(1)} %copy-done.2, f32[512,2400]{1,0:T(8,128)} %all-gather.7.cloned.1.call-done), kind=kOutput, calls=%fused_computation.25 | convolution fusion | flops 1415577600 | bytes 7151616 | tf_op jit(solution)/shard_map/dot_general | solution.py:45
  152.2 15.8 %all-to-all-done.1 = f32[8,24,2400]{2,1,0:T(8,128)S(1)} async-done(((f32[8,24,2400]{2,1,0:T(8,128)}), f32[8,24,2400]{2,1,0:T(8,128)S(1)}, u32[]{:S(2)}, u32[]{:S(2)}) %all-to-all-start.1) | async-done | bytes 1843232 | tf_op jit(solution)/shard_map/all_to_all | solution.py:50
  168.0 5.1 %fusion.5 = f32[192,512]{1,0:T(8,128)} fusion(f32[192,2400]{1,0:T(8,128)S(1)} %bitcast.88, f32[2400,512]{1,0:T(8,128)} %bitcast.74), kind=kOutput, calls=%fused_computation.26 | convolution fusion | flops 1415577600 | bytes 7151616 | tf_op jit(solution)/shard_map/dot_general | solution.py:53
  173.2 32.0 %all-gather.5.cloned.1.call-done = f32[512,2400]{1,0:T(8,128)} async-done(((f32[128,2400]{1,0:T(8,128)}), f32[512,2400]{1,0:T(8,128)}) %all-gather.5.cloned.1.call-update) | async-done | bytes 4915216 | tf_op jit(solution)/shard_map/all_gather | solution.py:39
  205.2 5.5 %convolution_bitcast_fusion = f32[192,2400]{1,0:T(8,128)} fusion(f32[512,2400]{1,0:T(8,128)} %all-gather.5.cloned.1.call-done, f32[192,512]{1,0:T(8,128)S(1)} %bitcast.83), kind=kOutput, calls=%fused_computation | convolution fusion | flops 1415577600 | bytes 7151616 | tf_op jit(solution)/shard_map/dot_general | solution.py:47
  213.3 5.6 %copy.63 = f32[8,24,3,8,100]{1,4,2,0,3:T(8,128)} copy(f32[8,24,3,8,100]{4,3,2,1,0:T(8,128)S(1)} %reshape.130) | data formatting | bytes 3686400 | tf_op jit(solution)/shard_map/reshape | solution.py:48
  218.9 7.6 %reshape.131 = f32[8,24,2400]{2,1,0:T(8,128)} reshape(f32[8,8,3,100,24]{4,3,2,1,0:T(8,128)} %bitcast.78) | data formatting | bytes 3686400 | tf_op jit(solution)/shard_map/reshape | solution.py:49
  230.6 5.5 %convolution_bitcast_fusion.1 = f32[192,2400]{1,0:T(8,128)} fusion(f32[512,2400]{1,0:T(8,128)} %all-gather.5.cloned.1.call-done, f32[192,512]{1,0:T(8,128)S(1)} %copy-done.2), kind=kOutput, calls=%fused_computation.1 | convolution fusion | flops 1415577600 | bytes 7151616 | tf_op jit(solution)/shard_map/dot_general | solution.py:45
  236.1 18.1 %all-to-all-done.2 = f32[8,24,2400]{2,1,0:T(8,128)S(1)} async-done(((f32[8,24,2400]{2,1,0:T(8,128)}), f32[8,24,2400]{2,1,0:T(8,128)S(1)}, u32[]{:S(2)}, u32[]{:S(2)}) %all-to-all-start.2) | async-done | bytes 1843232 | tf_op jit(solution)/shard_map/all_to_all | solution.py:50
  254.3 5.2 %fusion.6 = f32[192,512]{1,0:T(8,128)} fusion(f32[192,2400]{1,0:T(8,128)S(1)} %bitcast.89, f32[2400,512]{1,0:T(8,128)} %bitcast.75), kind=kOutput, calls=%fused_computation.27 | convolution fusion | flops 1415577600 | bytes 7151616 | tf_op jit(solution)/shard_map/dot_general | solution.py:53
  273.8 7.5 %all-to-all-done.3 = f32[8,8,2400]{2,1,0:T(8,128)S(1)} async-done(((f32[8,8,2400]{2,1,0:T(8,128)}), f32[8,8,2400]{2,1,0:T(8,128)S(1)}, u32[]{:S(2)}, u32[]{:S(2)}) %all-to-all-start.3) | async-done | bytes 614432 | tf_op jit(solution)/shard_map/all_to_all | solution.py:50
  281.3 4.0 %fusion = f32[64,512]{1,0:T(8,128)S(1)} fusion(f32[2400,512]{1,0:T(8,128)} %bitcast.76, f32[8,8,2400]{2,1,0:T(8,128)S(1)} %all-to-all-done.3), kind=kOutput, calls=%fused_computation.9 | convolution fusion | flops 471859200 | bytes 5660672 | tf_op jit(solution)/shard_map/dot_general | solution.py:53
  295.9 3.9 %all-to-all-start.4 = ((f32[8,8,2400]{2,1,0:T(8,128)}), f32[8,8,2400]{2,1,0:T(8,128)S(1)}, u32[]{:S(2)}, u32[]{:S(2)}) async-start(f32[8,8,2400]{2,1,0:T(8,128)} %reshape.140), calls=%async_computation.4 | async-start | bytes 1245184 | tf_op jit(solution)/shard_map/all_to_all | solution.py:50
  301.3 9.2 %all-to-all-done.4 = f32[8,8,2400]{2,1,0:T(8,128)S(1)} async-done(((f32[8,8,2400]{2,1,0:T(8,128)}), f32[8,8,2400]{2,1,0:T(8,128)S(1)}, u32[]{:S(2)}, u32[]{:S(2)}) %all-to-all-start.4) | async-done | bytes 614432 | tf_op jit(solution)/shard_map/all_to_all | solution.py:50
  310.5 4.0 %convolution_bitcast_fusion.7 = f32[8,8,1,512]{3,1,0,2:T(8,128)S(1)} fusion(f32[8,8,2400]{2,1,0:T(8,128)S(1)} %all-to-all-done.4, f32[2400,512,1]{1,0,2:T(8,128)} %bitcast.77), kind=kOutput, calls=%fused_computation.7 | convolution fusion | flops 471859200 | bytes 5660672 | tf_op jit(solution)/shard_map/dot_general | solution.py:53
  324.6 6.0 %concatenate.6 = f32[192,6400]{1,0:T(8,128)} concatenate(f32[192,2400]{1,0:T(8,128)S(1)} %copy-done.4, f32[192,2400]{1,0:T(8,128)} %convolution_bitcast_fusion.1, f32[192,800]{1,0:T(8,128)} %convolution_bitcast_fusion.6, f32[192,800]{1,0:T(8,128)} %convolution_bitcast_fusion.4), dimensions={1} | concatenate | bytes 9830400 | tf_op jit(solution)/shard_map/concatenate | solution.py:55
  330.6 15.7 %all-to-all-done.5 = f32[32,128,64]{1,2,0:T(8,128)S(1)} async-done(((f32[32,128,64]{1,2,0:T(8,128)}), f32[32,128,64]{1,2,0:T(8,128)S(1)}, u32[]{:S(2)}, u32[]{:S(2)}) %all-to-all-start.5) | async-done | bytes 1048608 | tf_op jit(solution)/shard_map/all_to_all | solution.py:63
  (62 shorter events, 55.4 us)
Async XLA Ops:
  7.2 103.6 %all-gather.7.cloned.1.call-start = ((), (), s32[]{:S(2)}) async-start(), calls=%async_computation.7 | async-start | bytes 6225920 | tf_op jit(solution)/shard_map/all_gather | solution.py:39
  10.8 1.0 copy-start.2
  10.8 194.3 %all-gather.5.cloned.1.call-start = ((), (), s32[]{:S(2)}) async-start(), calls=%async_computation.6 | async-start | bytes 6225920 | tf_op jit(solution)/shard_map/all_gather | solution.py:39
  39.7 219.8 %copy-start = (f32[4,2,24,512]{3,2,1,0:T(8,128)}, f32[4,2,24,512]{3,2,1,0:T(8,128)S(1)}, u32[]{:S(2)}) copy-start(f32[4,2,24,512]{3,2,1,0:T(8,128)S(1)} %copy.59) | copy-start | bytes 1179652
  140.1 28.0 %all-to-all-start.1 = ((f32[8,24,2400]{2,1,0:T(8,128)}), f32[8,24,2400]{2,1,0:T(8,128)S(1)}, u32[]{:S(2)}, u32[]{:S(2)}) async-start(f32[8,24,2400]{2,1,0:T(8,128)} %reshape.126), calls=%async_computation.1 | async-start | bytes 3735552 | tf_op jit(solution)/shard_map/all_to_all | solution.py:50
  143.9 115.6 %all-gather.9.cloned.1.call-start = ((), (), s32[]{:S(2)}) async-start(), calls=%async_computation.8 | async-start | bytes 2293760 | tf_op jit(solution)/shard_map/all_gather | solution.py:39
  226.5 27.8 %all-to-all-start.2 = ((f32[8,24,2400]{2,1,0:T(8,128)}), f32[8,24,2400]{2,1,0:T(8,128)S(1)}, u32[]{:S(2)}, u32[]{:S(2)}) async-start(f32[8,24,2400]{2,1,0:T(8,128)} %reshape.131), calls=%async_computation.2 | async-start | bytes 3735552 | tf_op jit(solution)/shard_map/all_to_all | solution.py:50
  230.1 58.3 %all-gather.11.cloned.1.call-start = ((), (), s32[]{:S(2)}) async-start(), calls=%async_computation.9 | async-start | bytes 2293760 | tf_op jit(solution)/shard_map/all_gather | solution.py:39
  267.1 14.3 %all-to-all-start.3 = ((f32[8,8,2400]{2,1,0:T(8,128)}), f32[8,8,2400]{2,1,0:T(8,128)S(1)}, u32[]{:S(2)}, u32[]{:S(2)}) async-start(f32[8,8,2400]{2,1,0:T(8,128)} %reshape.134), calls=%async_computation.3 | async-start | bytes 1245184 | tf_op jit(solution)/shard_map/all_to_all | solution.py:50
  273.8 14.5 %copy-start.1 = (f32[4,2,24,512]{3,2,1,0:T(8,128)S(1)}, f32[4,2,24,512]{3,2,1,0:T(8,128)}, u32[]{:S(2)}) copy-start(f32[4,2,24,512]{3,2,1,0:T(8,128)} %copy-done) | copy-start | bytes 1179652
  295.9 5.1 %copy-start.5 = (f32[192,512]{1,0:T(8,128)S(1)}, f32[192,512]{1,0:T(8,128)}, u32[]{:S(2)}) copy-start(f32[192,512]{1,0:T(8,128)} %fusion.6) | copy-start | bytes 1179652
  295.9 14.6 %all-to-all-start.4 = ((f32[8,8,2400]{2,1,0:T(8,128)}), f32[8,8,2400]{2,1,0:T(8,128)S(1)}, u32[]{:S(2)}, u32[]{:S(2)}) async-start(f32[8,8,2400]{2,1,0:T(8,128)} %reshape.140), calls=%async_computation.4 | async-start | bytes 1245184 | tf_op jit(solution)/shard_map/all_to_all | solution.py:50
  315.7 5.1 %copy-start.6 = (s32[96]{0:T(128)S(1)}, s32[96]{0:T(128)}, u32[]{:S(2)}) copy-start(s32[96]{0:T(128)} %param.8) | copy-start | bytes 1156
  315.7 5.7 %copy-start.3 = (f32[192,512]{1,0:T(8,128)S(1)}, f32[192,512]{1,0:T(8,128)}, u32[]{:S(2)}) copy-start(f32[192,512]{1,0:T(8,128)} %param.5) | copy-start | bytes 1179652
  317.3 7.3 %copy-start.4 = (f32[192,2400]{1,0:T(8,128)S(1)}, f32[192,2400]{1,0:T(8,128)}, u32[]{:S(2)}) copy-start(f32[192,2400]{1,0:T(8,128)} %fusion.4) | copy-start | bytes 5529604
  317.3 29.0 %all-to-all-start.5 = ((f32[32,128,64]{1,2,0:T(8,128)}), f32[32,128,64]{1,2,0:T(8,128)S(1)}, u32[]{:S(2)}, u32[]{:S(2)}) async-start(f32[32,128,64]{1,2,0:T(8,128)} %bitcast.30), calls=%async_computation.5 | async-start | bytes 2097152 | tf_op jit(solution)/shard_map/all_to_all | solution.py:63
Sparse Core Ops, SparseCore 0:
  11.0 99.7 all-gather.6
  112.3 92.8 all-gather.4
  206.8 39.7 all-gather.8
  248.0 40.2 all-gather.10

commit v13 on v12

--- a/solution.py
+++ b/solution.py
@@ -31,13 +31,28 @@
     ).reshape(ibat * k_local, pw)
     w2 = cycle_integrals.transpose(1, 0, 2).reshape(c_local * k_local, columns)
 
+    col_local = columns // n_amp
+
+    def reduce_block(parts, a_count):
+        parts = parts.reshape(n_amp, n_int, i_local, a_count, n_amp, col_local)
+        parts = parts.transpose(1, 4, 2, 0, 3, 5).reshape(n_int * n_amp, i_local * n_amp * a_count, col_local)
+        got = lax.all_to_all(parts, ("int", "amp"), split_axis=0, concat_axis=0, tiled=True)
+        return jnp.sum(got, axis=0).reshape(i_local, n_amp, a_count, col_local)
+
     ladder_chunks = []
     cycle_chunks = []
+    reduced = []
     for t in range(chunks):
         a_chunk = sizes[t]
         v = lax.slice_in_dim(slab_integrals, starts[t] * nvir, (starts[t] + a_chunk) * nvir, axis=1)
         v_all = lax.all_gather(v, "int", axis=0, tiled=True)
-        if t:
+        if t and t == chunks - 1:
+            early = jnp.concatenate(cycle_chunks, axis=2)
+            reduced.append(reduce_block(early, early.shape[2]))
+            v_all, ladder_chunks[-1], reduced[0] = lax.optimization_barrier(
+                (v_all, ladder_chunks[-1], reduced[0])
+            )
+        elif t:
             v_all, ladder_chunks[-1], cycle_chunks[-1] = lax.optimization_barrier(
                 (v_all, ladder_chunks[-1], cycle_chunks[-1])
             )
@@ -49,19 +64,12 @@
         l_cyc = l_cyc.reshape(n_amp, ibat * a_chunk, c_local * k_local)
         moved = lax.all_to_all(l_cyc, "amp", split_axis=0, concat_axis=0, tiled=True)
         moved = moved.reshape(n_amp * ibat * a_chunk, c_local * k_local)
-        cycle_chunks.append(
-            jnp.dot(moved, w2, precision=PRECISION, preferred_element_type=jnp.float32)
-        )
+        part = jnp.dot(moved, w2, precision=PRECISION, preferred_element_type=jnp.float32)
+        cycle_chunks.append(part.reshape(n_amp, ibat, a_chunk, columns))
     ladder = jnp.concatenate(ladder_chunks, axis=1)
+    reduced.append(reduce_block(cycle_chunks[-1], sizes[-1]))
 
-    parts = jnp.concatenate(
-        [c.reshape(n_amp, ibat, sizes[t], columns) for t, c in enumerate(cycle_chunks)], axis=2
-    )
-    col_local = columns // n_amp
-    parts = parts.transpose(1, 0, 2, 3).reshape(n_int, i_local * slab, n_amp, col_local)
-    parts = parts.transpose(0, 2, 1, 3).reshape(n_int * n_amp, i_local * slab, col_local)
-    gathered = lax.all_to_all(parts, ("int", "amp"), split_axis=0, concat_axis=0, tiled=True)
-    sums = jnp.sum(gathered, axis=0)
+    sums = jnp.concatenate(reduced, axis=2).reshape(i_local * slab, col_local)
 
     row_start = lax.axis_index("int") * i_local
     batch_labels = lax.dynamic_slice_in_dim(occ_irrep, row_start, i_local, 0)

time: 355 us -> 388 us (1.093)
  waiting for transfers between devices: 173 us -> 191 us
  local copies, waits for them, and re-layouts: 68 us -> 75.7 us
    all_to_all x1 -> x2, waiting for transfers between devices: 15.7 us -> 38.8 us  [reduce_block(): lax.all_to_all(parts, ('int', 'amp'), split_axis=0, concat_axis=0, tiled=...]
    dot_general x1 -> x2, local copies, waits for them, and re-layouts: 0.14 us -> 5.88 us  [per_device(): jnp.dot(moved, w2, precision=PRECISION, preferred_element_type=jnp.float32)]
    dot_general x4, matrix products: 18.4 us -> 22.9 us  [per_device(): jnp.dot(moved, w2, precision=PRECISION, preferred_element_type=jnp.float32)]
  transfers between devices with their start and end apart: 9 -> 10, of which waited for: 8 -> 7; matrix products, arithmetic and copies ran while one was open for 29% -> 27% of each run, Pallas kernels for 0% -> 0%
where the time goes in v13:
time: 388 us; the launch traced here: 387 us
  waiting for transfers between devices  191 us (49%)
  local copies, waits for them, and re-layouts  75.7 us (20%)
  matrix products  53.8 us (14%)
  blocking collectives  27.5 us (7%)
  starting transfers between devices  21.4 us (6%)
  between operations  14.1 us (4%)
    all_gather x4, waiting for transfers between devices, per_device(): v_all = lax.all_gather(v, 'int', axis=0, tiled=True)  103 us
    all_to_all x4, waiting for transfers between devices, per_device(): lax.all_to_all(l_cyc, 'amp', split_axis=0, concat_axis=0, tiled=True)  48.5 us
    all_to_all x2, waiting for transfers between devices, reduce_block(): lax.all_to_all(parts, ('int', 'amp'), split_axis=0, concat_axis=0, tiled=...  38.8 us
    all_to_all x1, blocking collectives, per_device(): lax.all_to_all(amplitudes.reshape(i_local, nocc, pw), 'int', split_axis=1...  27.5 us
    dot_general x4, matrix products, per_device(): jnp.dot(moved, w2, precision=PRECISION, preferred_element_type=jnp.float32)  22.9 us
    reshape x4, local copies, waits for them, and re-layouts, per_device(): l_cyc = l_cyc.reshape(n_amp, ibat * a_chunk, c_local * k_local)  18.7 us
    dot_general x4, matrix products, per_device(): jnp.dot(amplitudes, v_all, precision=PRECISION, preferred_element_type=jn...  15.9 us
    reshape x6, local copies, waits for them, and re-layouts, per_device(): l_cyc.reshape(ibat, k_local, a_chunk, n_amp, c_local)  15.3 us
  transfers between devices with their start and end apart: 10, of which 7 were waited for; matrix products, arithmetic and copies ran while one was open for 27% of the time, Pallas kernels for 0%

profile of v13, /device:TPU:0, one launch (start us, length us, event | category | flops | bytes accessed | tf_op | source)
XLA Modules:
  0.0 386.8 jit_solution(17407000539166638858)
XLA Ops:
  12.1 27.5 %all_to_all.45 = f32[2,96,512]{2,0,1:T(2,128)S(1)} all-to-all(f32[2,96,512]{2,0,1:T(2,128)S(1)} %copy.110), channel_id=1, replica_groups=mesh['amp'=8,'int'=4] {'int'}, dimensions={1} | all-to-all | bytes 786432 | tf_op jit(solution)/shard_map/all_to_all | solution.py:29
  39.7 71.0 %all-gather.7.cloned.1.call-done = f32[512,2400]{1,0:T(8,128)} async-done(((f32[128,2400]{1,0:T(8,128)}), f32[512,2400]{1,0:T(8,128)}) %all-gather.7.cloned.1.call-update) | async-done | bytes 4915216 | tf_op jit(solution)/shard_map/all_gather | solution.py:48
  110.7 5.7 %copy.113 = f32[2400,512]{1,0:T(8,128)} copy(f32[2400,512]{0,1:T(8,128)} %bitcast.108) | data formatting | bytes 9830400 | tf_op jit(solution)/shard_map/dot_general | solution.py:62
  116.4 5.4 %reshape.160 = f32[3,8,100,512,1]{3,2,1,0,4:T(8,128)} reshape(f32[2400,512]{1,0:T(8,128)} %copy.113) | data formatting | bytes 9830400 | tf_op jit(solution)/shard_map/dot_general | solution.py:62
  121.9 4.9 %convolution_bitcast_fusion.2 = f32[8,8,3,100,24]{3,4,0,2,1:T(8,128)S(1)} fusion(f32[8,24,512,1,1]{2,1,4,3,0:T(8,128)S(1)} %bitcast.111, f32[3,8,100,512,1]{3,2,1,0,4:T(8,128)} %reshape.160), kind=kOutput, calls=%fused_computation.3 | convolution fusion | flops 1415577600 | bytes 7151616 | tf_op jit(solution)/shard_map/dot_general | solution.py:62
  126.8 5.6 %copy.114 = f32[8,8,3,100,24]{4,3,2,1,0:T(8,128)} copy(f32[8,8,3,100,24]{3,4,0,2,1:T(8,128)S(1)} %convolution_bitcast_fusion.2) | data formatting | bytes 3686400 | tf_op jit(solution)/shard_map/transpose | solution.py:63
  132.5 7.6 %reshape.144 = f32[8,24,2400]{2,1,0:T(8,128)} reshape(f32[8,8,3,100,24]{4,3,2,1,0:T(8,128)} %copy.114) | data formatting | bytes 3686400 | tf_op jit(solution)/shard_map/reshape | solution.py:64
  146.6 5.6 %fusion.2 = f32[192,2400]{1,0:T(8,128)} fusion(f32[192,512]{1,0:T(8,128)S(1)} %copy-done.2, f32[512,2400]{1,0:T(8,128)} %all-gather.7.cloned.1.call-done), kind=kOutput, calls=%fused_computation.25 | convolution fusion | flops 1415577600 | bytes 7151616 | tf_op jit(solution)/shard_map/dot_general | solution.py:60
  152.2 15.8 %all-to-all-done.1 = f32[8,24,2400]{2,1,0:T(8,128)S(1)} async-done(((f32[8,24,2400]{2,1,0:T(8,128)}), f32[8,24,2400]{2,1,0:T(8,128)S(1)}, u32[]{:S(2)}, u32[]{:S(2)}) %all-to-all-start.1) | async-done | bytes 1843232 | tf_op jit(solution)/shard_map/all_to_all | solution.py:65
  168.4 5.1 %fusion.3 = f32[8,8,3,512]{3,0,2,1:T(8,128)} fusion(f32[8,8,3,2400]{3,0,2,1:T(8,128)S(1)} %bitcast.122, f32[2400,512,1,1]{1,0,3,2:T(8,128)} %bitcast.117), kind=kOutput, calls=%fused_computation.26 | convolution fusion | flops 1415577600 | bytes 7151616 | tf_op jit(solution)/shard_map/dot_general | solution.py:67
  173.6 31.6 %all-gather.5.cloned.1.call-done = f32[512,2400]{1,0:T(8,128)} async-done(((f32[128,2400]{1,0:T(8,128)}), f32[512,2400]{1,0:T(8,128)}) %all-gather.5.cloned.1.call-update) | async-done | bytes 4915216 | tf_op jit(solution)/shard_map/all_gather | solution.py:48
  205.2 5.5 %convolution_bitcast_fusion = f32[192,2400]{1,0:T(8,128)} fusion(f32[512,2400]{1,0:T(8,128)} %all-gather.5.cloned.1.call-done, f32[192,512]{1,0:T(8,128)S(1)} %bitcast.112), kind=kOutput, calls=%fused_computation | convolution fusion | flops 1415577600 | bytes 7151616 | tf_op jit(solution)/shard_map/dot_general | solution.py:62
  213.3 5.6 %copy.117 = f32[8,24,3,8,100]{1,4,2,0,3:T(8,128)} copy(f32[8,24,3,8,100]{4,3,2,1,0:T(8,128)S(1)} %reshape.147) | data formatting | bytes 3686400 | tf_op jit(solution)/shard_map/reshape | solution.py:63
  218.9 7.6 %reshape.148 = f32[8,24,2400]{2,1,0:T(8,128)} reshape(f32[8,8,3,100,24]{4,3,2,1,0:T(8,128)} %bitcast.107) | data formatting | bytes 3686400 | tf_op jit(solution)/shard_map/reshape | solution.py:64
  230.3 5.5 %convolution_bitcast_fusion.1 = f32[192,2400]{1,0:T(8,128)} fusion(f32[512,2400]{1,0:T(8,128)} %all-gather.5.cloned.1.call-done, f32[192,512]{1,0:T(8,128)S(1)} %copy-done.2), kind=kOutput, calls=%fused_computation.1 | convolution fusion | flops 1415577600 | bytes 7151616 | tf_op jit(solution)/shard_map/dot_general | solution.py:60
  235.8 18.5 %all-to-all-done.2 = f32[8,24,2400]{2,1,0:T(8,128)S(1)} async-done(((f32[8,24,2400]{2,1,0:T(8,128)}), f32[8,24,2400]{2,1,0:T(8,128)S(1)}, u32[]{:S(2)}, u32[]{:S(2)}) %all-to-all-start.2) | async-done | bytes 1843232 | tf_op jit(solution)/shard_map/all_to_all | solution.py:65
  254.6 5.1 %fusion.4 = f32[8,8,3,512]{3,0,2,1:T(8,128)} fusion(f32[8,8,3,2400]{3,0,2,1:T(8,128)S(1)} %bitcast.123, f32[2400,512,1,1]{1,0,3,2:T(8,128)} %bitcast.118), kind=kOutput, calls=%fused_computation.27 | convolution fusion | flops 1415577600 | bytes 7151616 | tf_op jit(solution)/shard_map/dot_general | solution.py:67
  271.5 5.8 %copy.121 = f32[512,2400]{1,0:T(8,128)} copy(f32[512,2400]{0,1:T(8,128)} %bitcast.119) | data formatting | bytes 9830400 | tf_op jit(solution)/shard_map/dot_general | solution.py:67
  277.7 3.9 %all-to-all-done.3 = f32[8,8,2400]{2,1,0:T(8,128)S(1)} async-done(((f32[8,8,2400]{2,1,0:T(8,128)}), f32[8,8,2400]{2,1,0:T(8,128)S(1)}, u32[]{:S(2)}, u32[]{:S(2)}) %all-to-all-start.3) | async-done | bytes 614432 | tf_op jit(solution)/shard_map/all_to_all | solution.py:65
  281.8 6.3 %convolution_bitcast_fusion.8 = f32[8,4,2,1,8,64]{5,0,4,2,1,3:T(8,128)S(1)} fusion(f32[8,4,2,2400,1]{3,0,4,2,1:T(8,128)S(1)} %bitcast.121, f32[8,64,2400,1,1]{2,1,0,4,3:T(8,128)} %bitcast.105), kind=kOutput, calls=%fused_computation.9 | convolution fusion | flops 471859200 | bytes 5660672 | tf_op jit(solution)/shard_map/dot_general | solution.py:67
  296.7 38.8 %all-to-all-done.4 = f32[32,112,64]{1,2,0:T(8,128)} async-done(((f32[32,112,64]{1,2,0:T(8,128)}), f32[32,112,64]{1,2,0:T(8,128)}, u32[]{:S(2)}, u32[]{:S(2)}) %all-to-all-start.4) | async-done | bytes 917536 | tf_op jit(solution)/shard_map/all_to_all | solution.py:39
  348.8 10.3 %all-to-all-done.5 = f32[8,8,2400]{2,1,0:T(8,128)S(1)} async-done(((f32[8,8,2400]{2,1,0:T(8,128)}), f32[8,8,2400]{2,1,0:T(8,128)S(1)}, u32[]{:S(2)}, u32[]{:S(2)}) %all-to-all-start.5) | async-done | bytes 614432 | tf_op jit(solution)/shard_map/all_to_all | solution.py:65
  359.2 6.3 %convolution_bitcast_fusion.7 = f32[4,8,2,8,1,64]{5,3,1,2,0,4:T(8,128)S(1)} fusion(f32[8,4,2,2400,1]{3,0,4,2,1:T(8,128)S(1)} %bitcast.120, f32[8,64,2400,1,1]{2,1,0,4,3:T(8,128)} %bitcast.106), kind=kOutput, calls=%fused_computation.8 | convolution fusion | flops 471859200 | bytes 5660672 | tf_op jit(solution)/shard_map/dot_general | solution.py:67
  372.2 5.7 %concatenate.17 = f32[192,6400]{1,0:T(8,128)} concatenate(f32[192,2400]{1,0:T(8,128)S(1)} %copy-done.5, f32[192,2400]{1,0:T(8,128)} %convolution_bitcast_fusion.1, f32[192,800]{1,0:T(8,128)S(1)} %copy-done.7, f32[192,800]{1,0:T(8,128)} %convolution_bitcast_fusion.4), dimensions={1} | concatenate | bytes 9830400 | tf_op jit(solution)/shard_map/concatenate | solution.py:69
  (84 shorter events, 61.9 us)
Async XLA Ops:
  7.2 103.6 %all-gather.7.cloned.1.call-start = ((), (), s32[]{:S(2)}) async-start(), calls=%async_computation.8 | async-start | bytes 6225920 | tf_op jit(solution)/shard_map/all_gather | solution.py:48
  10.8 1.0 copy-start.2
  10.8 194.3 %all-gather.5.cloned.1.call-start = ((), (), s32[]{:S(2)}) async-start(), calls=%async_computation.7 | async-start | bytes 6225920 | tf_op jit(solution)/shard_map/all_gather | solution.py:48
  39.7 220.0 %copy-start = (f32[4,2,24,512]{3,2,1,0:T(8,128)}, f32[4,2,24,512]{3,2,1,0:T(8,128)S(1)}, u32[]{:S(2)}) copy-start(f32[4,2,24,512]{3,2,1,0:T(8,128)S(1)} %copy.112) | copy-start | bytes 1179652
  140.1 28.0 %all-to-all-start.1 = ((f32[8,24,2400]{2,1,0:T(8,128)}), f32[8,24,2400]{2,1,0:T(8,128)S(1)}, u32[]{:S(2)}, u32[]{:S(2)}) async-start(f32[8,24,2400]{2,1,0:T(8,128)} %reshape.144), calls=%async_computation.1 | async-start | bytes 3735552 | tf_op jit(solution)/shard_map/all_to_all | solution.py:65
  143.9 115.9 %all-gather.9.cloned.1.call-start = ((), (), s32[]{:S(2)}) async-start(), calls=%async_computation.9 | async-start | bytes 2293760 | tf_op jit(solution)/shard_map/all_gather | solution.py:48
  226.5 27.8 %all-to-all-start.2 = ((f32[8,24,2400]{2,1,0:T(8,128)}), f32[8,24,2400]{2,1,0:T(8,128)S(1)}, u32[]{:S(2)}, u32[]{:S(2)}) async-start(f32[8,24,2400]{2,1,0:T(8,128)} %reshape.148), calls=%async_computation.2 | async-start | bytes 3735552 | tf_op jit(solution)/shard_map/all_to_all | solution.py:65
  267.4 14.3 %all-to-all-start.3 = ((f32[8,8,2400]{2,1,0:T(8,128)}), f32[8,8,2400]{2,1,0:T(8,128)S(1)}, u32[]{:S(2)}, u32[]{:S(2)}) async-start(f32[8,8,2400]{2,1,0:T(8,128)} %reshape.150), calls=%async_computation.3 | async-start | bytes 1245184 | tf_op jit(solution)/shard_map/all_to_all | solution.py:65
  270.9 66.1 %all-gather.11.cloned.1.call-start = ((), (), s32[]{:S(2)}) async-start(), calls=%async_computation.10 | async-start | bytes 2293760 | tf_op jit(solution)/shard_map/all_gather | solution.py:48
  271.5 5.8 %copy-start.8 = (f32[8,8,3,512]{3,0,2,1:T(8,128)S(1)}, f32[8,8,3,512]{3,0,2,1:T(8,128)}, u32[]{:S(2)}) copy-start(f32[8,8,3,512]{3,0,2,1:T(8,128)} %fusion.3) | copy-start | bytes 1179652
  271.5 6.0 %copy-start.9 = (f32[8,8,3,512]{3,0,2,1:T(8,128)S(1)}, f32[8,8,3,512]{3,0,2,1:T(8,128)}, u32[]{:S(2)}) copy-start(f32[8,8,3,512]{3,0,2,1:T(8,128)} %fusion.4) | copy-start | bytes 1179652
  288.3 6.6 %copy-start.10 = (s32[96]{0:T(128)S(1)}, s32[96]{0:T(128)}, u32[]{:S(2)}) copy-start(s32[96]{0:T(128)} %param.8) | copy-start | bytes 1156
  288.3 6.7 %copy-start.3 = (f32[192,512]{1,0:T(8,128)S(1)}, f32[192,512]{1,0:T(8,128)}, u32[]{:S(2)}) copy-start(f32[192,512]{1,0:T(8,128)} %param.5) | copy-start | bytes 1179652
  290.5 4.6 %copy-start.6 = (f32[512,800]{1,0:T(8,128)S(1)}, f32[512,800]{1,0:T(8,128)}, u32[]{:S(2)}) copy-start(f32[512,800]{1,0:T(8,128)} %all-gather.9.cloned.1.call-done) | copy-start | bytes 4915204
  290.5 45.0 %all-to-all-start.4 = ((f32[32,112,64]{1,2,0:T(8,128)}), f32[32,112,64]{1,2,0:T(8,128)}, u32[]{:S(2)}, u32[]{:S(2)}) async-start(f32[32,112,64]{1,2,0:T(8,128)} %copy.125), calls=%async_computation.4 | async-start | bytes 2097152 | tf_op jit(solution)/shard_map/all_to_all | solution.py:39
  295.0 41.9 %copy-start.1 = (f32[4,2,24,512]{3,2,1,0:T(8,128)S(1)}, f32[4,2,24,512]{3,2,1,0:T(8,128)}, u32[]{:S(2)}) copy-start(f32[4,2,24,512]{3,2,1,0:T(8,128)} %copy-done) | copy-start | bytes 1179652
  344.6 14.4 %all-to-all-start.5 = ((f32[8,8,2400]{2,1,0:T(8,128)}), f32[8,8,2400]{2,1,0:T(8,128)S(1)}, u32[]{:S(2)}, u32[]{:S(2)}) async-start(f32[8,8,2400]{2,1,0:T(8,128)} %reshape.155), calls=%async_computation.5 | async-start | bytes 1245184 | tf_op jit(solution)/shard_map/all_to_all | solution.py:65
  359.2 9.8 %copy-start.4 = (f32[192,512]{1,0:T(8,128)S(1)}, f32[192,512]{1,0:T(8,128)}, u32[]{:S(2)}) copy-start(f32[192,512]{1,0:T(8,128)} %param.5) | copy-start | bytes 1179652
  365.6 6.6 %copy-start.5 = (f32[192,2400]{1,0:T(8,128)S(1)}, f32[192,2400]{1,0:T(8,128)}, u32[]{:S(2)}) copy-start(f32[192,2400]{1,0:T(8,128)} %fusion.2) | copy-start | bytes 5529604
  365.6 6.6 %copy-start.7 = (f32[192,800]{1,0:T(8,128)S(1)}, f32[192,800]{1,0:T(8,128)}, u32[]{:S(2)}) copy-start(f32[192,800]{1,0:T(8,128)} %convolution_bitcast_fusion.6) | copy-start | bytes 1843204
  366.4 11.5 %all-to-all-start.6 = ((f32[32,1,1024]{2,1,0:T(1,128)}), f32[32,1,1024]{2,1,0:T(1,128)S(1)}, u32[]{:S(2)}, u32[]{:S(2)}) async-start(f32[32,1,1024]{2,1,0:T(1,128)} %reshape.166), calls=%async_computation.6 | async-start | bytes 262144 | tf_op jit(solution)/shard_map/all_to_all | solution.py:39
Sparse Core Ops, SparseCore 0:
  11.0 99.7 all-gather.6
  112.3 92.8 all-gather.4
  206.8 39.7 all-gather.8
  273.0 59.3 all-gather.10

commit v14 on v12

--- a/solution.py
+++ b/solution.py
@@ -18,7 +18,7 @@
     slab = a_local * n_amp
     k_local, c_local, columns = cycle_integrals.shape
     if a_local >= 4:
-        sizes = [(a_local - 1) // 2, a_local - 2 - (a_local - 1) // 2, 1, 1]
+        sizes = [a_local - 3, 2, 1]
     elif a_local >= 2:
         sizes = [a_local - 1, 1]
     else:

time: 355 us -> 376 us (1.059)
  waiting for transfers between devices: 173 us -> 193 us
  local copies, waits for them, and re-layouts: 68 us -> 79.1 us
  matrix products: 50.8 us -> 44 us
    all_gather x4 -> x3, waiting for transfers between devices: 106 us -> 127 us  [per_device(): v_all = lax.all_gather(v, 'int', axis=0, tiled=True)]
    dot_general x2, local copies, waits for them, and re-layouts: 11.1 us -> 18.3 us  [per_device(): jnp.dot(t_cyc, v_all, precision=PRECISION, preferred_element_type=jnp.flo...]
    reshape x6 -> x4, local copies, waits for them, and re-layouts: 15.3 us -> 9.62 us  [per_device(): l_cyc.reshape(ibat, k_local, a_chunk, n_amp, c_local)]
    transpose x1, local copies, waits for them, and re-layouts: 5.63 us -> 10.7 us  [per_device(): l_cyc.reshape(ibat, k_local, a_chunk, n_amp, c_local)]
    all_to_all x4 -> x3, starting transfers between devices: 14.9 us -> 11.7 us  [per_device(): lax.all_to_all(l_cyc, 'amp', split_axis=0, concat_axis=0, tiled=True)]
    dot_general x4 -> x3, matrix products: 18.4 us -> 15.3 us  [per_device(): jnp.dot(moved, w2, precision=PRECISION, preferred_element_type=jnp.float32)]
    dot_general x4 -> x3, matrix products: 17.4 us -> 14.7 us  [per_device(): jnp.dot(amplitudes, v_all, precision=PRECISION, preferred_element_type=jn...]
    all_to_all x4 -> x3, waiting for transfers between devices: 50.6 us -> 49.5 us  [per_device(): lax.all_to_all(l_cyc, 'amp', split_axis=0, concat_axis=0, tiled=True)]
  transfers between devices with their start and end apart: 9 -> 7, of which waited for: 8 -> 5; matrix products, arithmetic and copies ran while one was open for 29% -> 28% of each run, Pallas kernels for 0% -> 0%
where the time goes in v14:
time: 376 us; the launch traced here: 374 us
  waiting for transfers between devices  193 us (51%)
  local copies, waits for them, and re-layouts  79.1 us (21%)
  matrix products  44 us (12%)
  blocking collectives  26.4 us (7%)
  starting transfers between devices  15.4 us (4%)
  between operations  13.9 us (4%)
    all_gather x3, waiting for transfers between devices, per_device(): v_all = lax.all_gather(v, 'int', axis=0, tiled=True)  127 us
    all_to_all x3, waiting for transfers between devices, per_device(): lax.all_to_all(l_cyc, 'amp', split_axis=0, concat_axis=0, tiled=True)  49.5 us
    all_to_all x1, blocking collectives, per_device(): lax.all_to_all(amplitudes.reshape(i_local, nocc, pw), 'int', split_axis=1...  26.4 us
    reshape x3, local copies, waits for them, and re-layouts, per_device(): l_cyc = l_cyc.reshape(n_amp, ibat * a_chunk, c_local * k_local)  18.7 us
    dot_general x2, local copies, waits for them, and re-layouts, per_device(): jnp.dot(t_cyc, v_all, precision=PRECISION, preferred_element_type=jnp.flo...  18.3 us
    all_to_all x1, waiting for transfers between devices, per_device(): lax.all_to_all(parts, ('int', 'amp'), split_axis=0, concat_axis=0, tiled=...  16.3 us
    dot_general x3, matrix products, per_device(): jnp.dot(moved, w2, precision=PRECISION, preferred_element_type=jnp.float32)  15.3 us
    dot_general x3, matrix products, per_device(): jnp.dot(amplitudes, v_all, precision=PRECISION, preferred_element_type=jn...  14.7 us
  transfers between devices with their start and end apart: 7, of which 5 were waited for; matrix products, arithmetic and copies ran while one was open for 28% of the time, Pallas kernels for 0%

profile of v14, /device:TPU:0, one launch (start us, length us, event | category | flops | bytes accessed | tf_op | source)
XLA Modules:
  0.0 374.2 jit_solution(3203376121363250753)
XLA Ops:
  13.2 26.4 %all_to_all.35 = f32[2,96,512]{2,0,1:T(2,128)S(1)} all-to-all(f32[2,96,512]{2,0,1:T(2,128)S(1)} %copy.48), channel_id=1, replica_groups=mesh['amp'=8,'int'=4] {'int'}, dimensions={1} | all-to-all | bytes 786432 | tf_op jit(solution)/shard_map/all_to_all | solution.py:29
  39.7 126.8 %all-gather.6.cloned.1.call-done = f32[512,4000]{1,0:T(8,128)} async-done(((f32[128,4000]{1,0:T(8,128)}), f32[512,4000]{1,0:T(8,128)}) %all-gather.6.cloned.1.call-update) | async-done | bytes 8192016 | tf_op jit(solution)/shard_map/all_gather | solution.py:39
  166.6 9.1 %copy.51 = f32[4000,512]{1,0:T(8,128)} copy(f32[4000,512]{0,1:T(8,128)} %bitcast.61) | data formatting | bytes 16384000 | tf_op jit(solution)/shard_map/dot_general | solution.py:47
  175.6 9.3 %reshape.128 = f32[5,8,100,512,1]{3,2,1,0,4:T(8,128)} reshape(f32[4000,512]{1,0:T(8,128)} %copy.51) | data formatting | bytes 16384000 | tf_op jit(solution)/shard_map/dot_general | solution.py:47
  184.9 8.4 %convolution_bitcast_fusion.2 = f32[8,8,5,100,24]{3,4,0,2,1:T(8,128)} fusion(f32[8,24,512,1,1]{2,1,4,3,0:T(8,128)S(1)} %bitcast.68, f32[5,8,100,512,1]{3,2,1,0,4:T(8,128)} %reshape.128), kind=kOutput, calls=%fused_computation.2 | convolution fusion | flops 2359296000 | bytes 11657216 | tf_op jit(solution)/shard_map/dot_general | solution.py:47
  193.3 10.7 %copy.52 = f32[8,8,5,100,24]{4,3,2,1,0:T(8,128)} copy(f32[8,8,5,100,24]{3,4,0,2,1:T(8,128)} %convolution_bitcast_fusion.2) | data formatting | bytes 6144000 | tf_op jit(solution)/shard_map/transpose | solution.py:48
  204.0 11.3 %reshape.114 = f32[8,40,2400]{2,1,0:T(8,128)} reshape(f32[8,8,5,100,24]{4,3,2,1,0:T(8,128)} %copy.52) | data formatting | bytes 6144000 | tf_op jit(solution)/shard_map/reshape | solution.py:49
  215.3 3.7 all-to-all-start.1
  221.2 8.1 %fusion = f32[192,4000]{1,0:T(8,128)} fusion(f32[192,512]{1,0:T(8,128)S(1)} %copy-done.2, f32[512,4000]{1,0:T(8,128)} %all-gather.6.cloned.1.call-done), kind=kOutput, calls=%fused_computation.19 | convolution fusion | flops 2359296000 | bytes 11657216 | tf_op jit(solution)/shard_map/dot_general | solution.py:45
  229.3 27.1 %all-to-all-done.1 = f32[8,40,2400]{2,1,0:T(8,128)S(1)} async-done(((f32[8,40,2400]{2,1,0:T(8,128)}), f32[8,40,2400]{2,1,0:T(8,128)S(1)}, u32[]{:S(2)}, u32[]{:S(2)}) %all-to-all-start.1) | async-done | bytes 3072032 | tf_op jit(solution)/shard_map/all_to_all | solution.py:50
  256.4 6.3 %fusion.1 = f32[320,512]{1,0:T(8,128)} fusion(f32[320,2400]{1,0:T(8,128)S(1)} %bitcast.64, f32[2400,512]{1,0:T(8,128)} %bitcast.58), kind=kOutput, calls=%fused_computation.20 | convolution fusion | flops 2359296000 | bytes 8642560 | tf_op jit(solution)/shard_map/dot_general | solution.py:53
  267.5 4.6 %copy.54 = f32[8,24,2,8,100]{1,4,2,0,3:T(8,128)} copy(f32[8,24,2,8,100]{4,3,2,1,0:T(8,128)S(1)} %reshape.118) | data formatting | bytes 2457600 | tf_op jit(solution)/shard_map/reshape | solution.py:48
  272.1 5.7 %reshape.119 = f32[8,16,2400]{2,1,0:T(8,128)} reshape(f32[8,8,2,100,24]{4,3,2,1,0:T(8,128)} %bitcast.62) | data formatting | bytes 2457600 | tf_op jit(solution)/shard_map/reshape | solution.py:49
  277.8 4.5 %all-to-all-start.2 = ((f32[8,16,2400]{2,1,0:T(8,128)}), f32[8,16,2400]{2,1,0:T(8,128)}, u32[]{:S(2)}, u32[]{:S(2)}) async-start(f32[8,16,2400]{2,1,0:T(8,128)} %reshape.119), calls=%async_computation.2 | async-start | bytes 2490368 | tf_op jit(solution)/shard_map/all_to_all | solution.py:50
  282.3 3.4 convolution_bitcast_fusion.1
  285.7 13.9 %all-to-all-done.2 = f32[8,16,2400]{2,1,0:T(8,128)} async-done(((f32[8,16,2400]{2,1,0:T(8,128)}), f32[8,16,2400]{2,1,0:T(8,128)}, u32[]{:S(2)}, u32[]{:S(2)}) %all-to-all-start.2) | async-done | bytes 1228832 | tf_op jit(solution)/shard_map/all_to_all | solution.py:50
  299.6 5.0 %fusion.2 = f32[128,512]{1,0:T(8,128)} fusion(f32[128,2400]{1,0:T(8,128)} %bitcast.16, f32[2400,512]{1,0:T(8,128)} %bitcast.59), kind=kOutput, calls=%fused_computation.21 | convolution fusion | flops 943718400 | bytes 6406144 | tf_op jit(solution)/shard_map/dot_general | solution.py:53
  312.2 3.5 all-to-all-start.3
  318.0 8.4 %all-to-all-done.3 = f32[8,8,2400]{2,1,0:T(8,128)S(1)} async-done(((f32[8,8,2400]{2,1,0:T(8,128)}), f32[8,8,2400]{2,1,0:T(8,128)S(1)}, u32[]{:S(2)}, u32[]{:S(2)}) %all-to-all-start.3) | async-done | bytes 614432 | tf_op jit(solution)/shard_map/all_to_all | solution.py:50
  326.5 4.0 %convolution_bitcast_fusion.5 = f32[8,8,1,512]{3,1,0,2:T(8,128)S(1)} fusion(f32[8,8,2400]{2,1,0:T(8,128)S(1)} %all-to-all-done.3, f32[2400,512,1]{1,0,2:T(8,128)} %bitcast.60), kind=kOutput, calls=%fused_computation.5 | convolution fusion | flops 471859200 | bytes 5660672 | tf_op jit(solution)/shard_map/dot_general | solution.py:53
  332.8 3.3 copy.58
  336.1 3.4 all-to-all-start.4
  344.0 5.4 %concatenate.6 = f32[192,6400]{1,0:T(8,128)} concatenate(f32[192,4000]{1,0:T(8,128)S(1)} %copy-done.1, f32[192,1600]{1,0:T(8,128)} %convolution_bitcast_fusion.1, f32[192,800]{1,0:T(8,128)} %convolution_bitcast_fusion.4), dimensions={1} | concatenate | bytes 9830400 | tf_op jit(solution)/shard_map/concatenate | solution.py:55
  349.4 16.3 %all-to-all-done.4 = f32[32,128,64]{1,2,0:T(8,128)} async-done(((f32[32,128,64]{1,2,0:T(8,128)}), f32[32,128,64]{1,2,0:T(8,128)}, u32[]{:S(2)}, u32[]{:S(2)}) %all-to-all-start.4) | async-done | bytes 1048608 | tf_op jit(solution)/shard_map/all_to_all | solution.py:63
  (53 shorter events, 31.7 us)
Async XLA Ops:
  7.2 5.7 %copy-start.2 = (f32[192,512]{1,0:T(8,128)S(1)}, f32[192,512]{1,0:T(8,128)}, u32[]{:S(2)}) copy-start(f32[192,512]{1,0:T(8,128)} %param.5) | copy-start | bytes 1179652
  7.2 159.4 %all-gather.6.cloned.1.call-start = ((), (), s32[]{:S(2)}) async-start(), calls=%async_computation.6 | async-start | bytes 10485760 | tf_op jit(solution)/shard_map/all_gather | solution.py:39
  10.4 252.3 %all-gather.4.cloned.1.call-start = ((), (), s32[]{:S(2)}) async-start(), calls=%async_computation.5 | async-start | bytes 4259840 | tf_op jit(solution)/shard_map/all_gather | solution.py:39
  39.7 145.2 %copy-start.4 = (f32[4,2,24,512]{3,2,1,0:T(8,128)}, f32[4,2,24,512]{3,2,1,0:T(8,128)S(1)}, u32[]{:S(2)}) copy-start(f32[4,2,24,512]{3,2,1,0:T(8,128)S(1)} %copy.50) | copy-start | bytes 1179652
  215.3 41.1 %all-to-all-start.1 = ((f32[8,40,2400]{2,1,0:T(8,128)}), f32[8,40,2400]{2,1,0:T(8,128)S(1)}, u32[]{:S(2)}, u32[]{:S(2)}) async-start(f32[8,40,2400]{2,1,0:T(8,128)} %reshape.114), calls=%async_computation.1 | async-start | bytes 6225920 | tf_op jit(solution)/shard_map/all_to_all | solution.py:50
  219.0 85.6 %all-gather.8.cloned.1.call-start = ((), (), s32[]{:S(2)}) async-start(), calls=%async_computation.7 | async-start | bytes 2293760 | tf_op jit(solution)/shard_map/all_gather | solution.py:39
  256.4 6.3 %copy-start.5 = (f32[4,2,24,512]{3,2,1,0:T(8,128)S(1)}, f32[4,2,24,512]{3,2,1,0:T(8,128)}, u32[]{:S(2)}) copy-start(f32[4,2,24,512]{3,2,1,0:T(8,128)} %copy-done.4) | copy-start | bytes 1179652
  272.1 10.2 %copy-start = (f32[512,1600]{1,0:T(8,128)S(1)}, f32[512,1600]{1,0:T(8,128)}, u32[]{:S(2)}) copy-start(f32[512,1600]{1,0:T(8,128)} %all-gather.4.cloned.1.call-done) | copy-start | bytes 9830404
  277.8 21.8 %all-to-all-start.2 = ((f32[8,16,2400]{2,1,0:T(8,128)}), f32[8,16,2400]{2,1,0:T(8,128)}, u32[]{:S(2)}, u32[]{:S(2)}) async-start(f32[8,16,2400]{2,1,0:T(8,128)} %reshape.119), calls=%async_computation.2 | async-start | bytes 2490368 | tf_op jit(solution)/shard_map/all_to_all | solution.py:50
  285.7 18.9 %copy-start.6 = (f32[4,2,24,512]{3,2,1,0:T(8,128)S(1)}, f32[4,2,24,512]{3,2,1,0:T(8,128)}, u32[]{:S(2)}) copy-start(f32[4,2,24,512]{3,2,1,0:T(8,128)} %copy-done.4) | copy-start | bytes 1179652
  312.2 14.3 %all-to-all-start.3 = ((f32[8,8,2400]{2,1,0:T(8,128)}), f32[8,8,2400]{2,1,0:T(8,128)S(1)}, u32[]{:S(2)}, u32[]{:S(2)}) async-start(f32[8,8,2400]{2,1,0:T(8,128)} %reshape.124), calls=%async_computation.3 | async-start | bytes 1245184 | tf_op jit(solution)/shard_map/all_to_all | solution.py:50
  332.8 7.4 %copy-start.7 = (s32[96]{0:T(128)S(1)}, s32[96]{0:T(128)}, u32[]{:S(2)}) copy-start(s32[96]{0:T(128)} %param.8) | copy-start | bytes 1156
  332.8 8.0 %copy-start.3 = (f32[192,512]{1,0:T(8,128)S(1)}, f32[192,512]{1,0:T(8,128)}, u32[]{:S(2)}) copy-start(f32[192,512]{1,0:T(8,128)} %param.5) | copy-start | bytes 1179652
  332.8 11.2 %copy-start.1 = (f32[192,4000]{1,0:T(8,128)S(1)}, f32[192,4000]{1,0:T(8,128)}, u32[]{:S(2)}) copy-start(f32[192,4000]{1,0:T(8,128)} %fusion) | copy-start | bytes 9216004
  336.1 29.6 %all-to-all-start.4 = ((f32[32,128,64]{1,2,0:T(8,128)}), f32[32,128,64]{1,2,0:T(8,128)}, u32[]{:S(2)}, u32[]{:S(2)}) async-start(f32[32,128,64]{1,2,0:T(8,128)} %bitcast.67), calls=%async_computation.4 | async-start | bytes 2097152 | tf_op jit(solution)/shard_map/all_to_all | solution.py:63
Sparse Core Ops, SparseCore 0:
  10.5 156.0 all-gather.5
  168.1 66.9 all-gather.3
  236.7 39.9 all-gather.7

commit v15 on v12

--- a/solution.py
+++ b/solution.py
@@ -58,10 +58,11 @@
         [c.reshape(n_amp, ibat, sizes[t], columns) for t, c in enumerate(cycle_chunks)], axis=2
     )
     col_local = columns // n_amp
-    parts = parts.transpose(1, 0, 2, 3).reshape(n_int, i_local * slab, n_amp, col_local)
-    parts = parts.transpose(0, 2, 1, 3).reshape(n_int * n_amp, i_local * slab, col_local)
-    gathered = lax.all_to_all(parts, ("int", "amp"), split_axis=0, concat_axis=0, tiled=True)
-    sums = jnp.sum(gathered, axis=0)
+    parts = parts.reshape(n_amp, ibat, a_local, n_amp, col_local).transpose(3, 0, 1, 2, 4)
+    parts = jnp.sum(lax.all_to_all(parts, "amp", split_axis=0, concat_axis=0, tiled=True), axis=0)
+    parts = parts.reshape(n_amp, n_int, i_local, a_local, col_local).transpose(1, 2, 0, 3, 4)
+    parts = jnp.sum(lax.all_to_all(parts, "int", split_axis=0, concat_axis=0, tiled=True), axis=0)
+    sums = parts.reshape(i_local * slab, col_local)
 
     row_start = lax.axis_index("int") * i_local
     batch_labels = lax.dynamic_slice_in_dim(occ_irrep, row_start, i_local, 0)

time: 355 us -> 372 us (1.048); the launches traced: 354 us -> 366 us
  local copies, waits for them, and re-layouts: 68 us -> 78 us
  waiting for transfers between devices: 173 us -> 164 us
  other arithmetic: 1.68 us -> 6.04 us
  starting transfers between devices: 18.2 us -> 22.3 us
    all_to_all x4, waiting for transfers between devices: 50.6 us -> 43.6 us  [per_device(): lax.all_to_all(l_cyc, 'amp', split_axis=0, concat_axis=0, tiled=True)]
    dot_general x1 -> x2, local copies, waits for them, and re-layouts: 0.14 us -> 6.07 us  [per_device(): jnp.dot(moved, w2, precision=PRECISION, preferred_element_type=jnp.float32)]
    unnamed x14 -> x27, local copies, waits for them, and re-layouts: 0.25 us -> 5.48 us
    all_to_all x0 -> x2, other arithmetic: none -> 4.11 us  [the longest x1 3.13 us: per_device(): lax.all_to_all(parts, 'amp', split_axis=0, concat_axis=0, tiled=True)]
    all_to_all x1 -> x2, starting transfers between devices: 2.78 us -> 6.88 us  [the longest x1 3.56 us: per_device(): lax.all_to_all(parts, 'amp', split_axis=0, concat_axis=0, tiled=True)]
    all_to_all x1 -> x2, waiting for transfers between devices: 15.7 us -> 14 us  [the longest x1 14 us: per_device(): lax.all_to_all(parts, 'amp', split_axis=0, concat_axis=0, tiled=True)]
  transfers between devices with their start and end apart: 9 -> 10, of which waited for: 8 -> 8; matrix products, arithmetic and copies ran while one was open for 29% -> 30% of each run, Pallas kernels for 0% -> 0%
where the time goes in v15:
time: 372 us; the launch traced here: 366 us
  waiting for transfers between devices  164 us (44%)
  local copies, waits for them, and re-layouts  78 us (21%)
  matrix products  53.9 us (14%)
  blocking collectives  27.5 us (7%)
  starting transfers between devices  22.3 us (6%)
  between operations  14.5 us (4%)
  other arithmetic  6.04 us (2%)
    all_gather x4, waiting for transfers between devices, per_device(): v_all = lax.all_gather(v, 'int', axis=0, tiled=True)  105 us
    all_to_all x4, waiting for transfers between devices, per_device(): lax.all_to_all(l_cyc, 'amp', split_axis=0, concat_axis=0, tiled=True)  43.6 us
    all_to_all x1, blocking collectives, per_device(): lax.all_to_all(amplitudes.reshape(i_local, nocc, pw), 'int', split_axis=1...  27.5 us
    dot_general x4, matrix products, per_device(): jnp.dot(moved, w2, precision=PRECISION, preferred_element_type=jnp.float32)  21.4 us
    reshape x4, local copies, waits for them, and re-layouts, per_device(): l_cyc = l_cyc.reshape(n_amp, ibat * a_chunk, c_local * k_local)  18.7 us
    dot_general x4, matrix products, per_device(): jnp.dot(amplitudes, v_all, precision=PRECISION, preferred_element_type=jn...  17.5 us
    reshape x6, local copies, waits for them, and re-layouts, per_device(): l_cyc.reshape(ibat, k_local, a_chunk, n_amp, c_local)  15.2 us
    dot_general x4, matrix products, per_device(): jnp.dot(t_cyc, v_all, precision=PRECISION, preferred_element_type=jnp.flo...  15 us
  transfers between devices with their start and end apart: 10, of which 8 were waited for; matrix products, arithmetic and copies ran while one was open for 30% of the time, Pallas kernels for 0%

profile of v15, /device:TPU:0, one launch (start us, length us, event | category | flops | bytes accessed | tf_op | source)
XLA Modules:
  0.0 366.3 jit_solution(6203085691384477026)
XLA Ops:
  12.1 27.5 %all_to_all.45 = f32[2,96,512]{2,0,1:T(2,128)S(1)} all-to-all(f32[2,96,512]{2,0,1:T(2,128)S(1)} %copy.80), channel_id=1, replica_groups=mesh['amp'=8,'int'=4] {'int'}, dimensions={1} | all-to-all | bytes 786432 | tf_op jit(solution)/shard_map/all_to_all | solution.py:29
  39.7 71.0 %all-gather.7.cloned.1.call-done = f32[512,2400]{1,0:T(8,128)} async-done(((f32[128,2400]{1,0:T(8,128)}), f32[512,2400]{1,0:T(8,128)}) %all-gather.7.cloned.1.call-update) | async-done | bytes 4915216 | tf_op jit(solution)/shard_map/all_gather | solution.py:39
  110.7 5.7 %copy.83 = f32[2400,512]{1,0:T(8,128)} copy(f32[2400,512]{0,1:T(8,128)} %bitcast.91) | data formatting | bytes 9830400 | tf_op jit(solution)/shard_map/dot_general | solution.py:47
  116.4 5.4 %reshape.151 = f32[3,8,100,512,1]{3,2,1,0,4:T(8,128)} reshape(f32[2400,512]{1,0:T(8,128)} %copy.83) | data formatting | bytes 9830400 | tf_op jit(solution)/shard_map/dot_general | solution.py:47
  121.9 4.9 %convolution_bitcast_fusion.2 = f32[8,8,3,100,24]{3,4,0,2,1:T(8,128)S(1)} fusion(f32[8,24,512,1,1]{2,1,4,3,0:T(8,128)S(1)} %bitcast.95, f32[3,8,100,512,1]{3,2,1,0,4:T(8,128)} %reshape.151), kind=kOutput, calls=%fused_computation.3 | convolution fusion | flops 1415577600 | bytes 7151616 | tf_op jit(solution)/shard_map/dot_general | solution.py:47
  126.8 5.6 %copy.84 = f32[8,8,3,100,24]{4,3,2,1,0:T(8,128)} copy(f32[8,8,3,100,24]{3,4,0,2,1:T(8,128)S(1)} %convolution_bitcast_fusion.2) | data formatting | bytes 3686400 | tf_op jit(solution)/shard_map/transpose | solution.py:48
  132.4 7.6 %reshape.135 = f32[8,24,2400]{2,1,0:T(8,128)} reshape(f32[8,8,3,100,24]{4,3,2,1,0:T(8,128)} %copy.84) | data formatting | bytes 3686400 | tf_op jit(solution)/shard_map/reshape | solution.py:49
  146.5 5.6 %fusion.5 = f32[192,2400]{1,0:T(8,128)} fusion(f32[192,512]{1,0:T(8,128)S(1)} %copy-done.2, f32[512,2400]{1,0:T(8,128)} %all-gather.7.cloned.1.call-done), kind=kOutput, calls=%fused_computation.28 | convolution fusion | flops 1415577600 | bytes 7151616 | tf_op jit(solution)/shard_map/dot_general | solution.py:45
  152.1 15.9 %all-to-all-done.1 = f32[8,24,2400]{2,1,0:T(8,128)S(1)} async-done(((f32[8,24,2400]{2,1,0:T(8,128)}), f32[8,24,2400]{2,1,0:T(8,128)S(1)}, u32[]{:S(2)}, u32[]{:S(2)}) %all-to-all-start.1) | async-done | bytes 1843232 | tf_op jit(solution)/shard_map/all_to_all | solution.py:50
  168.0 5.1 %fusion.6 = f32[192,512]{1,0:T(8,128)} fusion(f32[192,2400]{1,0:T(8,128)S(1)} %bitcast.100, f32[2400,512]{1,0:T(8,128)} %bitcast.86), kind=kOutput, calls=%fused_computation.29 | convolution fusion | flops 1415577600 | bytes 7151616 | tf_op jit(solution)/shard_map/dot_general | solution.py:53
  173.1 32.1 %all-gather.5.cloned.1.call-done = f32[512,2400]{1,0:T(8,128)} async-done(((f32[128,2400]{1,0:T(8,128)}), f32[512,2400]{1,0:T(8,128)}) %all-gather.5.cloned.1.call-update) | async-done | bytes 4915216 | tf_op jit(solution)/shard_map/all_gather | solution.py:39
  205.2 5.5 %convolution_bitcast_fusion = f32[192,2400]{1,0:T(8,128)} fusion(f32[512,2400]{1,0:T(8,128)} %all-gather.5.cloned.1.call-done, f32[192,512]{1,0:T(8,128)S(1)} %bitcast.96), kind=kOutput, calls=%fused_computation | convolution fusion | flops 1415577600 | bytes 7151616 | tf_op jit(solution)/shard_map/dot_general | solution.py:47
  213.3 5.6 %copy.86 = f32[8,24,3,8,100]{1,4,2,0,3:T(8,128)} copy(f32[8,24,3,8,100]{4,3,2,1,0:T(8,128)S(1)} %reshape.139) | data formatting | bytes 3686400 | tf_op jit(solution)/shard_map/reshape | solution.py:48
  218.9 7.5 %reshape.140 = f32[8,24,2400]{2,1,0:T(8,128)} reshape(f32[8,8,3,100,24]{4,3,2,1,0:T(8,128)} %bitcast.90) | data formatting | bytes 3686400 | tf_op jit(solution)/shard_map/reshape | solution.py:49
  230.6 5.5 %convolution_bitcast_fusion.1 = f32[192,2400]{1,0:T(8,128)} fusion(f32[512,2400]{1,0:T(8,128)} %all-gather.5.cloned.1.call-done, f32[192,512]{1,0:T(8,128)S(1)} %copy-done.2), kind=kOutput, calls=%fused_computation.1 | convolution fusion | flops 1415577600 | bytes 7151616 | tf_op jit(solution)/shard_map/dot_general | solution.py:45
  236.1 18.1 %all-to-all-done.2 = f32[8,24,2400]{2,1,0:T(8,128)S(1)} async-done(((f32[8,24,2400]{2,1,0:T(8,128)}), f32[8,24,2400]{2,1,0:T(8,128)S(1)}, u32[]{:S(2)}, u32[]{:S(2)}) %all-to-all-start.2) | async-done | bytes 1843232 | tf_op jit(solution)/shard_map/all_to_all | solution.py:50
  254.2 5.3 %fusion.7 = f32[192,512]{1,0:T(8,128)} fusion(f32[192,2400]{1,0:T(8,128)S(1)} %bitcast.101, f32[2400,512]{1,0:T(8,128)} %bitcast.87), kind=kOutput, calls=%fused_computation.30 | convolution fusion | flops 1415577600 | bytes 7151616 | tf_op jit(solution)/shard_map/dot_general | solution.py:53
  273.9 7.5 %all-to-all-done.3 = f32[8,8,2400]{2,1,0:T(8,128)S(1)} async-done(((f32[8,8,2400]{2,1,0:T(8,128)}), f32[8,8,2400]{2,1,0:T(8,128)S(1)}, u32[]{:S(2)}, u32[]{:S(2)}) %all-to-all-start.3) | async-done | bytes 614432 | tf_op jit(solution)/shard_map/all_to_all | solution.py:50
  281.4 4.7 %fusion.1 = f32[64,512]{1,0:T(8,128)} fusion(f32[2400,512]{1,0:T(8,128)} %bitcast.88, f32[8,8,2400]{2,1,0:T(8,128)S(1)} %all-to-all-done.3), kind=kOutput, calls=%fused_computation.10 | convolution fusion | flops 471859200 | bytes 5660672 | tf_op jit(solution)/shard_map/dot_general | solution.py:53
  295.9 3.9 %all-to-all-start.4 = ((f32[8,8,2400]{2,1,0:T(8,128)}), f32[8,8,2400]{2,1,0:T(8,128)S(1)}, u32[]{:S(2)}, u32[]{:S(2)}) async-start(f32[8,8,2400]{2,1,0:T(8,128)} %reshape.146), calls=%async_computation.4 | async-start | bytes 1245184 | tf_op jit(solution)/shard_map/all_to_all | solution.py:50
  299.8 5.8 %copy.89 = f32[512,2400]{1,0:T(8,128)} copy(f32[512,2400]{0,1:T(8,128)} %bitcast.89) | data formatting | bytes 9830400 | tf_op jit(solution)/shard_map/dot_general | solution.py:53
  310.6 6.4 %convolution_bitcast_fusion.7 = f32[8,8,1,8,64]{4,1,3,0,2:T(8,128)S(1)} fusion(f32[8,64,2400,1]{2,1,0,3:T(8,128)} %bitcast.92, f32[8,8,2400]{2,1,0:T(8,128)S(1)} %all-to-all-done.4), kind=kOutput, calls=%fused_computation.8 | convolution fusion | flops 471859200 | bytes 5660672 | tf_op jit(solution)/shard_map/dot_general | solution.py:53
  325.4 14.0 %all-to-all-done.5 = f32[8,1,32768]{2,1,0:T(1,128)S(1)} async-done(((f32[8,1,32768]{2,1,0:T(1,128)}), f32[8,1,32768]{2,1,0:T(1,128)S(1)}, u32[]{:S(2)}, u32[]{:S(2)}) %all-to-all-start.5) | async-done | bytes 1048608 | tf_op jit(solution)/shard_map/all_to_all | solution.py:62
  351.6 5.7 %concatenate.13 = f32[192,6400]{1,0:T(8,128)} concatenate(f32[192,2400]{1,0:T(8,128)S(1)} %copy-done.4, f32[192,2400]{1,0:T(8,128)} %convolution_bitcast_fusion.1, f32[192,800]{1,0:T(8,128)S(1)} %copy-done.6, f32[192,800]{1,0:T(8,128)} %convolution_bitcast_fusion.4), dimensions={1} | concatenate | bytes 9830400 | tf_op jit(solution)/shard_map/concatenate | solution.py:55
  (84 shorter events, 69.9 us)
Async XLA Ops:
  7.2 103.6 %all-gather.7.cloned.1.call-start = ((), (), s32[]{:S(2)}) async-start(), calls=%async_computation.8 | async-start | bytes 6225920 | tf_op jit(solution)/shard_map/all_gather | solution.py:39
  10.8 1.0 copy-start.2
  10.8 194.3 %all-gather.5.cloned.1.call-start = ((), (), s32[]{:S(2)}) async-start(), calls=%async_computation.7 | async-start | bytes 6225920 | tf_op jit(solution)/shard_map/all_gather | solution.py:39
  39.7 219.8 %copy-start = (f32[4,2,24,512]{3,2,1,0:T(8,128)}, f32[4,2,24,512]{3,2,1,0:T(8,128)S(1)}, u32[]{:S(2)}) copy-start(f32[4,2,24,512]{3,2,1,0:T(8,128)S(1)} %copy.82) | copy-start | bytes 1179652
  140.0 28.0 %all-to-all-start.1 = ((f32[8,24,2400]{2,1,0:T(8,128)}), f32[8,24,2400]{2,1,0:T(8,128)S(1)}, u32[]{:S(2)}, u32[]{:S(2)}) async-start(f32[8,24,2400]{2,1,0:T(8,128)} %reshape.135), calls=%async_computation.1 | async-start | bytes 3735552 | tf_op jit(solution)/shard_map/all_to_all | solution.py:50
  143.8 115.7 %all-gather.9.cloned.1.call-start = ((), (), s32[]{:S(2)}) async-start(), calls=%async_computation.9 | async-start | bytes 2293760 | tf_op jit(solution)/shard_map/all_gather | solution.py:39
  226.4 27.8 %all-to-all-start.2 = ((f32[8,24,2400]{2,1,0:T(8,128)}), f32[8,24,2400]{2,1,0:T(8,128)S(1)}, u32[]{:S(2)}, u32[]{:S(2)}) async-start(f32[8,24,2400]{2,1,0:T(8,128)} %reshape.140), calls=%async_computation.2 | async-start | bytes 3735552 | tf_op jit(solution)/shard_map/all_to_all | solution.py:50
  230.0 58.3 %all-gather.11.cloned.1.call-start = ((), (), s32[]{:S(2)}) async-start(), calls=%async_computation.10 | async-start | bytes 2293760 | tf_op jit(solution)/shard_map/all_gather | solution.py:39
  267.1 14.3 %all-to-all-start.3 = ((f32[8,8,2400]{2,1,0:T(8,128)}), f32[8,8,2400]{2,1,0:T(8,128)S(1)}, u32[]{:S(2)}, u32[]{:S(2)}) async-start(f32[8,8,2400]{2,1,0:T(8,128)} %reshape.143), calls=%async_computation.3 | async-start | bytes 1245184 | tf_op jit(solution)/shard_map/all_to_all | solution.py:50
  273.9 14.5 %copy-start.1 = (f32[4,2,24,512]{3,2,1,0:T(8,128)S(1)}, f32[4,2,24,512]{3,2,1,0:T(8,128)}, u32[]{:S(2)}) copy-start(f32[4,2,24,512]{3,2,1,0:T(8,128)} %copy-done) | copy-start | bytes 1179652
  295.9 14.7 %all-to-all-start.4 = ((f32[8,8,2400]{2,1,0:T(8,128)}), f32[8,8,2400]{2,1,0:T(8,128)S(1)}, u32[]{:S(2)}, u32[]{:S(2)}) async-start(f32[8,8,2400]{2,1,0:T(8,128)} %reshape.146), calls=%async_computation.4 | async-start | bytes 1245184 | tf_op jit(solution)/shard_map/all_to_all | solution.py:50
  299.8 5.8 %copy-start.7 = (f32[192,512]{1,0:T(8,128)S(1)}, f32[192,512]{1,0:T(8,128)}, u32[]{:S(2)}) copy-start(f32[192,512]{1,0:T(8,128)} %fusion.6) | copy-start | bytes 1179652
  305.7 1.0 copy-start.8
  305.8 2.3 copy-start.9
  310.6 6.6 %copy-start.5 = (f32[8,8,3,8,64]{4,2,1,0,3:T(4,128)S(1)}, f32[8,8,3,8,64]{4,2,1,0,3:T(4,128)}, u32[]{:S(2)}) copy-start(f32[8,8,3,8,64]{4,2,1,0,3:T(4,128)} %copy.91) | copy-start | bytes 1179652
  318.4 6.4 %copy-start.10 = (s32[96]{0:T(128)S(1)}, s32[96]{0:T(128)}, u32[]{:S(2)}) copy-start(s32[96]{0:T(128)} %param.8) | copy-start | bytes 1156
  320.6 18.9 %all-to-all-start.5 = ((f32[8,1,32768]{2,1,0:T(1,128)}), f32[8,1,32768]{2,1,0:T(1,128)S(1)}, u32[]{:S(2)}, u32[]{:S(2)}) async-start(f32[8,1,32768]{2,1,0:T(1,128)} %reshape.155), calls=%async_computation.5 | async-start | bytes 2097152 | tf_op jit(solution)/shard_map/all_to_all | solution.py:62
  344.0 4.5 %copy-start.3 = (f32[192,512]{1,0:T(8,128)S(1)}, f32[192,512]{1,0:T(8,128)}, u32[]{:S(2)}) copy-start(f32[192,512]{1,0:T(8,128)} %param.5) | copy-start | bytes 1179652
  344.2 7.4 %copy-start.4 = (f32[192,2400]{1,0:T(8,128)S(1)}, f32[192,2400]{1,0:T(8,128)}, u32[]{:S(2)}) copy-start(f32[192,2400]{1,0:T(8,128)} %fusion.5) | copy-start | bytes 5529604
  344.2 7.4 %copy-start.6 = (f32[192,800]{1,0:T(8,128)S(1)}, f32[192,800]{1,0:T(8,128)}, u32[]{:S(2)}) copy-start(f32[192,800]{1,0:T(8,128)} %convolution_bitcast_fusion.6) | copy-start | bytes 1843204
  345.1 12.2 %all-to-all-start.6 = ((f32[4,1,8192]{2,1,0:T(1,128)}), f32[4,1,8192]{2,1,0:T(1,128)S(1)}, u32[]{:S(2)}, u32[]{:S(2)}) async-start(f32[4,1,8192]{2,1,0:T(1,128)} %reshape.157), calls=%async_computation.6 | async-start | bytes 262144 | tf_op jit(solution)/shard_map/all_to_all | solution.py:64
Sparse Core Ops, SparseCore 0:
  10.9 99.7 all-gather.6
  112.3 92.8 all-gather.4
  206.7 39.7 all-gather.8
  248.0 40.2 all-gather.10

commit v16 on v12

--- a/solution.py
+++ b/solution.py
@@ -33,11 +33,14 @@
 
     ladder_chunks = []
     cycle_chunks = []
+    pending = None
     for t in range(chunks):
         a_chunk = sizes[t]
         v = lax.slice_in_dim(slab_integrals, starts[t] * nvir, (starts[t] + a_chunk) * nvir, axis=1)
         v_all = lax.all_gather(v, "int", axis=0, tiled=True)
-        if t:
+        if t and pending is not None:
+            v_all, ladder_chunks[-1], pending = lax.optimization_barrier((v_all, ladder_chunks[-1], pending))
+        elif t:
             v_all, ladder_chunks[-1], cycle_chunks[-1] = lax.optimization_barrier(
                 (v_all, ladder_chunks[-1], cycle_chunks[-1])
             )
@@ -49,9 +52,17 @@
         l_cyc = l_cyc.reshape(n_amp, ibat * a_chunk, c_local * k_local)
         moved = lax.all_to_all(l_cyc, "amp", split_axis=0, concat_axis=0, tiled=True)
         moved = moved.reshape(n_amp * ibat * a_chunk, c_local * k_local)
-        cycle_chunks.append(
-            jnp.dot(moved, w2, precision=PRECISION, preferred_element_type=jnp.float32)
-        )
+        if pending is not None:
+            cycle_chunks.append(
+                jnp.dot(pending, w2, precision=PRECISION, preferred_element_type=jnp.float32)
+            )
+            pending = None
+        if t == chunks - 2:
+            pending = moved
+        else:
+            cycle_chunks.append(
+                jnp.dot(moved, w2, precision=PRECISION, preferred_element_type=jnp.float32)
+            )
     ladder = jnp.concatenate(ladder_chunks, axis=1)
 
     parts = jnp.concatenate(

time: 355 us -> 356 us (level)
    all_to_all x4, waiting for transfers between devices: 50.6 us -> 39.1 us  [per_device(): lax.all_to_all(l_cyc, 'amp', split_axis=0, concat_axis=0, tiled=True)]
    all_gather x4, waiting for transfers between devices: 106 us -> 118 us  [per_device(): v_all = lax.all_gather(v, 'int', axis=0, tiled=True)]
    dot_general x4 -> x3, matrix products: 18.4 us -> 14.4 us  [per_device(): jnp.dot(moved, w2, precision=PRECISION, preferred_element_type=jnp.float32)]
    dot_general x0 -> x1, matrix products: none -> 4.03 us  [per_device(): jnp.dot(pending, w2, precision=PRECISION, preferred_element_type=jnp.floa...]
  transfers between devices with their start and end apart: 9 -> 9, of which waited for: 8 -> 7; matrix products, arithmetic and copies ran while one was open for 29% -> 29% of each run, Pallas kernels for 0% -> 0%
where the time goes in v16:
time: 356 us; the launch traced here: 354 us
  waiting for transfers between devices  173 us (49%)
  local copies, waits for them, and re-layouts  68.8 us (19%)
  matrix products  50.8 us (14%)
  blocking collectives  27.5 us (8%)
  starting transfers between devices  18.3 us (5%)
  between operations  14 us (4%)
    all_gather x4, waiting for transfers between devices, per_device(): v_all = lax.all_gather(v, 'int', axis=0, tiled=True)  118 us
    all_to_all x4, waiting for transfers between devices, per_device(): lax.all_to_all(l_cyc, 'amp', split_axis=0, concat_axis=0, tiled=True)  39.1 us
    all_to_all x1, blocking collectives, per_device(): lax.all_to_all(amplitudes.reshape(i_local, nocc, pw), 'int', split_axis=1...  27.5 us
    reshape x4, local copies, waits for them, and re-layouts, per_device(): l_cyc = l_cyc.reshape(n_amp, ibat * a_chunk, c_local * k_local)  18.6 us
    dot_general x4, matrix products, per_device(): jnp.dot(amplitudes, v_all, precision=PRECISION, preferred_element_type=jn...  17.4 us
    all_to_all x1, waiting for transfers between devices, per_device(): lax.all_to_all(parts, ('int', 'amp'), split_axis=0, concat_axis=0, tiled=...  15.7 us
    reshape x6, local copies, waits for them, and re-layouts, per_device(): l_cyc.reshape(ibat, k_local, a_chunk, n_amp, c_local)  15.2 us
    all_to_all x4, starting transfers between devices, per_device(): lax.all_to_all(l_cyc, 'amp', split_axis=0, concat_axis=0, tiled=True)  15 us
  transfers between devices with their start and end apart: 9, of which 7 were waited for; matrix products, arithmetic and copies ran while one was open for 29% of the time, Pallas kernels for 0%

profile of v16, /device:TPU:0, one launch (start us, length us, event | category | flops | bytes accessed | tf_op | source)
XLA Modules:
  0.0 354.4 jit_solution(17321239701526264994)
XLA Ops:
  12.1 27.5 %all_to_all.40 = f32[2,96,512]{2,0,1:T(2,128)S(1)} all-to-all(f32[2,96,512]{2,0,1:T(2,128)S(1)} %copy.57), channel_id=1, replica_groups=mesh['amp'=8,'int'=4] {'int'}, dimensions={1} | all-to-all | bytes 786432 | tf_op jit(solution)/shard_map/all_to_all | solution.py:29
  39.7 71.0 %all-gather.7.cloned.1.call-done = f32[512,2400]{1,0:T(8,128)} async-done(((f32[128,2400]{1,0:T(8,128)}), f32[512,2400]{1,0:T(8,128)}) %all-gather.7.cloned.1.call-update) | async-done | bytes 4915216 | tf_op jit(solution)/shard_map/all_gather | solution.py:40
  110.8 5.7 %copy.60 = f32[2400,512]{1,0:T(8,128)} copy(f32[2400,512]{0,1:T(8,128)} %bitcast.81) | data formatting | bytes 9830400 | tf_op jit(solution)/shard_map/dot_general | solution.py:50
  116.5 5.4 %reshape.146 = f32[3,8,100,512,1]{3,2,1,0,4:T(8,128)} reshape(f32[2400,512]{1,0:T(8,128)} %copy.60) | data formatting | bytes 9830400 | tf_op jit(solution)/shard_map/dot_general | solution.py:50
  121.9 4.9 %convolution_bitcast_fusion.2 = f32[8,8,3,100,24]{3,4,0,2,1:T(8,128)S(1)} fusion(f32[8,24,512,1,1]{2,1,4,3,0:T(8,128)S(1)} %bitcast.84, f32[3,8,100,512,1]{3,2,1,0,4:T(8,128)} %reshape.146), kind=kOutput, calls=%fused_computation.2 | convolution fusion | flops 1415577600 | bytes 7151616 | tf_op jit(solution)/shard_map/dot_general | solution.py:50
  126.8 5.6 %copy.61 = f32[8,8,3,100,24]{4,3,2,1,0:T(8,128)} copy(f32[8,8,3,100,24]{3,4,0,2,1:T(8,128)S(1)} %convolution_bitcast_fusion.2) | data formatting | bytes 3686400 | tf_op jit(solution)/shard_map/transpose | solution.py:51
  132.5 7.6 %reshape.129 = f32[8,24,2400]{2,1,0:T(8,128)} reshape(f32[8,8,3,100,24]{4,3,2,1,0:T(8,128)} %copy.61) | data formatting | bytes 3686400 | tf_op jit(solution)/shard_map/reshape | solution.py:52
  146.6 5.6 %fusion.3 = f32[192,2400]{1,0:T(8,128)} fusion(f32[192,512]{1,0:T(8,128)S(1)} %copy-done.2, f32[512,2400]{1,0:T(8,128)} %all-gather.7.cloned.1.call-done), kind=kOutput, calls=%fused_computation.25 | convolution fusion | flops 1415577600 | bytes 7151616 | tf_op jit(solution)/shard_map/dot_general | solution.py:48
  152.2 15.8 %all-to-all-done.1 = f32[8,24,2400]{2,1,0:T(8,128)S(1)} async-done(((f32[8,24,2400]{2,1,0:T(8,128)}), f32[8,24,2400]{2,1,0:T(8,128)S(1)}, u32[]{:S(2)}, u32[]{:S(2)}) %all-to-all-start.1) | async-done | bytes 1843232 | tf_op jit(solution)/shard_map/all_to_all | solution.py:53
  168.0 5.1 %fusion.4 = f32[192,512]{1,0:T(8,128)} fusion(f32[192,2400]{1,0:T(8,128)S(1)} %bitcast.90, f32[2400,512]{1,0:T(8,128)} %bitcast.76), kind=kOutput, calls=%fused_computation.26 | convolution fusion | flops 1415577600 | bytes 7151616 | tf_op jit(solution)/shard_map/dot_general | solution.py:64
  173.1 32.1 %all-gather.5.cloned.1.call-done = f32[512,2400]{1,0:T(8,128)} async-done(((f32[128,2400]{1,0:T(8,128)}), f32[512,2400]{1,0:T(8,128)}) %all-gather.5.cloned.1.call-update) | async-done | bytes 4915216 | tf_op jit(solution)/shard_map/all_gather | solution.py:40
  205.2 5.4 %convolution_bitcast_fusion = f32[192,2400]{1,0:T(8,128)} fusion(f32[512,2400]{1,0:T(8,128)} %all-gather.5.cloned.1.call-done, f32[192,512]{1,0:T(8,128)S(1)} %bitcast.85), kind=kOutput, calls=%fused_computation | convolution fusion | flops 1415577600 | bytes 7151616 | tf_op jit(solution)/shard_map/dot_general | solution.py:50
  213.3 5.6 %copy.63 = f32[8,24,3,8,100]{1,4,2,0,3:T(8,128)} copy(f32[8,24,3,8,100]{4,3,2,1,0:T(8,128)S(1)} %reshape.133) | data formatting | bytes 3686400 | tf_op jit(solution)/shard_map/reshape | solution.py:51
  218.8 7.6 %reshape.134 = f32[8,24,2400]{2,1,0:T(8,128)} reshape(f32[8,8,3,100,24]{4,3,2,1,0:T(8,128)} %bitcast.80) | data formatting | bytes 3686400 | tf_op jit(solution)/shard_map/reshape | solution.py:52
  230.6 5.5 %convolution_bitcast_fusion.1 = f32[192,2400]{1,0:T(8,128)} fusion(f32[512,2400]{1,0:T(8,128)} %all-gather.5.cloned.1.call-done, f32[192,512]{1,0:T(8,128)S(1)} %copy-done.2), kind=kOutput, calls=%fused_computation.1 | convolution fusion | flops 1415577600 | bytes 7151616 | tf_op jit(solution)/shard_map/dot_general | solution.py:48
  236.1 18.2 %all-to-all-done.2 = f32[8,24,2400]{2,1,0:T(8,128)S(1)} async-done(((f32[8,24,2400]{2,1,0:T(8,128)}), f32[8,24,2400]{2,1,0:T(8,128)S(1)}, u32[]{:S(2)}, u32[]{:S(2)}) %all-to-all-start.2) | async-done | bytes 1843232 | tf_op jit(solution)/shard_map/all_to_all | solution.py:53
  254.2 5.2 %fusion.5 = f32[192,512]{1,0:T(8,128)} fusion(f32[192,2400]{1,0:T(8,128)S(1)} %bitcast.91, f32[2400,512]{1,0:T(8,128)} %bitcast.77), kind=kOutput, calls=%fused_computation.27 | convolution fusion | flops 1415577600 | bytes 7151616 | tf_op jit(solution)/shard_map/dot_general | solution.py:64
  273.9 14.4 %all-gather.11.cloned.1.call-done = f32[512,800]{1,0:T(8,128)} async-done(((f32[128,800]{1,0:T(8,128)}), f32[512,800]{1,0:T(8,128)}) %all-gather.11.cloned.1.call-update) | async-done | bytes 1638416 | tf_op jit(solution)/shard_map/all_gather | solution.py:40
  296.7 3.9 %all-to-all-start.4 = ((f32[8,8,2400]{2,1,0:T(8,128)}), f32[8,8,2400]{2,1,0:T(8,128)S(1)}, u32[]{:S(2)}, u32[]{:S(2)}) async-start(f32[8,8,2400]{2,1,0:T(8,128)} %reshape.142), calls=%async_computation.4 | async-start | bytes 1245184 | tf_op jit(solution)/shard_map/all_to_all | solution.py:53
  302.0 4.0 %convolution_bitcast_fusion.8 = f32[8,8,1,512]{3,1,0,2:T(8,128)S(1)} fusion(f32[2400,512,1]{1,0,2:T(8,128)} %bitcast.78, f32[64,2400]{1,0:T(8,128)S(1)} %bitcast.92), kind=kOutput, calls=%fused_computation.8 | convolution fusion | flops 471859200 | bytes 5660672 | tf_op jit(solution)/shard_map/dot_general | solution.py:57
  306.2 5.1 %all-to-all-done.4 = f32[8,8,2400]{2,1,0:T(8,128)S(1)} async-done(((f32[8,8,2400]{2,1,0:T(8,128)}), f32[8,8,2400]{2,1,0:T(8,128)S(1)}, u32[]{:S(2)}, u32[]{:S(2)}) %all-to-all-start.4) | async-done | bytes 614432 | tf_op jit(solution)/shard_map/all_to_all | solution.py:53
  311.3 4.0 %convolution_bitcast_fusion.7 = f32[8,8,1,512]{3,1,0,2:T(8,128)S(1)} fusion(f32[8,8,2400]{2,1,0:T(8,128)S(1)} %all-to-all-done.4, f32[2400,512,1]{1,0,2:T(8,128)} %bitcast.79), kind=kOutput, calls=%fused_computation.7 | convolution fusion | flops 471859200 | bytes 5660672 | tf_op jit(solution)/shard_map/dot_general | solution.py:64
  325.4 6.0 %concatenate.6 = f32[192,6400]{1,0:T(8,128)} concatenate(f32[192,2400]{1,0:T(8,128)S(1)} %copy-done.4, f32[192,2400]{1,0:T(8,128)} %convolution_bitcast_fusion.1, f32[192,800]{1,0:T(8,128)} %convolution_bitcast_fusion.6, f32[192,800]{1,0:T(8,128)} %convolution_bitcast_fusion.4), dimensions={1} | concatenate | bytes 9830400 | tf_op jit(solution)/shard_map/concatenate | solution.py:66
  331.4 15.7 %all-to-all-done.5 = f32[32,128,64]{1,2,0:T(8,128)S(1)} async-done(((f32[32,128,64]{1,2,0:T(8,128)}), f32[32,128,64]{1,2,0:T(8,128)S(1)}, u32[]{:S(2)}, u32[]{:S(2)}) %all-to-all-start.5) | async-done | bytes 1048608 | tf_op jit(solution)/shard_map/all_to_all | solution.py:74
  (66 shorter events, 53.3 us)
Async XLA Ops:
  7.2 103.6 %all-gather.7.cloned.1.call-start = ((), (), s32[]{:S(2)}) async-start(), calls=%async_computation.7 | async-start | bytes 6225920 | tf_op jit(solution)/shard_map/all_gather | solution.py:40
  10.8 1.0 copy-start.2
  10.8 194.3 %all-gather.5.cloned.1.call-start = ((), (), s32[]{:S(2)}) async-start(), calls=%async_computation.6 | async-start | bytes 6225920 | tf_op jit(solution)/shard_map/all_gather | solution.py:40
  39.7 219.8 %copy-start = (f32[4,2,24,512]{3,2,1,0:T(8,128)}, f32[4,2,24,512]{3,2,1,0:T(8,128)S(1)}, u32[]{:S(2)}) copy-start(f32[4,2,24,512]{3,2,1,0:T(8,128)S(1)} %copy.59) | copy-start | bytes 1179652
  140.1 28.0 %all-to-all-start.1 = ((f32[8,24,2400]{2,1,0:T(8,128)}), f32[8,24,2400]{2,1,0:T(8,128)S(1)}, u32[]{:S(2)}, u32[]{:S(2)}) async-start(f32[8,24,2400]{2,1,0:T(8,128)} %reshape.129), calls=%async_computation.1 | async-start | bytes 3735552 | tf_op jit(solution)/shard_map/all_to_all | solution.py:53
  143.8 115.6 %all-gather.9.cloned.1.call-start = ((), (), s32[]{:S(2)}) async-start(), calls=%async_computation.8 | async-start | bytes 2293760 | tf_op jit(solution)/shard_map/all_gather | solution.py:40
  226.4 27.8 %all-to-all-start.2 = ((f32[8,24,2400]{2,1,0:T(8,128)}), f32[8,24,2400]{2,1,0:T(8,128)S(1)}, u32[]{:S(2)}, u32[]{:S(2)}) async-start(f32[8,24,2400]{2,1,0:T(8,128)} %reshape.134), calls=%async_computation.2 | async-start | bytes 3735552 | tf_op jit(solution)/shard_map/all_to_all | solution.py:53
  230.0 58.3 %all-gather.11.cloned.1.call-start = ((), (), s32[]{:S(2)}) async-start(), calls=%async_computation.9 | async-start | bytes 2293760 | tf_op jit(solution)/shard_map/all_gather | solution.py:40
  267.0 22.2 %copy-start.1 = (f32[4,2,24,512]{3,2,1,0:T(8,128)S(1)}, f32[4,2,24,512]{3,2,1,0:T(8,128)}, u32[]{:S(2)}) copy-start(f32[4,2,24,512]{3,2,1,0:T(8,128)} %copy-done) | copy-start | bytes 1179652
  267.0 21.3 %all-to-all-start.3 = ((f32[8,8,2400]{2,1,0:T(8,128)}), f32[8,8,2400]{2,1,0:T(8,128)S(1)}, u32[]{:S(2)}, u32[]{:S(2)}) async-start(f32[8,8,2400]{2,1,0:T(8,128)} %reshape.137), calls=%async_computation.3 | async-start | bytes 1245184 | tf_op jit(solution)/shard_map/all_to_all | solution.py:53
  288.3 0.8 copy-start.5
  296.7 5.1 %copy-start.7 = (f32[192,512]{1,0:T(8,128)S(1)}, f32[192,512]{1,0:T(8,128)}, u32[]{:S(2)}) copy-start(f32[192,512]{1,0:T(8,128)} %fusion.5) | copy-start | bytes 1179652
  296.7 5.3 %copy-start.6 = (f32[8,8,2400]{2,1,0:T(8,128)S(1)}, f32[8,8,2400]{2,1,0:T(8,128)}, u32[]{:S(2)}) copy-start(f32[8,8,2400]{2,1,0:T(8,128)} %copy-done.5) | copy-start | bytes 1843204
  296.7 14.6 %all-to-all-start.4 = ((f32[8,8,2400]{2,1,0:T(8,128)}), f32[8,8,2400]{2,1,0:T(8,128)S(1)}, u32[]{:S(2)}, u32[]{:S(2)}) async-start(f32[8,8,2400]{2,1,0:T(8,128)} %reshape.142), calls=%async_computation.4 | async-start | bytes 1245184 | tf_op jit(solution)/shard_map/all_to_all | solution.py:53
  316.5 5.1 %copy-start.8 = (s32[96]{0:T(128)S(1)}, s32[96]{0:T(128)}, u32[]{:S(2)}) copy-start(s32[96]{0:T(128)} %param.8) | copy-start | bytes 1156
  316.5 5.7 %copy-start.3 = (f32[192,512]{1,0:T(8,128)S(1)}, f32[192,512]{1,0:T(8,128)}, u32[]{:S(2)}) copy-start(f32[192,512]{1,0:T(8,128)} %param.5) | copy-start | bytes 1179652
  318.1 7.3 %copy-start.4 = (f32[192,2400]{1,0:T(8,128)S(1)}, f32[192,2400]{1,0:T(8,128)}, u32[]{:S(2)}) copy-start(f32[192,2400]{1,0:T(8,128)} %fusion.3) | copy-start | bytes 5529604
  318.1 29.0 %all-to-all-start.5 = ((f32[32,128,64]{1,2,0:T(8,128)}), f32[32,128,64]{1,2,0:T(8,128)S(1)}, u32[]{:S(2)}, u32[]{:S(2)}) async-start(f32[32,128,64]{1,2,0:T(8,128)} %bitcast.32), calls=%async_computation.5 | async-start | bytes 2097152 | tf_op jit(solution)/shard_map/all_to_all | solution.py:74
Sparse Core Ops, SparseCore 0:
  11.0 99.7 all-gather.6
  112.3 92.8 all-gather.4
  206.8 39.7 all-gather.8
  248.0 40.2 all-gather.10

commit v17 on v12

--- a/solution.py
+++ b/solution.py
@@ -26,9 +26,19 @@
     chunks = len(sizes)
     starts = [sum(sizes[:t]) for t in range(chunks)]
 
-    t_cyc = lax.all_to_all(
-        amplitudes.reshape(i_local, nocc, pw), "int", split_axis=1, concat_axis=0, tiled=True
-    ).reshape(ibat * k_local, pw)
+    if pw % n_amp == 0:
+        piece = pw // n_amp
+        mine = lax.dynamic_slice_in_dim(amplitudes, lax.axis_index("amp") * piece, piece, axis=1)
+        mine = lax.all_to_all(
+            mine.reshape(i_local, nocc, piece), "int", split_axis=1, concat_axis=0, tiled=True
+        )
+        copies = jnp.broadcast_to(mine[None], (n_amp, ibat, k_local, piece))
+        t_cyc = lax.all_to_all(copies, "amp", split_axis=0, concat_axis=3, tiled=True)
+        t_cyc = t_cyc.reshape(ibat * k_local, pw)
+    else:
+        t_cyc = lax.all_to_all(
+            amplitudes.reshape(i_local, nocc, pw), "int", split_axis=1, concat_axis=0, tiled=True
+        ).reshape(ibat * k_local, pw)
     w2 = cycle_integrals.transpose(1, 0, 2).reshape(c_local * k_local, columns)
 
     ladder_chunks = []

time: 355 us -> 364 us (1.025)
  local copies, waits for them, and re-layouts: 68 us -> 87.8 us
  waiting for transfers between devices: 173 us -> 167 us
  matrix products: 50.8 us -> 46.7 us
  blocking collectives: 27.5 us -> 23.7 us
    dot_general x2 -> x8, local copies, waits for them, and re-layouts: 11.1 us -> 28.7 us  [per_device(): jnp.dot(t_cyc, v_all, precision=PRECISION, preferred_element_type=jnp.flo...]
    reshape x7 -> x1, local copies, waits for them, and re-layouts: 15.6 us -> 0.08 us  [per_device(): mine.reshape(i_local, nocc, piece)]
    transpose x1 -> x4, local copies, waits for them, and re-layouts: 5.63 us -> 16.1 us  [per_device(): l_cyc.reshape(ibat, k_local, a_chunk, n_amp, c_local)]
    all_gather x4, waiting for transfers between devices: 106 us -> 97.9 us  [per_device(): v_all = lax.all_gather(v, 'int', axis=0, tiled=True)]
    all_to_all x1 -> x2, blocking collectives: 27.5 us -> 23.7 us  [the longest x1 11.9 us: per_device(): lax.all_to_all(copies, 'amp', split_axis=0, concat_axis=3, tiled=True)]
  transfers between devices with their start and end apart: 9 -> 9, of which waited for: 8 -> 7; matrix products, arithmetic and copies ran while one was open for 29% -> 32% of each run, Pallas kernels for 0% -> 0%
where the time goes in v17:
time: 364 us; the launch traced here: 362 us
  waiting for transfers between devices  167 us (46%)
  local copies, waits for them, and re-layouts  87.8 us (24%)
  matrix products  46.7 us (13%)
  blocking collectives  23.7 us (7%)
  starting transfers between devices  18.1 us (5%)
  between operations  14.1 us (4%)
  other arithmetic  4.03 us (1%)
    all_gather x4, waiting for transfers between devices, per_device(): v_all = lax.all_gather(v, 'int', axis=0, tiled=True)  97.9 us
    all_to_all x4, waiting for transfers between devices, per_device(): lax.all_to_all(l_cyc, 'amp', split_axis=0, concat_axis=0, tiled=True)  52.8 us
    dot_general x8, local copies, waits for them, and re-layouts, per_device(): jnp.dot(t_cyc, v_all, precision=PRECISION, preferred_element_type=jnp.flo...  28.7 us
    reshape x4, local copies, waits for them, and re-layouts, per_device(): l_cyc = l_cyc.reshape(n_amp, ibat * a_chunk, c_local * k_local)  21.9 us
    dot_general x4, matrix products, per_device(): jnp.dot(moved, w2, precision=PRECISION, preferred_element_type=jnp.float32)  18.9 us
    transpose x4, local copies, waits for them, and re-layouts, per_device(): l_cyc.reshape(ibat, k_local, a_chunk, n_amp, c_local)  16.1 us
    dot_general x4, matrix products, per_device(): jnp.dot(amplitudes, v_all, precision=PRECISION, preferred_element_type=jn...  15.9 us
    all_to_all x1, waiting for transfers between devices, per_device(): lax.all_to_all(parts, ('int', 'amp'), split_axis=0, concat_axis=0, tiled=...  15.7 us
  transfers between devices with their start and end apart: 9, of which 7 were waited for; matrix products, arithmetic and copies ran while one was open for 32% of the time, Pallas kernels for 0%

profile of v17, /device:TPU:0, one launch (start us, length us, event | category | flops | bytes accessed | tf_op | source)
XLA Modules:
  0.0 361.9 jit_solution(6106018996561869550)
XLA Ops:
  11.9 11.8 %all_to_all.55 = f32[4,1,3072]{2,1,0:T(1,128)S(1)} all-to-all(f32[4,1,3072]{2,1,0:T(1,128)S(1)} %reshape.167), channel_id=1, replica_groups=mesh['amp'=8,'int'=4] {'int'}, dimensions={0} | all-to-all | bytes 98304 | tf_op jit(solution)/shard_map/all_to_all | solution.py:32
  25.8 11.9 %all_to_all.56 = f32[8,1,12288]{2,1,0:T(1,128)S(1)} all-to-all(f32[8,1,12288]{2,1,0:T(1,128)S(1)} %reshape.169), channel_id=1, replica_groups=mesh['amp'=8,'int'=4] {'amp'}, dimensions={0} | all-to-all | bytes 786432 | tf_op jit(solution)/shard_map/all_to_all | solution.py:36
  41.0 66.5 %all-gather.7.cloned.1.call-done = f32[512,2400]{1,0:T(8,128)} async-done(((f32[128,2400]{1,0:T(8,128)}), f32[512,2400]{1,0:T(8,128)}) %all-gather.7.cloned.1.call-update) | async-done | bytes 4915216 | tf_op jit(solution)/shard_map/all_gather | solution.py:49
  107.4 5.7 %copy.75 = f32[2400,512]{1,0:T(8,128)} copy(f32[2400,512]{0,1:T(8,128)} %bitcast.95) | data formatting | bytes 9830400 | tf_op jit(solution)/shard_map/dot_general | solution.py:57
  113.2 5.5 %reshape.155 = f32[3,8,100,512,1]{3,2,1,0,4:T(8,128)} reshape(f32[2400,512]{1,0:T(8,128)} %copy.75) | data formatting | bytes 9830400 | tf_op jit(solution)/shard_map/dot_general | solution.py:57
  118.7 4.9 %convolution_bitcast_fusion.2 = f32[8,8,3,100,24]{3,4,0,2,1:T(8,128)S(1)} fusion(f32[3,8,100,512,1]{3,2,1,0,4:T(8,128)} %reshape.155, f32[8,24,512,1,1]{2,1,0,3,4:T(8,128)} %reshape.154), kind=kOutput, calls=%fused_computation.2 | convolution fusion | flops 1415577600 | bytes 7151616 | tf_op jit(solution)/shard_map/dot_general | solution.py:57
  123.6 5.6 %copy.76 = f32[8,8,3,100,24]{4,3,2,1,0:T(8,128)} copy(f32[8,8,3,100,24]{3,4,0,2,1:T(8,128)S(1)} %convolution_bitcast_fusion.2) | data formatting | bytes 3686400 | tf_op jit(solution)/shard_map/transpose | solution.py:58
  129.2 7.6 %reshape.139 = f32[8,24,2400]{2,1,0:T(8,128)} reshape(f32[8,8,3,100,24]{4,3,2,1,0:T(8,128)} %copy.76) | data formatting | bytes 3686400 | tf_op jit(solution)/shard_map/reshape | solution.py:59
  143.2 5.6 %fusion.8 = f32[192,2400]{1,0:T(8,128)} fusion(f32[192,512]{1,0:T(8,128)S(1)} %copy-done, f32[512,2400]{1,0:T(8,128)} %all-gather.7.cloned.1.call-done), kind=kOutput, calls=%fused_computation.31 | convolution fusion | flops 1415577600 | bytes 7151616 | tf_op jit(solution)/shard_map/dot_general | solution.py:55
  148.8 15.8 %all-to-all-done.2 = f32[8,24,2400]{2,1,0:T(8,128)S(1)} async-done(((f32[8,24,2400]{2,1,0:T(8,128)}), f32[8,24,2400]{2,1,0:T(8,128)S(1)}, u32[]{:S(2)}, u32[]{:S(2)}) %all-to-all-start.2) | async-done | bytes 1843232 | tf_op jit(solution)/shard_map/all_to_all | solution.py:60
  164.6 5.1 %fusion.9 = f32[192,512]{1,0:T(8,128)} fusion(f32[192,2400]{1,0:T(8,128)S(1)} %bitcast.97, f32[2400,512]{1,0:T(8,128)} %bitcast.90), kind=kOutput, calls=%fused_computation.32 | convolution fusion | flops 1415577600 | bytes 7151616 | tf_op jit(solution)/shard_map/dot_general | solution.py:63
  169.7 31.4 %all-gather.5.cloned.1.call-done = f32[512,2400]{1,0:T(8,128)} async-done(((f32[128,2400]{1,0:T(8,128)}), f32[512,2400]{1,0:T(8,128)}) %all-gather.5.cloned.1.call-update) | async-done | bytes 4915216 | tf_op jit(solution)/shard_map/all_gather | solution.py:49
  201.2 5.7 %copy.77 = f32[2400,512]{1,0:T(8,128)} copy(f32[2400,512]{0,1:T(8,128)} %bitcast.94) | data formatting | bytes 9830400 | tf_op jit(solution)/shard_map/dot_general | solution.py:57
  206.9 5.4 %reshape.156 = f32[3,8,100,512,1]{3,2,1,0,4:T(8,128)} reshape(f32[2400,512]{1,0:T(8,128)} %copy.77) | data formatting | bytes 9830400 | tf_op jit(solution)/shard_map/dot_general | solution.py:57
  212.3 4.9 %convolution_bitcast_fusion.1 = f32[8,8,3,100,24]{3,4,0,2,1:T(8,128)S(1)} fusion(f32[3,8,100,512,1]{3,2,1,0,4:T(8,128)} %reshape.156, f32[8,24,512,1,1]{2,1,0,3,4:T(8,128)} %reshape.154), kind=kOutput, calls=%fused_computation.1 | convolution fusion | flops 1415577600 | bytes 7151616 | tf_op jit(solution)/shard_map/dot_general | solution.py:57
  217.2 5.6 %copy.78 = f32[8,8,3,100,24]{4,3,2,1,0:T(8,128)} copy(f32[8,8,3,100,24]{3,4,0,2,1:T(8,128)S(1)} %convolution_bitcast_fusion.1) | data formatting | bytes 3686400 | tf_op jit(solution)/shard_map/transpose | solution.py:58
  222.8 7.6 %reshape.142 = f32[8,24,2400]{2,1,0:T(8,128)} reshape(f32[8,8,3,100,24]{4,3,2,1,0:T(8,128)} %copy.78) | data formatting | bytes 3686400 | tf_op jit(solution)/shard_map/reshape | solution.py:59
  234.9 5.4 %convolution_bitcast_fusion = f32[192,2400]{1,0:T(8,128)} fusion(f32[512,2400]{1,0:T(8,128)} %all-gather.5.cloned.1.call-done, f32[192,512]{1,0:T(8,128)S(1)} %copy-done), kind=kOutput, calls=%fused_computation | convolution fusion | flops 1415577600 | bytes 7151616 | tf_op jit(solution)/shard_map/dot_general | solution.py:55
  240.3 18.0 %all-to-all-done.3 = f32[8,24,2400]{2,1,0:T(8,128)S(1)} async-done(((f32[8,24,2400]{2,1,0:T(8,128)}), f32[8,24,2400]{2,1,0:T(8,128)S(1)}, u32[]{:S(2)}, u32[]{:S(2)}) %all-to-all-start.3) | async-done | bytes 1843232 | tf_op jit(solution)/shard_map/all_to_all | solution.py:60
  258.3 5.1 %fusion.10 = f32[192,512]{1,0:T(8,128)} fusion(f32[192,2400]{1,0:T(8,128)S(1)} %bitcast.98, f32[2400,512]{1,0:T(8,128)} %bitcast.91), kind=kOutput, calls=%fused_computation.33 | convolution fusion | flops 1415577600 | bytes 7151616 | tf_op jit(solution)/shard_map/dot_general | solution.py:63
  279.7 9.0 %all-to-all-done.4 = f32[8,8,2400]{2,1,0:T(8,128)S(1)} async-done(((f32[8,8,2400]{2,1,0:T(8,128)}), f32[8,8,2400]{2,1,0:T(8,128)S(1)}, u32[]{:S(2)}, u32[]{:S(2)}) %all-to-all-start.4) | async-done | bytes 614432 | tf_op jit(solution)/shard_map/all_to_all | solution.py:60
  308.9 9.9 %all-to-all-done.5 = f32[8,8,2400]{2,1,0:T(8,128)S(1)} async-done(((f32[8,8,2400]{2,1,0:T(8,128)}), f32[8,8,2400]{2,1,0:T(8,128)S(1)}, u32[]{:S(2)}, u32[]{:S(2)}) %all-to-all-start.5) | async-done | bytes 614432 | tf_op jit(solution)/shard_map/all_to_all | solution.py:60
  332.9 6.0 %concatenate.6 = f32[192,6400]{1,0:T(8,128)} concatenate(f32[192,2400]{1,0:T(8,128)S(1)} %copy-done.1, f32[192,2400]{1,0:T(8,128)} %convolution_bitcast_fusion, f32[192,800]{1,0:T(8,128)} %convolution_bitcast_fusion.6, f32[192,800]{1,0:T(8,128)} %convolution_bitcast_fusion.5), dimensions={1} | concatenate | bytes 9830400 | tf_op jit(solution)/shard_map/concatenate | solution.py:65
  338.9 15.7 %all-to-all-done.6 = f32[32,128,64]{1,2,0:T(8,128)S(1)} async-done(((f32[32,128,64]{1,2,0:T(8,128)}), f32[32,128,64]{1,2,0:T(8,128)S(1)}, u32[]{:S(2)}, u32[]{:S(2)}) %all-to-all-start.6) | async-done | bytes 1048608 | tf_op jit(solution)/shard_map/all_to_all | solution.py:73
  (78 shorter events, 71.9 us)
Async XLA Ops:
  7.2 4.5 %copy-start = (f32[192,512]{1,0:T(8,128)S(1)}, f32[192,512]{1,0:T(8,128)}, u32[]{:S(2)}) copy-start(f32[192,512]{1,0:T(8,128)} %param.5) | copy-start | bytes 1179652
  7.2 100.3 %all-gather.7.cloned.1.call-start = ((), (), s32[]{:S(2)}) async-start(), calls=%async_computation.8 | async-start | bytes 6225920 | tf_op jit(solution)/shard_map/all_gather | solution.py:49
  10.9 190.3 %all-gather.5.cloned.1.call-start = ((), (), s32[]{:S(2)}) async-start(), calls=%async_computation.7 | async-start | bytes 6225920 | tf_op jit(solution)/shard_map/all_gather | solution.py:49
  136.8 27.8 %all-to-all-start.2 = ((f32[8,24,2400]{2,1,0:T(8,128)}), f32[8,24,2400]{2,1,0:T(8,128)S(1)}, u32[]{:S(2)}, u32[]{:S(2)}) async-start(f32[8,24,2400]{2,1,0:T(8,128)} %reshape.139), calls=%async_computation.2 | async-start | bytes 3735552 | tf_op jit(solution)/shard_map/all_to_all | solution.py:60
  140.5 122.9 %all-gather.9.cloned.1.call-start = ((), (), s32[]{:S(2)}) async-start(), calls=%async_computation.9 | async-start | bytes 2293760 | tf_op jit(solution)/shard_map/all_gather | solution.py:49
  230.4 27.9 %all-to-all-start.3 = ((f32[8,24,2400]{2,1,0:T(8,128)}), f32[8,24,2400]{2,1,0:T(8,128)S(1)}, u32[]{:S(2)}, u32[]{:S(2)}) async-start(f32[8,24,2400]{2,1,0:T(8,128)} %reshape.142), calls=%async_computation.3 | async-start | bytes 3735552 | tf_op jit(solution)/shard_map/all_to_all | solution.py:60
  234.1 59.3 %all-gather.11.cloned.1.call-start = ((), (), s32[]{:S(2)}) async-start(), calls=%async_computation.10 | async-start | bytes 2293760 | tf_op jit(solution)/shard_map/all_gather | solution.py:49
  271.0 7.0 %copy-start.2 = (f32[512,800]{1,0:T(8,128)S(1)}, f32[512,800]{1,0:T(8,128)}, u32[]{:S(2)}) copy-start(f32[512,800]{1,0:T(8,128)} %all-gather.9.cloned.1.call-done) | copy-start | bytes 4915204
  274.4 14.3 %all-to-all-start.4 = ((f32[8,8,2400]{2,1,0:T(8,128)}), f32[8,8,2400]{2,1,0:T(8,128)S(1)}, u32[]{:S(2)}, u32[]{:S(2)}) async-start(f32[8,8,2400]{2,1,0:T(8,128)} %reshape.145), calls=%async_computation.4 | async-start | bytes 1245184 | tf_op jit(solution)/shard_map/all_to_all | solution.py:60
  301.0 7.3 %copy-start.3 = (f32[192,512]{1,0:T(8,128)S(1)}, f32[192,512]{1,0:T(8,128)}, u32[]{:S(2)}) copy-start(f32[192,512]{1,0:T(8,128)} %fusion.9) | copy-start | bytes 1179652
  301.0 7.5 %copy-start.4 = (f32[192,512]{1,0:T(8,128)S(1)}, f32[192,512]{1,0:T(8,128)}, u32[]{:S(2)}) copy-start(f32[192,512]{1,0:T(8,128)} %fusion.10) | copy-start | bytes 1179652
  304.4 4.3 %copy-start.5 = (f32[64,512]{1,0:T(8,128)S(1)}, f32[64,512]{1,0:T(8,128)}, u32[]{:S(2)}) copy-start(f32[64,512]{1,0:T(8,128)} %fusion) | copy-start | bytes 393220
  304.4 14.4 %all-to-all-start.5 = ((f32[8,8,2400]{2,1,0:T(8,128)}), f32[8,8,2400]{2,1,0:T(8,128)S(1)}, u32[]{:S(2)}, u32[]{:S(2)}) async-start(f32[8,8,2400]{2,1,0:T(8,128)} %reshape.151), calls=%async_computation.5 | async-start | bytes 1245184 | tf_op jit(solution)/shard_map/all_to_all | solution.py:60
  324.0 5.1 %copy-start.6 = (s32[96]{0:T(128)S(1)}, s32[96]{0:T(128)}, u32[]{:S(2)}) copy-start(s32[96]{0:T(128)} %param.8) | copy-start | bytes 1156
  325.6 7.3 %copy-start.1 = (f32[192,2400]{1,0:T(8,128)S(1)}, f32[192,2400]{1,0:T(8,128)}, u32[]{:S(2)}) copy-start(f32[192,2400]{1,0:T(8,128)} %fusion.8) | copy-start | bytes 5529604
  325.6 29.0 %all-to-all-start.6 = ((f32[32,128,64]{1,2,0:T(8,128)}), f32[32,128,64]{1,2,0:T(8,128)S(1)}, u32[]{:S(2)}, u32[]{:S(2)}) async-start(f32[32,128,64]{1,2,0:T(8,128)} %bitcast.32), calls=%async_computation.6 | async-start | bytes 2097152 | tf_op jit(solution)/shard_map/all_to_all | solution.py:73
Sparse Core Ops, SparseCore 0:
  11.0 96.4 all-gather.6
  109.0 92.1 all-gather.4
  202.8 39.7 all-gather.8
  244.0 40.2 all-gather.10

commit v18 on v12

--- a/solution.py
+++ b/solution.py
@@ -63,18 +63,10 @@
     gathered = lax.all_to_all(parts, ("int", "amp"), split_axis=0, concat_axis=0, tiled=True)
     sums = jnp.sum(gathered, axis=0)
 
-    row_start = lax.axis_index("int") * i_local
-    batch_labels = lax.dynamic_slice_in_dim(occ_irrep, row_start, i_local, 0)
-    slab_labels = vir_irrep[:slab]
-    row_labels = jnp.bitwise_xor(batch_labels[:, None], slab_labels[None, :]).reshape(-1)
-    col_ids = lax.axis_index("amp") * col_local + jnp.arange(col_local, dtype=jnp.int32)
-    col_occ = col_ids // slab
-    col_vir = col_ids % slab
-    occ_match = col_occ[:, None] == jnp.arange(nocc, dtype=jnp.int32)[None, :]
-    vir_match = col_vir[:, None] == jnp.arange(slab, dtype=jnp.int32)[None, :]
-    occ_lookup = jnp.sum(jnp.where(occ_match, occ_irrep[None, :], 0), axis=1)
-    vir_lookup = jnp.sum(jnp.where(vir_match, slab_labels[None, :], 0), axis=1)
-    col_labels = jnp.bitwise_xor(occ_lookup, vir_lookup)
+    labels = jnp.bitwise_xor(occ_irrep[:ibat, None], vir_irrep[None, :slab]).reshape(-1)
+    rows_local = i_local * slab
+    row_labels = lax.dynamic_slice_in_dim(labels, lax.axis_index("int") * rows_local, rows_local, 0)
+    col_labels = lax.dynamic_slice_in_dim(labels, lax.axis_index("amp") * col_local, col_local, 0)
     keep = row_labels[:, None] == col_labels[None, :]
     cycle = jnp.where(keep, sums, jnp.zeros_like(sums))
     return (ladder, cycle)

time: 355 us -> 355 us (level)
  transfers between devices with their start and end apart: 9 -> 9, of which waited for: 8 -> 8; matrix products, arithmetic and copies ran while one was open for 29% -> 28% of each run, Pallas kernels for 0% -> 0%
where the time goes in v18:
time: 355 us; the launch traced here: 354 us
  waiting for transfers between devices  174 us (49%)
  local copies, waits for them, and re-layouts  67.5 us (19%)
  matrix products  50.8 us (14%)
  blocking collectives  27.5 us (8%)
  starting transfers between devices  18.2 us (5%)
  between operations  14 us (4%)
    all_gather x4, waiting for transfers between devices, per_device(): v_all = lax.all_gather(v, 'int', axis=0, tiled=True)  106 us
    all_to_all x4, waiting for transfers between devices, per_device(): lax.all_to_all(l_cyc, 'amp', split_axis=0, concat_axis=0, tiled=True)  50.6 us
    all_to_all x1, blocking collectives, per_device(): lax.all_to_all(amplitudes.reshape(i_local, nocc, pw), 'int', split_axis=1...  27.5 us
    reshape x4, local copies, waits for them, and re-layouts, per_device(): l_cyc = l_cyc.reshape(n_amp, ibat * a_chunk, c_local * k_local)  18.6 us
    dot_general x4, matrix products, per_device(): jnp.dot(moved, w2, precision=PRECISION, preferred_element_type=jnp.float32)  18.4 us
    dot_general x4, matrix products, per_device(): jnp.dot(amplitudes, v_all, precision=PRECISION, preferred_element_type=jn...  17.5 us
    all_to_all x1, waiting for transfers between devices, per_device(): lax.all_to_all(parts, ('int', 'amp'), split_axis=0, concat_axis=0, tiled=...  16.7 us
    reshape x6, local copies, waits for them, and re-layouts, per_device(): l_cyc.reshape(ibat, k_local, a_chunk, n_amp, c_local)  15.2 us
  transfers between devices with their start and end apart: 9, of which 8 were waited for; matrix products, arithmetic and copies ran while one was open for 28% of the time, Pallas kernels for 0%

profile of v18, /device:TPU:0, one launch (start us, length us, event | category | flops | bytes accessed | tf_op | source)
XLA Modules:
  0.0 353.6 jit_solution(11521295411177690165)
XLA Ops:
  12.2 27.5 %all_to_all.40 = f32[2,96,512]{2,0,1:T(2,128)S(1)} all-to-all(f32[2,96,512]{2,0,1:T(2,128)S(1)} %copy.44), channel_id=1, replica_groups=mesh['amp'=8,'int'=4] {'int'}, dimensions={1} | all-to-all | bytes 786432 | tf_op jit(solution)/shard_map/all_to_all | solution.py:29
  39.8 71.0 %all-gather.7.cloned.1.call-done = f32[512,2400]{1,0:T(8,128)} async-done(((f32[128,2400]{1,0:T(8,128)}), f32[512,2400]{1,0:T(8,128)}) %all-gather.7.cloned.1.call-update) | async-done | bytes 4915216 | tf_op jit(solution)/shard_map/all_gather | solution.py:39
  110.8 5.7 %copy.47 = f32[2400,512]{1,0:T(8,128)} copy(f32[2400,512]{0,1:T(8,128)} %bitcast.80) | data formatting | bytes 9830400 | tf_op jit(solution)/shard_map/dot_general | solution.py:47
  116.5 5.5 %reshape.98 = f32[3,8,100,512,1]{3,2,1,0,4:T(8,128)} reshape(f32[2400,512]{1,0:T(8,128)} %copy.47) | data formatting | bytes 9830400 | tf_op jit(solution)/shard_map/dot_general | solution.py:47
  122.0 4.9 %convolution_bitcast_fusion.2 = f32[8,8,3,100,24]{3,4,0,2,1:T(8,128)S(1)} fusion(f32[8,24,512,1,1]{2,1,4,3,0:T(8,128)S(1)} %bitcast.83, f32[3,8,100,512,1]{3,2,1,0,4:T(8,128)} %reshape.98), kind=kOutput, calls=%fused_computation.2 | convolution fusion | flops 1415577600 | bytes 7151616 | tf_op jit(solution)/shard_map/dot_general | solution.py:47
  126.9 5.7 %copy.48 = f32[8,8,3,100,24]{4,3,2,1,0:T(8,128)} copy(f32[8,8,3,100,24]{3,4,0,2,1:T(8,128)S(1)} %convolution_bitcast_fusion.2) | data formatting | bytes 3686400 | tf_op jit(solution)/shard_map/transpose | solution.py:48
  132.6 7.6 %reshape.80 = f32[8,24,2400]{2,1,0:T(8,128)} reshape(f32[8,8,3,100,24]{4,3,2,1,0:T(8,128)} %copy.48) | data formatting | bytes 3686400 | tf_op jit(solution)/shard_map/reshape | solution.py:49
  146.7 5.6 %fusion.4 = f32[192,2400]{1,0:T(8,128)} fusion(f32[192,512]{1,0:T(8,128)S(1)} %copy-done.2, f32[512,2400]{1,0:T(8,128)} %all-gather.7.cloned.1.call-done), kind=kOutput, calls=%fused_computation.15 | convolution fusion | flops 1415577600 | bytes 7151616 | tf_op jit(solution)/shard_map/dot_general | solution.py:45
  152.3 15.8 %all-to-all-done.1 = f32[8,24,2400]{2,1,0:T(8,128)S(1)} async-done(((f32[8,24,2400]{2,1,0:T(8,128)}), f32[8,24,2400]{2,1,0:T(8,128)S(1)}, u32[]{:S(2)}, u32[]{:S(2)}) %all-to-all-start.1) | async-done | bytes 1843232 | tf_op jit(solution)/shard_map/all_to_all | solution.py:50
  168.1 5.1 %fusion.5 = f32[192,512]{1,0:T(8,128)} fusion(f32[192,2400]{1,0:T(8,128)S(1)} %bitcast.89, f32[2400,512]{1,0:T(8,128)} %bitcast.75), kind=kOutput, calls=%fused_computation.16 | convolution fusion | flops 1415577600 | bytes 7151616 | tf_op jit(solution)/shard_map/dot_general | solution.py:53
  173.2 32.0 %all-gather.5.cloned.1.call-done = f32[512,2400]{1,0:T(8,128)} async-done(((f32[128,2400]{1,0:T(8,128)}), f32[512,2400]{1,0:T(8,128)}) %all-gather.5.cloned.1.call-update) | async-done | bytes 4915216 | tf_op jit(solution)/shard_map/all_gather | solution.py:39
  205.2 5.4 %convolution_bitcast_fusion = f32[192,2400]{1,0:T(8,128)} fusion(f32[512,2400]{1,0:T(8,128)} %all-gather.5.cloned.1.call-done, f32[192,512]{1,0:T(8,128)S(1)} %bitcast.84), kind=kOutput, calls=%fused_computation | convolution fusion | flops 1415577600 | bytes 7151616 | tf_op jit(solution)/shard_map/dot_general | solution.py:47
  213.3 5.6 %copy.50 = f32[8,24,3,8,100]{1,4,2,0,3:T(8,128)} copy(f32[8,24,3,8,100]{4,3,2,1,0:T(8,128)S(1)} %reshape.84) | data formatting | bytes 3686400 | tf_op jit(solution)/shard_map/reshape | solution.py:48
  218.9 7.6 %reshape.85 = f32[8,24,2400]{2,1,0:T(8,128)} reshape(f32[8,8,3,100,24]{4,3,2,1,0:T(8,128)} %bitcast.79) | data formatting | bytes 3686400 | tf_op jit(solution)/shard_map/reshape | solution.py:49
  230.6 5.5 %convolution_bitcast_fusion.1 = f32[192,2400]{1,0:T(8,128)} fusion(f32[512,2400]{1,0:T(8,128)} %all-gather.5.cloned.1.call-done, f32[192,512]{1,0:T(8,128)S(1)} %copy-done.2), kind=kOutput, calls=%fused_computation.1 | convolution fusion | flops 1415577600 | bytes 7151616 | tf_op jit(solution)/shard_map/dot_general | solution.py:45
  236.1 18.1 %all-to-all-done.2 = f32[8,24,2400]{2,1,0:T(8,128)S(1)} async-done(((f32[8,24,2400]{2,1,0:T(8,128)}), f32[8,24,2400]{2,1,0:T(8,128)S(1)}, u32[]{:S(2)}, u32[]{:S(2)}) %all-to-all-start.2) | async-done | bytes 1843232 | tf_op jit(solution)/shard_map/all_to_all | solution.py:50
  254.2 5.3 %fusion.6 = f32[192,512]{1,0:T(8,128)} fusion(f32[192,2400]{1,0:T(8,128)S(1)} %bitcast.90, f32[2400,512]{1,0:T(8,128)} %bitcast.76), kind=kOutput, calls=%fused_computation.17 | convolution fusion | flops 1415577600 | bytes 7151616 | tf_op jit(solution)/shard_map/dot_general | solution.py:53
  273.9 7.5 %all-to-all-done.3 = f32[8,8,2400]{2,1,0:T(8,128)S(1)} async-done(((f32[8,8,2400]{2,1,0:T(8,128)}), f32[8,8,2400]{2,1,0:T(8,128)S(1)}, u32[]{:S(2)}, u32[]{:S(2)}) %all-to-all-start.3) | async-done | bytes 614432 | tf_op jit(solution)/shard_map/all_to_all | solution.py:50
  281.4 4.0 %fusion = f32[64,512]{1,0:T(8,128)S(1)} fusion(f32[2400,512]{1,0:T(8,128)} %bitcast.77, f32[8,8,2400]{2,1,0:T(8,128)S(1)} %all-to-all-done.3), kind=kOutput, calls=%fused_computation.9 | convolution fusion | flops 471859200 | bytes 5660672 | tf_op jit(solution)/shard_map/dot_general | solution.py:53
  295.9 3.9 %all-to-all-start.4 = ((f32[8,8,2400]{2,1,0:T(8,128)}), f32[8,8,2400]{2,1,0:T(8,128)S(1)}, u32[]{:S(2)}, u32[]{:S(2)}) async-start(f32[8,8,2400]{2,1,0:T(8,128)} %reshape.94), calls=%async_computation.4 | async-start | bytes 1245184 | tf_op jit(solution)/shard_map/all_to_all | solution.py:50
  301.4 9.2 %all-to-all-done.4 = f32[8,8,2400]{2,1,0:T(8,128)S(1)} async-done(((f32[8,8,2400]{2,1,0:T(8,128)}), f32[8,8,2400]{2,1,0:T(8,128)S(1)}, u32[]{:S(2)}, u32[]{:S(2)}) %all-to-all-start.4) | async-done | bytes 614432 | tf_op jit(solution)/shard_map/all_to_all | solution.py:50
  310.5 4.0 %convolution_bitcast_fusion.7 = f32[8,8,1,512]{3,1,0,2:T(8,128)S(1)} fusion(f32[8,8,2400]{2,1,0:T(8,128)S(1)} %all-to-all-done.4, f32[2400,512,1]{1,0,2:T(8,128)} %bitcast.78), kind=kOutput, calls=%fused_computation.7 | convolution fusion | flops 471859200 | bytes 5660672 | tf_op jit(solution)/shard_map/dot_general | solution.py:53
  323.6 6.0 %concatenate.6 = f32[192,6400]{1,0:T(8,128)} concatenate(f32[192,2400]{1,0:T(8,128)S(1)} %copy-done.4, f32[192,2400]{1,0:T(8,128)} %convolution_bitcast_fusion.1, f32[192,800]{1,0:T(8,128)} %convolution_bitcast_fusion.6, f32[192,800]{1,0:T(8,128)} %convolution_bitcast_fusion.4), dimensions={1} | concatenate | bytes 9830400 | tf_op jit(solution)/shard_map/concatenate | solution.py:55
  329.7 16.7 %all-to-all-done.5 = f32[32,128,64]{1,2,0:T(8,128)S(1)} async-done(((f32[32,128,64]{1,2,0:T(8,128)}), f32[32,128,64]{1,2,0:T(8,128)S(1)}, u32[]{:S(2)}, u32[]{:S(2)}) %all-to-all-start.5) | async-done | bytes 1048608 | tf_op jit(solution)/shard_map/all_to_all | solution.py:63
  (60 shorter events, 54.5 us)
Async XLA Ops:
  7.2 103.6 %all-gather.7.cloned.1.call-start = ((), (), s32[]{:S(2)}) async-start(), calls=%async_computation.7 | async-start | bytes 6225920 | tf_op jit(solution)/shard_map/all_gather | solution.py:39
  10.9 1.0 copy-start.2
  10.9 194.3 %all-gather.5.cloned.1.call-start = ((), (), s32[]{:S(2)}) async-start(), calls=%async_computation.6 | async-start | bytes 6225920 | tf_op jit(solution)/shard_map/all_gather | solution.py:39
  39.7 219.8 %copy-start = (f32[4,2,24,512]{3,2,1,0:T(8,128)}, f32[4,2,24,512]{3,2,1,0:T(8,128)S(1)}, u32[]{:S(2)}) copy-start(f32[4,2,24,512]{3,2,1,0:T(8,128)S(1)} %copy.46) | copy-start | bytes 1179652
  140.1 28.0 %all-to-all-start.1 = ((f32[8,24,2400]{2,1,0:T(8,128)}), f32[8,24,2400]{2,1,0:T(8,128)S(1)}, u32[]{:S(2)}, u32[]{:S(2)}) async-start(f32[8,24,2400]{2,1,0:T(8,128)} %reshape.80), calls=%async_computation.1 | async-start | bytes 3735552 | tf_op jit(solution)/shard_map/all_to_all | solution.py:50
  143.9 115.6 %all-gather.9.cloned.1.call-start = ((), (), s32[]{:S(2)}) async-start(), calls=%async_computation.8 | async-start | bytes 2293760 | tf_op jit(solution)/shard_map/all_gather | solution.py:39
  226.4 27.8 %all-to-all-start.2 = ((f32[8,24,2400]{2,1,0:T(8,128)}), f32[8,24,2400]{2,1,0:T(8,128)S(1)}, u32[]{:S(2)}, u32[]{:S(2)}) async-start(f32[8,24,2400]{2,1,0:T(8,128)} %reshape.85), calls=%async_computation.2 | async-start | bytes 3735552 | tf_op jit(solution)/shard_map/all_to_all | solution.py:50
  230.0 58.3 %all-gather.11.cloned.1.call-start = ((), (), s32[]{:S(2)}) async-start(), calls=%async_computation.9 | async-start | bytes 2293760 | tf_op jit(solution)/shard_map/all_gather | solution.py:39
  267.1 14.3 %all-to-all-start.3 = ((f32[8,8,2400]{2,1,0:T(8,128)}), f32[8,8,2400]{2,1,0:T(8,128)S(1)}, u32[]{:S(2)}, u32[]{:S(2)}) async-start(f32[8,8,2400]{2,1,0:T(8,128)} %reshape.88), calls=%async_computation.3 | async-start | bytes 1245184 | tf_op jit(solution)/shard_map/all_to_all | solution.py:50
  273.9 14.5 %copy-start.1 = (f32[4,2,24,512]{3,2,1,0:T(8,128)S(1)}, f32[4,2,24,512]{3,2,1,0:T(8,128)}, u32[]{:S(2)}) copy-start(f32[4,2,24,512]{3,2,1,0:T(8,128)} %copy-done) | copy-start | bytes 1179652
  295.9 5.1 %copy-start.5 = (f32[192,512]{1,0:T(8,128)S(1)}, f32[192,512]{1,0:T(8,128)}, u32[]{:S(2)}) copy-start(f32[192,512]{1,0:T(8,128)} %fusion.6) | copy-start | bytes 1179652
  295.9 14.6 %all-to-all-start.4 = ((f32[8,8,2400]{2,1,0:T(8,128)}), f32[8,8,2400]{2,1,0:T(8,128)S(1)}, u32[]{:S(2)}, u32[]{:S(2)}) async-start(f32[8,8,2400]{2,1,0:T(8,128)} %reshape.94), calls=%async_computation.4 | async-start | bytes 1245184 | tf_op jit(solution)/shard_map/all_to_all | solution.py:50
  315.7 4.4 %copy-start.6 = (s32[96]{0:T(128)S(1)}, s32[96]{0:T(128)}, u32[]{:S(2)}) copy-start(s32[96]{0:T(128)} %param.8) | copy-start | bytes 1156
  315.7 4.4 %slice-start = ((s32[800]{0:T(1024)}), s32[64]{0:T(128)S(1)}, s32[]{:S(2)}) async-start(s32[800]{0:T(1024)} %param.9), calls=%async_computation.10 | async-start | bytes 1024 | tf_op jit(solution)/shard_map/slice | solution.py:66
  315.7 4.7 %copy-start.3 = (f32[192,512]{1,0:T(8,128)S(1)}, f32[192,512]{1,0:T(8,128)}, u32[]{:S(2)}) copy-start(f32[192,512]{1,0:T(8,128)} %param.5) | copy-start | bytes 1179652
  317.3 6.3 %copy-start.4 = (f32[192,2400]{1,0:T(8,128)S(1)}, f32[192,2400]{1,0:T(8,128)}, u32[]{:S(2)}) copy-start(f32[192,2400]{1,0:T(8,128)} %fusion.4) | copy-start | bytes 5529604
  317.3 29.0 %all-to-all-start.5 = ((f32[32,128,64]{1,2,0:T(8,128)}), f32[32,128,64]{1,2,0:T(8,128)S(1)}, u32[]{:S(2)}, u32[]{:S(2)}) async-start(f32[32,128,64]{1,2,0:T(8,128)} %bitcast.30), calls=%async_computation.5 | async-start | bytes 2097152 | tf_op jit(solution)/shard_map/all_to_all | solution.py:63
Sparse Core Ops, SparseCore 0:
  11.0 99.7 all-gather.6
  112.3 92.8 all-gather.4
  206.8 39.7 all-gather.8
  248.1 40.2 all-gather.10

commit v19 on v16

--- a/solution.py
+++ b/solution.py
@@ -74,18 +74,10 @@
     gathered = lax.all_to_all(parts, ("int", "amp"), split_axis=0, concat_axis=0, tiled=True)
     sums = jnp.sum(gathered, axis=0)
 
-    row_start = lax.axis_index("int") * i_local
-    batch_labels = lax.dynamic_slice_in_dim(occ_irrep, row_start, i_local, 0)
-    slab_labels = vir_irrep[:slab]
-    row_labels = jnp.bitwise_xor(batch_labels[:, None], slab_labels[None, :]).reshape(-1)
-    col_ids = lax.axis_index("amp") * col_local + jnp.arange(col_local, dtype=jnp.int32)
-    col_occ = col_ids // slab
-    col_vir = col_ids % slab
-    occ_match = col_occ[:, None] == jnp.arange(nocc, dtype=jnp.int32)[None, :]
-    vir_match = col_vir[:, None] == jnp.arange(slab, dtype=jnp.int32)[None, :]
-    occ_lookup = jnp.sum(jnp.where(occ_match, occ_irrep[None, :], 0), axis=1)
-    vir_lookup = jnp.sum(jnp.where(vir_match, slab_labels[None, :], 0), axis=1)
-    col_labels = jnp.bitwise_xor(occ_lookup, vir_lookup)
+    labels = jnp.bitwise_xor(occ_irrep[:ibat, None], vir_irrep[None, :slab]).reshape(-1)
+    rows_local = i_local * slab
+    row_labels = lax.dynamic_slice_in_dim(labels, lax.axis_index("int") * rows_local, rows_local, 0)
+    col_labels = lax.dynamic_slice_in_dim(labels, lax.axis_index("amp") * col_local, col_local, 0)
     keep = row_labels[:, None] == col_labels[None, :]
     cycle = jnp.where(keep, sums, jnp.zeros_like(sums))
     return (ladder, cycle)

time: 356 us -> 356 us (level)
  transfers between devices with their start and end apart: 9 -> 9, of which waited for: 7 -> 7; matrix products, arithmetic and copies ran while one was open for 29% -> 28% of each run, Pallas kernels for 0% -> 0%
where the time goes in v19:
time: 356 us; the launch traced here: 355 us
  waiting for transfers between devices  174 us (49%)
  local copies, waits for them, and re-layouts  68.5 us (19%)
  matrix products  50.8 us (14%)
  blocking collectives  27.5 us (8%)
  starting transfers between devices  18.3 us (5%)
  between operations  14 us (4%)
    all_gather x4, waiting for transfers between devices, per_device(): v_all = lax.all_gather(v, 'int', axis=0, tiled=True)  117 us
    all_to_all x4, waiting for transfers between devices, per_device(): lax.all_to_all(l_cyc, 'amp', split_axis=0, concat_axis=0, tiled=True)  39.1 us
    all_to_all x1, blocking collectives, per_device(): lax.all_to_all(amplitudes.reshape(i_local, nocc, pw), 'int', split_axis=1...  27.5 us
    reshape x4, local copies, waits for them, and re-layouts, per_device(): l_cyc = l_cyc.reshape(n_amp, ibat * a_chunk, c_local * k_local)  18.7 us
    dot_general x4, matrix products, per_device(): jnp.dot(amplitudes, v_all, precision=PRECISION, preferred_element_type=jn...  17.5 us
    all_to_all x1, waiting for transfers between devices, per_device(): lax.all_to_all(parts, ('int', 'amp'), split_axis=0, concat_axis=0, tiled=...  16.7 us
    reshape x6, local copies, waits for them, and re-layouts, per_device(): l_cyc.reshape(ibat, k_local, a_chunk, n_amp, c_local)  15.3 us
    all_to_all x4, starting transfers between devices, per_device(): lax.all_to_all(l_cyc, 'amp', split_axis=0, concat_axis=0, tiled=True)  15 us
  transfers between devices with their start and end apart: 9, of which 7 were waited for; matrix products, arithmetic and copies ran while one was open for 28% of the time, Pallas kernels for 0%

profile of v19, /device:TPU:0, one launch (start us, length us, event | category | flops | bytes accessed | tf_op | source)
XLA Modules:
  0.0 354.5 jit_solution(2008569485217853142)
XLA Ops:
  12.1 27.5 %all_to_all.40 = f32[2,96,512]{2,0,1:T(2,128)S(1)} all-to-all(f32[2,96,512]{2,0,1:T(2,128)S(1)} %copy.44), channel_id=1, replica_groups=mesh['amp'=8,'int'=4] {'int'}, dimensions={1} | all-to-all | bytes 786432 | tf_op jit(solution)/shard_map/all_to_all | solution.py:29
  39.7 71.0 %all-gather.7.cloned.1.call-done = f32[512,2400]{1,0:T(8,128)} async-done(((f32[128,2400]{1,0:T(8,128)}), f32[512,2400]{1,0:T(8,128)}) %all-gather.7.cloned.1.call-update) | async-done | bytes 4915216 | tf_op jit(solution)/shard_map/all_gather | solution.py:40
  110.8 5.7 %copy.47 = f32[2400,512]{1,0:T(8,128)} copy(f32[2400,512]{0,1:T(8,128)} %bitcast.82) | data formatting | bytes 9830400 | tf_op jit(solution)/shard_map/dot_general | solution.py:50
  116.5 5.5 %reshape.100 = f32[3,8,100,512,1]{3,2,1,0,4:T(8,128)} reshape(f32[2400,512]{1,0:T(8,128)} %copy.47) | data formatting | bytes 9830400 | tf_op jit(solution)/shard_map/dot_general | solution.py:50
  122.0 4.9 %convolution_bitcast_fusion.2 = f32[8,8,3,100,24]{3,4,0,2,1:T(8,128)S(1)} fusion(f32[8,24,512,1,1]{2,1,4,3,0:T(8,128)S(1)} %bitcast.85, f32[3,8,100,512,1]{3,2,1,0,4:T(8,128)} %reshape.100), kind=kOutput, calls=%fused_computation.2 | convolution fusion | flops 1415577600 | bytes 7151616 | tf_op jit(solution)/shard_map/dot_general | solution.py:50
  126.9 5.7 %copy.48 = f32[8,8,3,100,24]{4,3,2,1,0:T(8,128)} copy(f32[8,8,3,100,24]{3,4,0,2,1:T(8,128)S(1)} %convolution_bitcast_fusion.2) | data formatting | bytes 3686400 | tf_op jit(solution)/shard_map/transpose | solution.py:51
  132.6 7.6 %reshape.83 = f32[8,24,2400]{2,1,0:T(8,128)} reshape(f32[8,8,3,100,24]{4,3,2,1,0:T(8,128)} %copy.48) | data formatting | bytes 3686400 | tf_op jit(solution)/shard_map/reshape | solution.py:52
  146.7 5.6 %fusion.3 = f32[192,2400]{1,0:T(8,128)} fusion(f32[192,512]{1,0:T(8,128)S(1)} %copy-done.2, f32[512,2400]{1,0:T(8,128)} %all-gather.7.cloned.1.call-done), kind=kOutput, calls=%fused_computation.15 | convolution fusion | flops 1415577600 | bytes 7151616 | tf_op jit(solution)/shard_map/dot_general | solution.py:48
  152.3 15.8 %all-to-all-done.1 = f32[8,24,2400]{2,1,0:T(8,128)S(1)} async-done(((f32[8,24,2400]{2,1,0:T(8,128)}), f32[8,24,2400]{2,1,0:T(8,128)S(1)}, u32[]{:S(2)}, u32[]{:S(2)}) %all-to-all-start.1) | async-done | bytes 1843232 | tf_op jit(solution)/shard_map/all_to_all | solution.py:53
  168.2 5.1 %fusion.4 = f32[192,512]{1,0:T(8,128)} fusion(f32[192,2400]{1,0:T(8,128)S(1)} %bitcast.91, f32[2400,512]{1,0:T(8,128)} %bitcast.77), kind=kOutput, calls=%fused_computation.16 | convolution fusion | flops 1415577600 | bytes 7151616 | tf_op jit(solution)/shard_map/dot_general | solution.py:64
  173.2 32.0 %all-gather.5.cloned.1.call-done = f32[512,2400]{1,0:T(8,128)} async-done(((f32[128,2400]{1,0:T(8,128)}), f32[512,2400]{1,0:T(8,128)}) %all-gather.5.cloned.1.call-update) | async-done | bytes 4915216 | tf_op jit(solution)/shard_map/all_gather | solution.py:40
  205.2 5.5 %convolution_bitcast_fusion = f32[192,2400]{1,0:T(8,128)} fusion(f32[512,2400]{1,0:T(8,128)} %all-gather.5.cloned.1.call-done, f32[192,512]{1,0:T(8,128)S(1)} %bitcast.86), kind=kOutput, calls=%fused_computation | convolution fusion | flops 1415577600 | bytes 7151616 | tf_op jit(solution)/shard_map/dot_general | solution.py:50
  213.3 5.6 %copy.50 = f32[8,24,3,8,100]{1,4,2,0,3:T(8,128)} copy(f32[8,24,3,8,100]{4,3,2,1,0:T(8,128)S(1)} %reshape.87) | data formatting | bytes 3686400 | tf_op jit(solution)/shard_map/reshape | solution.py:51
  219.0 7.6 %reshape.88 = f32[8,24,2400]{2,1,0:T(8,128)} reshape(f32[8,8,3,100,24]{4,3,2,1,0:T(8,128)} %bitcast.81) | data formatting | bytes 3686400 | tf_op jit(solution)/shard_map/reshape | solution.py:52
  230.7 5.5 %convolution_bitcast_fusion.1 = f32[192,2400]{1,0:T(8,128)} fusion(f32[512,2400]{1,0:T(8,128)} %all-gather.5.cloned.1.call-done, f32[192,512]{1,0:T(8,128)S(1)} %copy-done.2), kind=kOutput, calls=%fused_computation.1 | convolution fusion | flops 1415577600 | bytes 7151616 | tf_op jit(solution)/shard_map/dot_general | solution.py:48
  236.2 18.1 %all-to-all-done.2 = f32[8,24,2400]{2,1,0:T(8,128)S(1)} async-done(((f32[8,24,2400]{2,1,0:T(8,128)}), f32[8,24,2400]{2,1,0:T(8,128)S(1)}, u32[]{:S(2)}, u32[]{:S(2)}) %all-to-all-start.2) | async-done | bytes 1843232 | tf_op jit(solution)/shard_map/all_to_all | solution.py:53
  254.3 5.3 %fusion.5 = f32[192,512]{1,0:T(8,128)} fusion(f32[192,2400]{1,0:T(8,128)S(1)} %bitcast.92, f32[2400,512]{1,0:T(8,128)} %bitcast.78), kind=kOutput, calls=%fused_computation.17 | convolution fusion | flops 1415577600 | bytes 7151616 | tf_op jit(solution)/shard_map/dot_general | solution.py:64
  274.1 14.3 %all-gather.11.cloned.1.call-done = f32[512,800]{1,0:T(8,128)} async-done(((f32[128,800]{1,0:T(8,128)}), f32[512,800]{1,0:T(8,128)}) %all-gather.11.cloned.1.call-update) | async-done | bytes 1638416 | tf_op jit(solution)/shard_map/all_gather | solution.py:40
  296.8 3.9 %all-to-all-start.4 = ((f32[8,8,2400]{2,1,0:T(8,128)}), f32[8,8,2400]{2,1,0:T(8,128)S(1)}, u32[]{:S(2)}, u32[]{:S(2)}) async-start(f32[8,8,2400]{2,1,0:T(8,128)} %reshape.96), calls=%async_computation.4 | async-start | bytes 1245184 | tf_op jit(solution)/shard_map/all_to_all | solution.py:53
  302.1 4.0 %convolution_bitcast_fusion.8 = f32[8,8,1,512]{3,1,0,2:T(8,128)S(1)} fusion(f32[2400,512,1]{1,0,2:T(8,128)} %bitcast.79, f32[64,2400]{1,0:T(8,128)S(1)} %bitcast.93), kind=kOutput, calls=%fused_computation.8 | convolution fusion | flops 471859200 | bytes 5660672 | tf_op jit(solution)/shard_map/dot_general | solution.py:57
  306.3 5.1 %all-to-all-done.4 = f32[8,8,2400]{2,1,0:T(8,128)S(1)} async-done(((f32[8,8,2400]{2,1,0:T(8,128)}), f32[8,8,2400]{2,1,0:T(8,128)S(1)}, u32[]{:S(2)}, u32[]{:S(2)}) %all-to-all-start.4) | async-done | bytes 614432 | tf_op jit(solution)/shard_map/all_to_all | solution.py:53
  311.4 4.0 %convolution_bitcast_fusion.7 = f32[8,8,1,512]{3,1,0,2:T(8,128)S(1)} fusion(f32[8,8,2400]{2,1,0:T(8,128)S(1)} %all-to-all-done.4, f32[2400,512,1]{1,0,2:T(8,128)} %bitcast.80), kind=kOutput, calls=%fused_computation.7 | convolution fusion | flops 471859200 | bytes 5660672 | tf_op jit(solution)/shard_map/dot_general | solution.py:64
  324.5 6.0 %concatenate.6 = f32[192,6400]{1,0:T(8,128)} concatenate(f32[192,2400]{1,0:T(8,128)S(1)} %copy-done.4, f32[192,2400]{1,0:T(8,128)} %convolution_bitcast_fusion.1, f32[192,800]{1,0:T(8,128)} %convolution_bitcast_fusion.6, f32[192,800]{1,0:T(8,128)} %convolution_bitcast_fusion.4), dimensions={1} | concatenate | bytes 9830400 | tf_op jit(solution)/shard_map/concatenate | solution.py:66
  330.5 16.7 %all-to-all-done.5 = f32[32,128,64]{1,2,0:T(8,128)S(1)} async-done(((f32[32,128,64]{1,2,0:T(8,128)}), f32[32,128,64]{1,2,0:T(8,128)S(1)}, u32[]{:S(2)}, u32[]{:S(2)}) %all-to-all-start.5) | async-done | bytes 1048608 | tf_op jit(solution)/shard_map/all_to_all | solution.py:74
  (64 shorter events, 52.5 us)
Async XLA Ops:
  7.2 103.6 %all-gather.7.cloned.1.call-start = ((), (), s32[]{:S(2)}) async-start(), calls=%async_computation.7 | async-start | bytes 6225920 | tf_op jit(solution)/shard_map/all_gather | solution.py:40
  10.8 1.0 copy-start.2
  10.9 194.3 %all-gather.5.cloned.1.call-start = ((), (), s32[]{:S(2)}) async-start(), calls=%async_computation.6 | async-start | bytes 6225920 | tf_op jit(solution)/shard_map/all_gather | solution.py:40
  39.7 219.8 %copy-start = (f32[4,2,24,512]{3,2,1,0:T(8,128)}, f32[4,2,24,512]{3,2,1,0:T(8,128)S(1)}, u32[]{:S(2)}) copy-start(f32[4,2,24,512]{3,2,1,0:T(8,128)S(1)} %copy.46) | copy-start | bytes 1179652
  140.2 28.0 %all-to-all-start.1 = ((f32[8,24,2400]{2,1,0:T(8,128)}), f32[8,24,2400]{2,1,0:T(8,128)S(1)}, u32[]{:S(2)}, u32[]{:S(2)}) async-start(f32[8,24,2400]{2,1,0:T(8,128)} %reshape.83), calls=%async_computation.1 | async-start | bytes 3735552 | tf_op jit(solution)/shard_map/all_to_all | solution.py:53
  144.0 115.6 %all-gather.9.cloned.1.call-start = ((), (), s32[]{:S(2)}) async-start(), calls=%async_computation.8 | async-start | bytes 2293760 | tf_op jit(solution)/shard_map/all_gather | solution.py:40
  226.5 27.8 %all-to-all-start.2 = ((f32[8,24,2400]{2,1,0:T(8,128)}), f32[8,24,2400]{2,1,0:T(8,128)S(1)}, u32[]{:S(2)}, u32[]{:S(2)}) async-start(f32[8,24,2400]{2,1,0:T(8,128)} %reshape.88), calls=%async_computation.2 | async-start | bytes 3735552 | tf_op jit(solution)/shard_map/all_to_all | solution.py:53
  230.1 58.2 %all-gather.11.cloned.1.call-start = ((), (), s32[]{:S(2)}) async-start(), calls=%async_computation.9 | async-start | bytes 2293760 | tf_op jit(solution)/shard_map/all_gather | solution.py:40
  267.2 22.1 %copy-start.1 = (f32[4,2,24,512]{3,2,1,0:T(8,128)S(1)}, f32[4,2,24,512]{3,2,1,0:T(8,128)}, u32[]{:S(2)}) copy-start(f32[4,2,24,512]{3,2,1,0:T(8,128)} %copy-done) | copy-start | bytes 1179652
  267.2 21.2 %all-to-all-start.3 = ((f32[8,8,2400]{2,1,0:T(8,128)}), f32[8,8,2400]{2,1,0:T(8,128)S(1)}, u32[]{:S(2)}, u32[]{:S(2)}) async-start(f32[8,8,2400]{2,1,0:T(8,128)} %reshape.91), calls=%async_computation.3 | async-start | bytes 1245184 | tf_op jit(solution)/shard_map/all_to_all | solution.py:53
  288.4 0.9 copy-start.5
  296.8 5.1 %copy-start.7 = (f32[192,512]{1,0:T(8,128)S(1)}, f32[192,512]{1,0:T(8,128)}, u32[]{:S(2)}) copy-start(f32[192,512]{1,0:T(8,128)} %fusion.5) | copy-start | bytes 1179652
  296.8 5.3 %copy-start.6 = (f32[8,8,2400]{2,1,0:T(8,128)S(1)}, f32[8,8,2400]{2,1,0:T(8,128)}, u32[]{:S(2)}) copy-start(f32[8,8,2400]{2,1,0:T(8,128)} %copy-done.5) | copy-start | bytes 1843204
  296.8 14.6 %all-to-all-start.4 = ((f32[8,8,2400]{2,1,0:T(8,128)}), f32[8,8,2400]{2,1,0:T(8,128)S(1)}, u32[]{:S(2)}, u32[]{:S(2)}) async-start(f32[8,8,2400]{2,1,0:T(8,128)} %reshape.96), calls=%async_computation.4 | async-start | bytes 1245184 | tf_op jit(solution)/shard_map/all_to_all | solution.py:53
  316.6 4.4 %copy-start.8 = (s32[96]{0:T(128)S(1)}, s32[96]{0:T(128)}, u32[]{:S(2)}) copy-start(s32[96]{0:T(128)} %param.8) | copy-start | bytes 1156
  316.6 4.4 %slice-start = ((s32[800]{0:T(1024)}), s32[64]{0:T(128)S(1)}, s32[]{:S(2)}) async-start(s32[800]{0:T(1024)} %param.9), calls=%async_computation.10 | async-start | bytes 1024 | tf_op jit(solution)/shard_map/slice | solution.py:77
  316.6 4.7 %copy-start.3 = (f32[192,512]{1,0:T(8,128)S(1)}, f32[192,512]{1,0:T(8,128)}, u32[]{:S(2)}) copy-start(f32[192,512]{1,0:T(8,128)} %param.5) | copy-start | bytes 1179652
  318.2 6.3 %copy-start.4 = (f32[192,2400]{1,0:T(8,128)S(1)}, f32[192,2400]{1,0:T(8,128)}, u32[]{:S(2)}) copy-start(f32[192,2400]{1,0:T(8,128)} %fusion.3) | copy-start | bytes 5529604
  318.2 29.0 %all-to-all-start.5 = ((f32[32,128,64]{1,2,0:T(8,128)}), f32[32,128,64]{1,2,0:T(8,128)S(1)}, u32[]{:S(2)}, u32[]{:S(2)}) async-start(f32[32,128,64]{1,2,0:T(8,128)} %bitcast.32), calls=%async_computation.5 | async-start | bytes 2097152 | tf_op jit(solution)/shard_map/all_to_all | solution.py:74
Sparse Core Ops, SparseCore 0:
  11.0 99.7 all-gather.6
  112.3 92.8 all-gather.4
  206.8 39.7 all-gather.8
  248.1 40.2 all-gather.10
